TPU v7x, 128 devices: a whole 4x4x4 slice. The times are simulated.
128 devices in a mesh: row: 8 (over z, core), col: 16 (over x, y).
Axes of the slice: x: 4, y: 4, z: 4, core: 2. Of those that a mesh axis runs over, the one named last changes fastest.
Arguments:
- page_tokens: bfloat16 [1024, 7168], P('row', 'col'), may hold values from -6 to 6
- weight_in: bfloat16 [7168, 28672], P('col', 'row'), may hold values from -0.0625 to 0.0625
- weight_out: bfloat16 [28672, 7168], P('row', 'col'), may hold values from -0.03125 to 0.03125
- upstream: bfloat16 [1024, 7168], P('row', 'col'), may hold values from -3 to 3
Outputs:
- block_out: bfloat16 [1024, 7168], P('row', 'col')
- grad_tokens: bfloat16 [1024, 7168], P('row', 'col')
- grad_weight_in: bfloat16 [7168, 28672], P('col', 'row')
- grad_weight_out: bfloat16 [28672, 7168], P('row', 'col')
All inputs are finite; a program needn't handle non-finite values.
Results may differ from a plain program's by a relative error of at most 0.028.
Values may be sent and summed in bfloat16 or wider, within the bound.
No kernel may reach another device: no remote copies, remote signals or barrier semaphores. Data moves between devices by JAX's collectives and lax.ppermute only.
A program may use at most 128 MiB of HBM per device.

v0:
```python
import jax
import jax.numpy as jnp
from jax import lax
from jax.sharding import Mesh
from jax.sharding import PartitionSpec as P

ROW = ("z", "core")
COL = ("x", "y")


def activate(values):
    return (
        0.5
        * values
        * (1.0 + jnp.tanh(0.7978845608 * (values + 0.044715 * values * values * values)))
    )


def activate_back(values, grads):
    return jax.vjp(activate, values)[1](grads)[0]


def contract_last(left, right):
    return lax.dot_general(
        left, right, (((1,), (1,)), ((), ())), preferred_element_type=jnp.float32
    )


def contract_first(left, right):
    return lax.dot_general(
        left, right, (((0,), (0,)), ((), ())), preferred_element_type=jnp.float32
    )


def ring_rs(blocks, ax, n, d):
    i = lax.axis_index(ax)
    perm = [(j, (j + d) % n) for j in range(n)]
    acc = lax.dynamic_index_in_dim(blocks, (i - d) % n, 0, keepdims=False)
    for s in range(1, n):
        acc = lax.ppermute(acc, ax, perm)
        acc = acc + lax.dynamic_index_in_dim(blocks, (i - d * (s + 1)) % n, 0, keepdims=False)
    return acc


def ring_ag(b, ax, n, d):
    i = lax.axis_index(ax)
    perm = [(j, (j + d) % n) for j in range(n)]
    out = jnp.zeros((n,) + b.shape, b.dtype)
    out = lax.dynamic_update_index_in_dim(out, b, i, 0)
    cur = b
    for s in range(1, n):
        cur = lax.ppermute(cur, ax, perm)
        out = lax.dynamic_update_index_in_dim(out, cur, (i - d * s) % n, 0)
    return out


def direct_ag(b, ax, n):
    i = lax.axis_index(ax)
    out = jnp.zeros((n,) + b.shape, b.dtype)
    out = lax.dynamic_update_index_in_dim(out, b, i, 0)
    for s in range(1, n):
        perm = [(j, (j + s) % n) for j in range(n)]
        out = lax.dynamic_update_index_in_dim(out, lax.ppermute(b, ax, perm), (i - s) % n, 0)
    return out


def direct_rs(blocks, ax, n):
    i = lax.axis_index(ax)
    acc = lax.dynamic_index_in_dim(blocks, i, 0, keepdims=False).astype(jnp.float32)
    for s in range(1, n):
        perm = [(j, (j + s) % n) for j in range(n)]
        send = lax.dynamic_index_in_dim(blocks, (i + s) % n, 0, keepdims=False)
        acc = acc + lax.ppermute(send, ax, perm).astype(jnp.float32)
    return acc


def to_ring_order(a):
    a5 = a.reshape(4, 4, 4, 16, a.shape[-1])
    pieces = []
    for q in range(4):
        piece = a5[:, :, q]
        if q >= 2:
            piece = piece.transpose(1, 0, 2, 3)
        pieces.append(piece.reshape(256, a.shape[-1]))
    return jnp.concatenate(pieces, 0)


def from_ring_order(a):
    pieces = []
    for q in range(4):
        piece = a[q * 256:(q + 1) * 256].reshape(4, 4, 16, a.shape[-1])
        if q >= 2:
            piece = piece.transpose(1, 0, 2, 3)
        pieces.append(piece)
    return jnp.stack(pieces, 2).reshape(a.shape)


def ring_scatter_col(a):
    qs = a.reshape(4, 4, 4, 16, a.shape[-1])
    r = [ring_rs(qs[q], "x" if q < 2 else "y", 4, 1 if q % 2 == 0 else -1) for q in range(4)]
    low = ring_rs(jnp.stack(r[:2], 1), "y", 4, 1)
    high = ring_rs(jnp.stack(r[2:], 1), "x", 4, -1)
    return jnp.concatenate([low, high], 0).reshape(64, a.shape[-1])


def ring_gather_col(b):
    parts = b.reshape(2, 2, 16, b.shape[-1])
    low = ring_ag(parts[0], "y", 4, 1)
    high = ring_ag(parts[1], "x", 4, -1)
    outs = []
    for q in range(4):
        g = (low if q < 2 else high)[:, q % 2]
        g = ring_ag(g, "x" if q < 2 else "y", 4, 1 if q % 2 == 0 else -1)
        outs.append(g.reshape(256, b.shape[-1]))
    return jnp.concatenate(outs, 0)


def gather_row(b):
    g = direct_ag(b, "core", 2)
    g = direct_ag(g, "z", 4)
    return g.reshape((-1, b.shape[-1]))


def scatter_row(part):
    p4 = part.reshape(4, 2, part.shape[0] // 8, part.shape[-1])
    acc = direct_rs(p4, "z", 4)
    c = lax.axis_index("core")
    mine = lax.dynamic_index_in_dim(acc, c, 0, keepdims=False)
    other = lax.dynamic_index_in_dim(acc, 1 - c, 0, keepdims=False)
    return (mine + lax.ppermute(other, "core", [(0, 1), (1, 0)])).astype(jnp.bfloat16)


def shards(page_tokens, weight_in, weight_out, upstream):
    width = page_tokens.shape[1]
    both = lax.all_gather(jnp.concatenate([page_tokens, upstream], 1), ROW, axis=0, tiled=True)
    features = both[:, :width]
    upstream_all = both[:, width:]
    both_ring = to_ring_order(both)
    hidden_pre = ring_scatter_col(
        jnp.dot(both_ring[:, :width], weight_in, preferred_element_type=jnp.float32).astype(jnp.bfloat16)
    ).astype(jnp.float32)
    grad_active = lax.psum_scatter(
        contract_last(upstream_all, weight_out).astype(jnp.bfloat16),
        COL,
        scatter_dimension=0,
        tiled=True,
    ).astype(jnp.float32)
    active = ring_gather_col(activate(hidden_pre).astype(jnp.bfloat16))
    grad_hidden = lax.all_gather(
        activate_back(hidden_pre, grad_active).astype(jnp.bfloat16), COL, axis=0, tiled=True
    )
    out_part = from_ring_order(
        jnp.dot(active, weight_out, preferred_element_type=jnp.float32).astype(jnp.bfloat16)
    )
    tokens_part = contract_last(grad_hidden, weight_in).astype(jnp.bfloat16)
    outs = scatter_row(jnp.concatenate([out_part, tokens_part], 1))
    block_out = outs[:, :width]
    grad_tokens = outs[:, width:]
    grad_weight_in = contract_first(features, grad_hidden).astype(jnp.bfloat16)
    grad_weight_out = contract_first(active, both_ring[:, width:]).astype(jnp.bfloat16)
    return (block_out, grad_tokens, grad_weight_in, grad_weight_out)


def solution(mesh):
    grid = Mesh(mesh.devices.reshape(mesh.shape["row"] // 2, 2, 4, mesh.shape["col"] // 4), ROW + COL)
    tok = P(ROW, COL)
    return jax.shard_map(
        shards,
        mesh=grid,
        in_specs=(tok, P(COL, ROW), tok, tok),
        out_specs=(tok, tok, P(COL, ROW), tok),
        check_vma=False,
    )
```

profile of v0, /device:TPU:1, one launch (start us, length us, event | category | flops | bytes accessed | tf_op | source)
XLA Modules:
  0.0 298.3 jit_solution(827564771316197415)
XLA Ops:
  7.2 1.2 copy.22
  10.6 28.4 %all-gather.3.cloned.1.call-done = bf16[1024,896]{1,0:T(8,128)(2,1)} async-done(((bf16[128,896]{1,0:T(8,128)(2,1)}), bf16[1024,896]{1,0:T(8,128)(2,1)}) %all-gather.3.cloned.1.call-update) | async-done | bytes 1835024 | tf_op jit(solution)/shard_map/all_gather | solution.py:135
  39.0 1.6 fusion.57
  40.9 1.2 copy-done.12
  42.1 1.2 copy-done.18
  43.3 4.2 %convolution_convert_fusion.1 = bf16[1024,3584]{1,0:T(8,128)(2,1)S(1)} fusion(bf16[448,3584]{1,0:T(8,128)(2,1)S(1)} %copy-done.18, bf16[1024,896]{1,0:T(8,128)(2,1)S(1)} %pad_maximum_fusion.1), kind=kOutput, calls=%fused_computation.1 | convolution fusion | flops 3292004352 | bytes 11599872 | tf_op jit(solution)/shard_map/dot_general | solution.py:140
  48.8 2.4 collective-permute-start.3
  52.8 2.5 collective-permute-start.12
  56.2 6.1 %convolution_convert_fusion = bf16[1024,3584]{1,0:T(8,128)(2,1)} fusion(bf16[3584,448]{0,1:T(8,128)(2,1)S(1)} %copy-done, bf16[1024,896]{1,0:T(8,128)(2,1)S(1)} %copy-done.10), kind=kOutput, calls=%fused_computation | convolution fusion | flops 3292004352 | bytes 11599872 | tf_op jit(solution)/shard_map/dot_general | solution.py:24
  62.4 1.3 bitcast_add_fusion.9
  63.7 2.7 collective-permute-start.4
  66.5 1.2 bitcast_add_fusion.12
  67.8 1.3 bitcast_add_fusion.3
  69.1 2.7 collective-permute-start.13
  71.8 1.1 bitcast_add_fusion.6
  73.1 4.6 %collective-permute-done.4 = bf16[4,16,3584]{2,1,0:T(8,128)(2,1)S(1)} collective-permute-done((bf16[4,16,3584]{2,1,0:T(8,128)(2,1)S(1)}, bf16[4,16,3584]{2,1,0:T(8,128)(2,1)S(1)}, u32[]{:S(2)}, u32[]{:S(2)}) %collective-permute-start.4) | collective-permute-done | bytes 458784 | tf_op jit(solution)/shard_map/ppermute | solution.py:40
  77.8 3.5 %collective-permute-start.5 = (bf16[4,16,3584]{2,1,0:T(8,128)(2,1)S(1)}, bf16[4,16,3584]{2,1,0:T(8,128)(2,1)S(1)}, u32[]{:S(2)}, u32[]{:S(2)}) collective-permute-start(bf16[4,16,3584]{2,1,0:T(8,128)(2,1)S(1)} %bitcast_add_fusion.8), channel_id=1, source_target_pairs={{0,12},{4,0},{8,4},{12,8},{1,13},{5,1},{9,5},{13,9},{2,14},{6,2},{... | collective-permute-start | bytes 1376264 | tf_op jit(solution)/shard_map/ppermute | solution.py:40
  81.3 2.1 collective-permute-done.1
  83.5 5.3 %collective-permute-done.13 = bf16[4,16,3584]{2,1,0:T(8,128)(2,1)S(1)} collective-permute-done((bf16[4,16,3584]{2,1,0:T(8,128)(2,1)S(1)}, bf16[4,16,3584]{2,1,0:T(8,128)(2,1)S(1)}, u32[]{:S(2)}, u32[]{:S(2)}) %collective-permute-start.13) | collective-permute-done | bytes 458784 | tf_op jit(solution)/shard_map/ppermute | solution.py:40
  88.9 3.6 %collective-permute-start.14 = (bf16[4,16,3584]{2,1,0:T(8,128)(2,1)S(1)}, bf16[4,16,3584]{2,1,0:T(8,128)(2,1)S(1)}, u32[]{:S(2)}, u32[]{:S(2)}) collective-permute-start(bf16[4,16,3584]{2,1,0:T(8,128)(2,1)S(1)} %bitcast_add_fusion.2), channel_id=1, source_target_pairs={{0,3},{1,0},{2,1},{3,2},{4,7},{5,4},{6,5},{7,6},{8,11},{9,8},{10,9... | collective-permute-start | bytes 1376264 | tf_op jit(solution)/shard_map/ppermute | solution.py:40
  93.0 3.1 %collective-permute-done.5 = bf16[4,16,3584]{2,1,0:T(8,128)(2,1)S(1)} collective-permute-done((bf16[4,16,3584]{2,1,0:T(8,128)(2,1)S(1)}, bf16[4,16,3584]{2,1,0:T(8,128)(2,1)S(1)}, u32[]{:S(2)}, u32[]{:S(2)}) %collective-permute-start.5) | collective-permute-done | bytes 458784 | tf_op jit(solution)/shard_map/ppermute | solution.py:40
  96.2 5.9 %collective-permute-done.2 = bf16[4,16,3584]{2,1,0:T(8,128)(2,1)S(1)} collective-permute-done((bf16[4,16,3584]{2,1,0:T(8,128)(2,1)S(1)}, bf16[4,16,3584]{2,1,0:T(8,128)(2,1)S(1)}, u32[]{:S(2)}, u32[]{:S(2)}) %collective-permute-start.2) | collective-permute-done | bytes 458784 | tf_op jit(solution)/shard_map/ppermute | solution.py:40
  102.3 1.5 collective-permute-start.6
  103.7 7.2 %collective-permute-done.14 = bf16[4,16,3584]{2,1,0:T(8,128)(2,1)S(1)} collective-permute-done((bf16[4,16,3584]{2,1,0:T(8,128)(2,1)S(1)}, bf16[4,16,3584]{2,1,0:T(8,128)(2,1)S(1)}, u32[]{:S(2)}, u32[]{:S(2)}) %collective-permute-start.14) | collective-permute-done | bytes 458784 | tf_op jit(solution)/shard_map/ppermute | solution.py:40
  112.0 4.6 %collective-permute-start.15 = (bf16[2,16,3584]{2,1,0:T(8,128)(2,1)S(1)}, bf16[2,16,3584]{2,1,0:T(8,128)(2,1)S(1)}, u32[]{:S(2)}, u32[]{:S(2)}) collective-permute-start(bf16[2,16,3584]{2,1,0:T(8,128)(2,1)S(1)} %fusion.36), channel_id=1, source_target_pairs={{0,12},{4,0},{8,4},{12,8},{1,13},{5,1},{9,5},{13,9},{2,14},{6,2},{... | collective-permute-start | bytes 688136 | tf_op jit(solution)/shard_map/ppermute | solution.py:40
  116.6 5.1 %collective-permute-done.6 = bf16[2,16,3584]{2,1,0:T(8,128)(2,1)S(1)} collective-permute-done((bf16[2,16,3584]{2,1,0:T(8,128)(2,1)S(1)}, bf16[2,16,3584]{2,1,0:T(8,128)(2,1)S(1)}, u32[]{:S(2)}, u32[]{:S(2)}) %collective-permute-start.6) | collective-permute-done | bytes 229408 | tf_op jit(solution)/shard_map/ppermute | solution.py:40
  121.8 1.1 collective-permute-start.7
  122.9 3.6 %collective-permute-start.16 = (bf16[2,16,3584]{2,1,0:T(8,128)(2,1)S(1)}, bf16[2,16,3584]{2,1,0:T(8,128)(2,1)S(1)}, u32[]{:S(2)}, u32[]{:S(2)}) collective-permute-start(bf16[2,16,3584]{2,1,0:T(8,128)(2,1)S(1)} %fusion.39), channel_id=1, source_target_pairs={{0,12},{4,0},{8,4},{12,8},{1,13},{5,1},{9,5},{13,9},{2,14},{6,2},{... | collective-permute-start | bytes 688136 | tf_op jit(solution)/shard_map/ppermute | solution.py:40
  126.5 5.6 %collective-permute-done.7 = bf16[2,16,3584]{2,1,0:T(8,128)(2,1)S(1)} collective-permute-done((bf16[2,16,3584]{2,1,0:T(8,128)(2,1)S(1)}, bf16[2,16,3584]{2,1,0:T(8,128)(2,1)S(1)}, u32[]{:S(2)}, u32[]{:S(2)}) %collective-permute-start.7) | collective-permute-done | bytes 229408 | tf_op jit(solution)/shard_map/ppermute | solution.py:40
  132.9 3.1 %collective-permute-start.17 = (bf16[2,16,3584]{2,1,0:T(8,128)(2,1)S(1)}, bf16[2,16,3584]{2,1,0:T(8,128)(2,1)S(1)}, u32[]{:S(2)}, u32[]{:S(2)}) collective-permute-start(bf16[2,16,3584]{2,1,0:T(8,128)(2,1)S(1)} %fusion.42), channel_id=1, source_target_pairs={{0,12},{4,0},{8,4},{12,8},{1,13},{5,1},{9,5},{13,9},{2,14},{6,2},{... | collective-permute-start | bytes 688136 | tf_op jit(solution)/shard_map/ppermute | solution.py:40
  136.0 2.5 collective-permute-done.8
  138.5 2.5 collective-permute-done.17
  141.9 14.3 %reduce-scatter.2.cloned.1.call-done = bf16[64,3584]{1,0:T(8,128)(2,1)} async-done(((bf16[1024,3584]{1,0:T(8,128)(2,1)}), bf16[64,3584]{1,0:T(8,128)(2,1)}) %reduce-scatter.2.cloned.1.call-update) | async-done | bytes 458768 | tf_op jit(solution)/shard_map/reduce_scatter | solution.py:142
  156.2 2.8 fusion.11
  159.8 1.4 collective-permute-start.27
  162.4 4.0 %collective-permute-done.18 = bf16[2,16,3584]{2,1,0:T(8,128)(2,1)} collective-permute-done((bf16[2,16,3584]{2,1,0:T(8,128)(2,1)}, bf16[2,16,3584]{2,1,0:T(8,128)(2,1)}, u32[]{:S(2)}, u32[]{:S(2)}) %collective-permute-start.18) | collective-permute-done | bytes 229408 | tf_op jit(solution)/shard_map/ppermute | solution.py:52
  167.5 1.4 collective-permute-start.28
  169.9 2.9 collective-permute-done.19
  172.8 2.7 collective-permute-start.29
  175.5 7.7 %collective-permute-done.20 = bf16[2,16,3584]{2,1,0:T(8,128)(2,1)S(1)} collective-permute-done((bf16[2,16,3584]{2,1,0:T(8,128)(2,1)S(1)}, bf16[2,16,3584]{2,1,0:T(8,128)(2,1)S(1)}, u32[]{:S(2)}, u32[]{:S(2)}) %collective-permute-start.20) | collective-permute-done | bytes 229408 | tf_op jit(solution)/shard_map/ppermute | solution.py:52
  183.8 2.7 collective-permute-start.24
  187.0 2.7 collective-permute-start.33
  189.9 2.8 collective-permute-done.21
  192.7 1.1 collective-permute-done.24
  193.8 2.4 collective-permute-start.25
  196.1 1.5 collective-permute-start.31
  197.6 2.8 collective-permute-start.34
  200.6 8.0 %collective-permute-done.22 = bf16[4,16,3584]{2,1,0:T(8,128)(2,1)S(1)} collective-permute-done((bf16[4,16,3584]{2,1,0:T(8,128)(2,1)S(1)}, bf16[4,16,3584]{2,1,0:T(8,128)(2,1)S(1)}, u32[]{:S(2)}, u32[]{:S(2)}) %collective-permute-start.22) | collective-permute-done | bytes 458784 | tf_op jit(solution)/shard_map/ppermute | solution.py:52
  208.6 5.3 %collective-permute-done.25 = bf16[4,16,3584]{2,1,0:T(8,128)(2,1)S(1)} collective-permute-done((bf16[4,16,3584]{2,1,0:T(8,128)(2,1)S(1)}, bf16[4,16,3584]{2,1,0:T(8,128)(2,1)S(1)}, u32[]{:S(2)}, u32[]{:S(2)}) %collective-permute-start.25) | collective-permute-done | bytes 458784 | tf_op jit(solution)/shard_map/ppermute | solution.py:52
  213.9 3.5 %collective-permute-start.26 = (bf16[4,16,3584]{2,1,0:T(8,128)(2,1)S(1)}, bf16[4,16,3584]{2,1,0:T(8,128)(2,1)S(1)}, u32[]{:S(2)}, u32[]{:S(2)}) collective-permute-start(bf16[4,16,3584]{2,1,0:T(8,128)(2,1)S(1)} %collective-permute-done.25), channel_id=1, source_target_pairs={{0,12},{4,0},{8,4},{12,8},{1,13},{5,1},{9,5},{13,9},{2,14},{6,2},{... | collective-permute-start | bytes 1376264 | tf_op jit(solution)/shard_map/ppermute | solution.py:52
  217.4 2.1 collective-permute-done.31
  219.4 3.2 %collective-permute-start.35 = (bf16[4,16,3584]{2,1,0:T(8,128)(2,1)S(1)}, bf16[4,16,3584]{2,1,0:T(8,128)(2,1)S(1)}, u32[]{:S(2)}, u32[]{:S(2)}) collective-permute-start(bf16[4,16,3584]{2,1,0:T(8,128)(2,1)S(1)} %collective-permute-done.34), channel_id=1, source_target_pairs={{0,3},{1,0},{2,1},{3,2},{4,7},{5,4},{6,5},{7,6},{8,11},{9,8},{10,9... | collective-permute-start | bytes 1376264 | tf_op jit(solution)/shard_map/ppermute | solution.py:52
  222.8 7.8 %collective-permute-done.23 = bf16[4,16,3584]{2,1,0:T(8,128)(2,1)S(1)} collective-permute-done((bf16[4,16,3584]{2,1,0:T(8,128)(2,1)S(1)}, bf16[4,16,3584]{2,1,0:T(8,128)(2,1)S(1)}, u32[]{:S(2)}, u32[]{:S(2)}) %collective-permute-start.23) | collective-permute-done | bytes 458784 | tf_op jit(solution)/shard_map/ppermute | solution.py:52
  230.7 5.2 %collective-permute-done.26 = bf16[4,16,3584]{2,1,0:T(8,128)(2,1)S(1)} collective-permute-done((bf16[4,16,3584]{2,1,0:T(8,128)(2,1)S(1)}, bf16[4,16,3584]{2,1,0:T(8,128)(2,1)S(1)}, u32[]{:S(2)}, u32[]{:S(2)}) %collective-permute-start.26) | collective-permute-done | bytes 458784 | tf_op jit(solution)/shard_map/ppermute | solution.py:52
  236.0 5.8 %collective-permute-done.32 = bf16[4,16,3584]{2,1,0:T(8,128)(2,1)S(1)} collective-permute-done((bf16[4,16,3584]{2,1,0:T(8,128)(2,1)S(1)}, bf16[4,16,3584]{2,1,0:T(8,128)(2,1)S(1)}, u32[]{:S(2)}, u32[]{:S(2)}) %collective-permute-start.32) | collective-permute-done | bytes 458784 | tf_op jit(solution)/shard_map/ppermute | solution.py:52
  241.9 7.8 %convolution_convert_fusion.5 = bf16[1024,448]{0,1:T(8,128)(2,1)S(1)} fusion(bf16[3584,448]{0,1:T(8,128)(2,1)S(1)} %copy-done, bf16[256,3584]{1,0:T(8,128)(2,1)S(1)} %bitcast.219, bf16[256,3584]{1,0:T(8,128)(2,1)S(1)} %bitcast.225, bf16[256,3584]{1,0:T(8,128)(2,1)S(1)} %bitcast.221, bf16[256,3584]{1,0:T(8,128)(2,1)S(1)} %bitcast.223), kind=kOutput, calls=%fused_computation.22 | convolution fusion | flops 3318153216 | bytes 11468800 | tf_op jit(solution)/shard_map/dot_general | solution.py:153
  251.4 7.5 %convolution_convert_fusion.4 = bf16[1024,448]{0,1:T(8,128)(2,1)S(1)} fusion(bf16[1024,3584]{1,0:T(8,128)(2,1)} %all-gather.5.cloned.1.call-done, bf16[448,3584]{1,0:T(8,128)(2,1)} %param.5), kind=kOutput, calls=%fused_computation.21 | convolution fusion | flops 3288793088 | bytes 11468800 | tf_op jit(solution)/shard_map/dot_general | solution.py:24
  260.0 1.6 collective-permute-start.36
  261.6 1.7 collective-permute-start.37
  263.2 1.8 collective-permute-start.38
  265.0 7.7 %convolution_convert_fusion.2 = bf16[3584,448]{0,1:T(8,128)(2,1)} fusion(bf16[256,3584]{1,0:T(8,128)(2,1)} %bitcast.220, bf16[256,3584]{1,0:T(8,128)(2,1)} %bitcast.226, bf16[256,3584]{1,0:T(8,128)(2,1)} %bitcast.222, bf16[256,3584]{1,0:T(8,128)(2,1)} %bitcast.224, bf16[1024,896]{1,0:T(8,128)(2,1)S(1)} %copy-done.13), kind=kOutput, calls=%fused_computation.3 | convolution fusion | flops 3319300096 | bytes 11599872 | tf_op jit(solution)/shard_map/dot_general | solution.py:30
  272.8 2.3 collective-permute-done.37
  275.4 9.7 %collective-permute-start.39 = (f32[128,896]{1,0:T(8,128)S(1)}, f32[128,896]{1,0:T(8,128)S(1)}, u32[]{:S(2)}, u32[]{:S(2)}) collective-permute-start(f32[128,896]{1,0:T(8,128)S(1)} %dynamic-slice_bitcast_fusion), channel_id=1, source_target_pairs={{0,16},{16,0},{1,17},{17,1},{2,18},{18,2},{3,19},{19,3},{4,20},{20... | collective-permute-start | bytes 1376264 | tf_op jit(solution)/shard_map/ppermute | solution.py:130
  285.1 4.9 %convolution_convert_fusion.3 = bf16[448,3584]{1,0:T(8,128)(2,1)} fusion(bf16[1024,3584]{1,0:T(8,128)(2,1)S(1)} %bitcast.234, bf16[1024,896]{1,0:T(8,128)(2,1)S(1)} %copy-done.11), kind=kOutput, calls=%fused_computation.4 | convolution fusion | flops 3289939968 | bytes 11599872 | tf_op jit(solution)/shard_map/dot_general | solution.py:30
  (157 shorter events, 20.2 us)
Async XLA Ops:
  7.2 49.0 %copy-start = (bf16[3584,448]{0,1:T(8,128)(2,1)S(1)}, bf16[3584,448]{0,1:T(8,128)(2,1)}, u32[]{:S(2)}) copy-start(bf16[3584,448]{0,1:T(8,128)(2,1)} %param.6) | copy-start | bytes 9633796
  7.2 31.9 %all-gather.3.cloned.1.call-start = ((), (), s32[]{:S(2)}) async-start(), calls=%async_computation.1 | async-start | bytes 2064384 | tf_op jit(solution)/shard_map/all_gather | solution.py:135
  10.2 146.0 %reduce-scatter.2.cloned.1.call-start = ((), (), s32[]{:S(2)}) async-start(), calls=%async_computation.2 | async-start | bytes 7798784 | tf_op jit(solution)/shard_map/reduce_scatter | solution.py:142
  40.7 2.6 copy-start.18
  40.9 1.2 copy-start.12
  48.0 8.2 %copy-start.2 = (bf16[256,3584]{1,0:T(8,128)(2,1)}, bf16[256,3584]{1,0:T(8,128)(2,1)S(1)}, u32[]{:S(2)}) copy-start(bf16[256,3584]{1,0:T(8,128)(2,1)S(1)} %get-tuple-element.10) | copy-start | bytes 5505028
  48.0 8.2 %copy-start.4 = (bf16[256,3584]{1,0:T(8,128)(2,1)}, bf16[256,3584]{1,0:T(8,128)(2,1)S(1)}, u32[]{:S(2)}) copy-start(bf16[256,3584]{1,0:T(8,128)(2,1)S(1)} %get-tuple-element.9) | copy-start | bytes 5505028
  48.0 8.2 %copy-start.6 = (bf16[256,3584]{1,0:T(8,128)(2,1)}, bf16[256,3584]{1,0:T(8,128)(2,1)S(1)}, u32[]{:S(2)}) copy-start(bf16[256,3584]{1,0:T(8,128)(2,1)S(1)} %get-tuple-element.11) | copy-start | bytes 5505028
  48.0 8.2 %copy-start.8 = (bf16[256,3584]{1,0:T(8,128)(2,1)}, bf16[256,3584]{1,0:T(8,128)(2,1)S(1)}, u32[]{:S(2)}) copy-start(bf16[256,3584]{1,0:T(8,128)(2,1)S(1)} %get-tuple-element.8) | copy-start | bytes 5505028
  48.0 8.2 %copy-start.10 = (bf16[1024,896]{1,0:T(8,128)(2,1)S(1)}, bf16[1024,896]{1,0:T(8,128)(2,1)}, u32[]{:S(2)}) copy-start(bf16[1024,896]{1,0:T(8,128)(2,1)} %all-gather.3.cloned.1.call-done) | copy-start | bytes 5505028
  48.8 13.5 %collective-permute-start.3 = (bf16[4,16,3584]{2,1,0:T(8,128)(2,1)}, bf16[4,16,3584]{2,1,0:T(8,128)(2,1)}, u32[]{:S(2)}, u32[]{:S(2)}) collective-permute-start(bf16[4,16,3584]{2,1,0:T(8,128)(2,1)} %dynamic-slice_bitcast_fusion.3), channel_id=1, source_target_pairs={{0,12},{4,0},{8,4},{12,8},{1,13},{5,1},{9,5},{13,9},{2,14},{6,2},{... | collective-permute-start | bytes 1376264 | tf_op jit(solution)/shard_map/ppermute | solution.py:40
  52.0 14.4 %collective-permute-start = (bf16[4,16,3584]{2,1,0:T(8,128)(2,1)}, bf16[4,16,3584]{2,1,0:T(8,128)(2,1)}, u32[]{:S(2)}, u32[]{:S(2)}) collective-permute-start(bf16[4,16,3584]{2,1,0:T(8,128)(2,1)} %dynamic-slice_bitcast_fusion.4), channel_id=1, source_target_pairs={{0,4},{4,8},{8,12},{12,0},{1,5},{5,9},{9,13},{13,1},{2,6},{6,10},{... | collective-permute-start | bytes 1376264 | tf_op jit(solution)/shard_map/ppermute | solution.py:40
  52.8 14.9 %collective-permute-start.12 = (bf16[4,16,3584]{2,1,0:T(8,128)(2,1)}, bf16[4,16,3584]{2,1,0:T(8,128)(2,1)}, u32[]{:S(2)}, u32[]{:S(2)}) collective-permute-start(bf16[4,16,3584]{2,1,0:T(8,128)(2,1)} %dynamic-slice_bitcast_fusion.1), channel_id=1, source_target_pairs={{0,3},{1,0},{2,1},{3,2},{4,7},{5,4},{6,5},{7,6},{8,11},{9,8},{10,9... | collective-permute-start | bytes 1376264 | tf_op jit(solution)/shard_map/ppermute | solution.py:40
  56.1 15.7 %collective-permute-start.9 = (bf16[4,16,3584]{2,1,0:T(8,128)(2,1)}, bf16[4,16,3584]{2,1,0:T(8,128)(2,1)}, u32[]{:S(2)}, u32[]{:S(2)}) collective-permute-start(bf16[4,16,3584]{2,1,0:T(8,128)(2,1)} %dynamic-slice_bitcast_fusion.2), channel_id=1, source_target_pairs={{0,1},{1,2},{2,3},{3,0},{4,5},{5,6},{6,7},{7,4},{8,9},{9,10},{10,1... | collective-permute-start | bytes 1376264 | tf_op jit(solution)/shard_map/ppermute | solution.py:40
  62.3 189.1 %all-gather.5.cloned.1.call-start = ((), (), s32[]{:S(2)}) async-start(), calls=%async_computation.3 | async-start | bytes 7798784 | tf_op jit(solution)/shard_map/all_gather | solution.py:149
  62.3 9.5 %copy-start.3 = (bf16[256,3584]{1,0:T(8,128)(2,1)S(1)}, bf16[256,3584]{1,0:T(8,128)(2,1)}, u32[]{:S(2)}) copy-start(bf16[256,3584]{1,0:T(8,128)(2,1)} %copy-done.2) | copy-start | bytes 5505028
  63.7 14.0 %copy-start.9 = (bf16[256,3584]{1,0:T(8,128)(2,1)S(1)}, bf16[256,3584]{1,0:T(8,128)(2,1)}, u32[]{:S(2)}) copy-start(bf16[256,3584]{1,0:T(8,128)(2,1)} %copy-done.8) | copy-start | bytes 5505028
  63.7 14.0 %collective-permute-start.4 = (bf16[4,16,3584]{2,1,0:T(8,128)(2,1)S(1)}, bf16[4,16,3584]{2,1,0:T(8,128)(2,1)S(1)}, u32[]{:S(2)}, u32[]{:S(2)}) collective-permute-start(bf16[4,16,3584]{2,1,0:T(8,128)(2,1)S(1)} %bitcast_add_fusion.9), channel_id=1, source_target_pairs={{0,12},{4,0},{8,4},{12,8},{1,13},{5,1},{9,5},{13,9},{2,14},{6,2},{... | collective-permute-start | bytes 1376264 | tf_op jit(solution)/shard_map/ppermute | solution.py:40
  67.7 15.7 %copy-start.7 = (bf16[256,3584]{1,0:T(8,128)(2,1)S(1)}, bf16[256,3584]{1,0:T(8,128)(2,1)}, u32[]{:S(2)}) copy-start(bf16[256,3584]{1,0:T(8,128)(2,1)} %copy-done.6) | copy-start | bytes 5505028
  67.7 15.7 %collective-permute-start.1 = (bf16[4,16,3584]{2,1,0:T(8,128)(2,1)S(1)}, bf16[4,16,3584]{2,1,0:T(8,128)(2,1)S(1)}, u32[]{:S(2)}, u32[]{:S(2)}) collective-permute-start(bf16[4,16,3584]{2,1,0:T(8,128)(2,1)S(1)} %bitcast_add_fusion.12), channel_id=1, source_target_pairs={{0,4},{4,8},{8,12},{12,0},{1,5},{5,9},{9,13},{13,1},{2,6},{6,10},{... | collective-permute-start | bytes 1376264 | tf_op jit(solution)/shard_map/ppermute | solution.py:40
  69.1 19.8 %copy-start.5 = (bf16[256,3584]{1,0:T(8,128)(2,1)S(1)}, bf16[256,3584]{1,0:T(8,128)(2,1)}, u32[]{:S(2)}) copy-start(bf16[256,3584]{1,0:T(8,128)(2,1)} %copy-done.4) | copy-start | bytes 5505028
  69.1 19.8 %collective-permute-start.13 = (bf16[4,16,3584]{2,1,0:T(8,128)(2,1)S(1)}, bf16[4,16,3584]{2,1,0:T(8,128)(2,1)S(1)}, u32[]{:S(2)}, u32[]{:S(2)}) collective-permute-start(bf16[4,16,3584]{2,1,0:T(8,128)(2,1)S(1)} %bitcast_add_fusion.3), channel_id=1, source_target_pairs={{0,3},{1,0},{2,1},{3,2},{4,7},{5,4},{6,5},{7,6},{8,11},{9,8},{10,9... | collective-permute-start | bytes 1376264 | tf_op jit(solution)/shard_map/ppermute | solution.py:40
  73.0 19.9 %collective-permute-start.10 = (bf16[4,16,3584]{2,1,0:T(8,128)(2,1)S(1)}, bf16[4,16,3584]{2,1,0:T(8,128)(2,1)S(1)}, u32[]{:S(2)}, u32[]{:S(2)}) collective-permute-start(bf16[4,16,3584]{2,1,0:T(8,128)(2,1)S(1)} %bitcast_add_fusion.6), channel_id=1, source_target_pairs={{0,1},{1,2},{2,3},{3,0},{4,5},{5,6},{6,7},{7,4},{8,9},{9,10},{10,1... | collective-permute-start | bytes 1376264 | tf_op jit(solution)/shard_map/ppermute | solution.py:40
  77.8 18.4 %collective-permute-start.5 = (bf16[4,16,3584]{2,1,0:T(8,128)(2,1)S(1)}, bf16[4,16,3584]{2,1,0:T(8,128)(2,1)S(1)}, u32[]{:S(2)}, u32[]{:S(2)}) collective-permute-start(bf16[4,16,3584]{2,1,0:T(8,128)(2,1)S(1)} %bitcast_add_fusion.8), channel_id=1, source_target_pairs={{0,12},{4,0},{8,4},{12,8},{1,13},{5,1},{9,5},{13,9},{2,14},{6,2},{... | collective-permute-start | bytes 1376264 | tf_op jit(solution)/shard_map/ppermute | solution.py:40
  83.4 18.7 %collective-permute-start.2 = (bf16[4,16,3584]{2,1,0:T(8,128)(2,1)S(1)}, bf16[4,16,3584]{2,1,0:T(8,128)(2,1)S(1)}, u32[]{:S(2)}, u32[]{:S(2)}) collective-permute-start(bf16[4,16,3584]{2,1,0:T(8,128)(2,1)S(1)} %bitcast_add_fusion.11), channel_id=1, source_target_pairs={{0,4},{4,8},{8,12},{12,0},{1,5},{5,9},{9,13},{13,1},{2,6},{6,10},{... | collective-permute-start | bytes 1376264 | tf_op jit(solution)/shard_map/ppermute | solution.py:40
  88.9 22.0 %collective-permute-start.14 = (bf16[4,16,3584]{2,1,0:T(8,128)(2,1)S(1)}, bf16[4,16,3584]{2,1,0:T(8,128)(2,1)S(1)}, u32[]{:S(2)}, u32[]{:S(2)}) collective-permute-start(bf16[4,16,3584]{2,1,0:T(8,128)(2,1)S(1)} %bitcast_add_fusion.2), channel_id=1, source_target_pairs={{0,3},{1,0},{2,1},{3,2},{4,7},{5,4},{6,5},{7,6},{8,11},{9,8},{10,9... | collective-permute-start | bytes 1376264 | tf_op jit(solution)/shard_map/ppermute | solution.py:40
  93.0 19.0 %collective-permute-start.11 = (bf16[4,16,3584]{2,1,0:T(8,128)(2,1)S(1)}, bf16[4,16,3584]{2,1,0:T(8,128)(2,1)S(1)}, u32[]{:S(2)}, u32[]{:S(2)}) collective-permute-start(bf16[4,16,3584]{2,1,0:T(8,128)(2,1)S(1)} %bitcast_add_fusion.5), channel_id=1, source_target_pairs={{0,1},{1,2},{2,3},{3,0},{4,5},{5,6},{6,7},{7,4},{8,9},{9,10},{10,1... | collective-permute-start | bytes 1376264 | tf_op jit(solution)/shard_map/ppermute | solution.py:40
  102.3 19.5 %collective-permute-start.6 = (bf16[2,16,3584]{2,1,0:T(8,128)(2,1)S(1)}, bf16[2,16,3584]{2,1,0:T(8,128)(2,1)S(1)}, u32[]{:S(2)}, u32[]{:S(2)}) collective-permute-start(bf16[2,16,3584]{2,1,0:T(8,128)(2,1)S(1)} %fusion.47), channel_id=1, source_target_pairs={{0,1},{1,2},{2,3},{3,0},{4,5},{5,6},{6,7},{7,4},{8,9},{9,10},{10,1... | collective-permute-start | bytes 688136 | tf_op jit(solution)/shard_map/ppermute | solution.py:40
  112.0 10.8 %collective-permute-start.15 = (bf16[2,16,3584]{2,1,0:T(8,128)(2,1)S(1)}, bf16[2,16,3584]{2,1,0:T(8,128)(2,1)S(1)}, u32[]{:S(2)}, u32[]{:S(2)}) collective-permute-start(bf16[2,16,3584]{2,1,0:T(8,128)(2,1)S(1)} %fusion.36), channel_id=1, source_target_pairs={{0,12},{4,0},{8,4},{12,8},{1,13},{5,1},{9,5},{13,9},{2,14},{6,2},{... | collective-permute-start | bytes 688136 | tf_op jit(solution)/shard_map/ppermute | solution.py:40
  121.8 10.3 %collective-permute-start.7 = (bf16[2,16,3584]{2,1,0:T(8,128)(2,1)S(1)}, bf16[2,16,3584]{2,1,0:T(8,128)(2,1)S(1)}, u32[]{:S(2)}, u32[]{:S(2)}) collective-permute-start(bf16[2,16,3584]{2,1,0:T(8,128)(2,1)S(1)} %fusion.50), channel_id=1, source_target_pairs={{0,1},{1,2},{2,3},{3,0},{4,5},{5,6},{6,7},{7,4},{8,9},{9,10},{10,1... | collective-permute-start | bytes 688136 | tf_op jit(solution)/shard_map/ppermute | solution.py:40
  122.9 10.0 %collective-permute-start.16 = (bf16[2,16,3584]{2,1,0:T(8,128)(2,1)S(1)}, bf16[2,16,3584]{2,1,0:T(8,128)(2,1)S(1)}, u32[]{:S(2)}, u32[]{:S(2)}) collective-permute-start(bf16[2,16,3584]{2,1,0:T(8,128)(2,1)S(1)} %fusion.39), channel_id=1, source_target_pairs={{0,12},{4,0},{8,4},{12,8},{1,13},{5,1},{9,5},{13,9},{2,14},{6,2},{... | collective-permute-start | bytes 688136 | tf_op jit(solution)/shard_map/ppermute | solution.py:40
  132.2 6.3 %collective-permute-start.8 = (bf16[2,16,3584]{2,1,0:T(8,128)(2,1)S(1)}, bf16[2,16,3584]{2,1,0:T(8,128)(2,1)S(1)}, u32[]{:S(2)}, u32[]{:S(2)}) collective-permute-start(bf16[2,16,3584]{2,1,0:T(8,128)(2,1)S(1)} %fusion.53), channel_id=1, source_target_pairs={{0,1},{1,2},{2,3},{3,0},{4,5},{5,6},{6,7},{7,4},{8,9},{9,10},{10,1... | collective-permute-start | bytes 688136 | tf_op jit(solution)/shard_map/ppermute | solution.py:40
  132.9 8.1 %collective-permute-start.17 = (bf16[2,16,3584]{2,1,0:T(8,128)(2,1)S(1)}, bf16[2,16,3584]{2,1,0:T(8,128)(2,1)S(1)}, u32[]{:S(2)}, u32[]{:S(2)}) collective-permute-start(bf16[2,16,3584]{2,1,0:T(8,128)(2,1)S(1)} %fusion.42), channel_id=1, source_target_pairs={{0,12},{4,0},{8,4},{12,8},{1,13},{5,1},{9,5},{13,9},{2,14},{6,2},{... | collective-permute-start | bytes 688136 | tf_op jit(solution)/shard_map/ppermute | solution.py:40
  159.7 6.8 %collective-permute-start.18 = (bf16[2,16,3584]{2,1,0:T(8,128)(2,1)}, bf16[2,16,3584]{2,1,0:T(8,128)(2,1)}, u32[]{:S(2)}, u32[]{:S(2)}) collective-permute-start(bf16[2,16,3584]{2,1,0:T(8,128)(2,1)} %bitcast.44), channel_id=1, source_target_pairs={{0,1},{1,2},{2,3},{3,0},{4,5},{5,6},{6,7},{7,4},{8,9},{9,10},{10,1... | collective-permute-start | bytes 688136 | tf_op jit(solution)/shard_map/ppermute | solution.py:52
  159.8 7.6 %collective-permute-start.27 = (bf16[2,16,3584]{2,1,0:T(8,128)(2,1)S(1)}, bf16[2,16,3584]{2,1,0:T(8,128)(2,1)}, u32[]{:S(2)}, u32[]{:S(2)}) collective-permute-start(bf16[2,16,3584]{2,1,0:T(8,128)(2,1)S(1)} %bitcast.231), channel_id=1, source_target_pairs={{0,12},{4,0},{8,4},{12,8},{1,13},{5,1},{9,5},{13,9},{2,14},{6,2},{... | collective-permute-start | bytes 688136 | tf_op jit(solution)/shard_map/ppermute | solution.py:52
  166.5 6.3 %collective-permute-start.19 = (bf16[2,16,3584]{2,1,0:T(8,128)(2,1)}, bf16[2,16,3584]{2,1,0:T(8,128)(2,1)S(1)}, u32[]{:S(2)}, u32[]{:S(2)}) collective-permute-start(bf16[2,16,3584]{2,1,0:T(8,128)(2,1)} %collective-permute-done.18), channel_id=1, source_target_pairs={{0,1},{1,2},{2,3},{3,0},{4,5},{5,6},{6,7},{7,4},{8,9},{9,10},{10,1... | collective-permute-start | bytes 688136 | tf_op jit(solution)/shard_map/ppermute | solution.py:52
  167.5 5.3 %collective-permute-start.28 = (bf16[2,16,3584]{2,1,0:T(8,128)(2,1)}, bf16[2,16,3584]{2,1,0:T(8,128)(2,1)S(1)}, u32[]{:S(2)}, u32[]{:S(2)}) collective-permute-start(bf16[2,16,3584]{2,1,0:T(8,128)(2,1)} %collective-permute-done.27), channel_id=1, source_target_pairs={{0,12},{4,0},{8,4},{12,8},{1,13},{5,1},{9,5},{13,9},{2,14},{6,2},{... | collective-permute-start | bytes 688136 | tf_op jit(solution)/shard_map/ppermute | solution.py:52
  172.7 10.5 %collective-permute-start.20 = (bf16[2,16,3584]{2,1,0:T(8,128)(2,1)S(1)}, bf16[2,16,3584]{2,1,0:T(8,128)(2,1)S(1)}, u32[]{:S(2)}, u32[]{:S(2)}) collective-permute-start(bf16[2,16,3584]{2,1,0:T(8,128)(2,1)S(1)} %collective-permute-done.19), channel_id=1, source_target_pairs={{0,1},{1,2},{2,3},{3,0},{4,5},{5,6},{6,7},{7,4},{8,9},{9,10},{10,1... | collective-permute-start | bytes 688136 | tf_op jit(solution)/shard_map/ppermute | solution.py:52
  172.8 13.8 %collective-permute-start.29 = (bf16[2,16,3584]{2,1,0:T(8,128)(2,1)S(1)}, bf16[2,16,3584]{2,1,0:T(8,128)(2,1)S(1)}, u32[]{:S(2)}, u32[]{:S(2)}) collective-permute-start(bf16[2,16,3584]{2,1,0:T(8,128)(2,1)S(1)} %collective-permute-done.28), channel_id=1, source_target_pairs={{0,12},{4,0},{8,4},{12,8},{1,13},{5,1},{9,5},{13,9},{2,14},{6,2},{... | collective-permute-start | bytes 688136 | tf_op jit(solution)/shard_map/ppermute | solution.py:52
  183.5 9.2 %collective-permute-start.21 = (bf16[4,16,3584]{2,1,0:T(8,128)(2,1)S(1)}, bf16[4,16,3584]{2,1,0:T(8,128)(2,1)S(1)}, u32[]{:S(2)}, u32[]{:S(2)}) collective-permute-start(bf16[4,16,3584]{2,1,0:T(8,128)(2,1)S(1)} %get-tuple-element.23), channel_id=1, source_target_pairs={{0,4},{4,8},{8,12},{12,0},{1,5},{5,9},{9,13},{13,1},{2,6},{6,10},{... | collective-permute-start | bytes 1376264 | tf_op jit(solution)/shard_map/ppermute | solution.py:52
  183.8 9.9 %collective-permute-start.24 = (bf16[4,16,3584]{2,1,0:T(8,128)(2,1)S(1)}, bf16[4,16,3584]{2,1,0:T(8,128)(2,1)S(1)}, u32[]{:S(2)}, u32[]{:S(2)}) collective-permute-start(bf16[4,16,3584]{2,1,0:T(8,128)(2,1)S(1)} %get-tuple-element.24), channel_id=1, source_target_pairs={{0,12},{4,0},{8,4},{12,8},{1,13},{5,1},{9,5},{13,9},{2,14},{6,2},{... | collective-permute-start | bytes 1376264 | tf_op jit(solution)/shard_map/ppermute | solution.py:52
  186.9 9.3 %collective-permute-start.30 = (bf16[4,16,3584]{2,1,0:T(8,128)(2,1)S(1)}, bf16[4,16,3584]{2,1,0:T(8,128)(2,1)S(1)}, u32[]{:S(2)}, u32[]{:S(2)}) collective-permute-start(bf16[4,16,3584]{2,1,0:T(8,128)(2,1)S(1)} %get-tuple-element.25), channel_id=1, source_target_pairs={{0,1},{1,2},{2,3},{3,0},{4,5},{5,6},{6,7},{7,4},{8,9},{9,10},{10,1... | collective-permute-start | bytes 1376264 | tf_op jit(solution)/shard_map/ppermute | solution.py:52
  187.0 10.7 %collective-permute-start.33 = (bf16[4,16,3584]{2,1,0:T(8,128)(2,1)S(1)}, bf16[4,16,3584]{2,1,0:T(8,128)(2,1)S(1)}, u32[]{:S(2)}, u32[]{:S(2)}) collective-permute-start(bf16[4,16,3584]{2,1,0:T(8,128)(2,1)S(1)} %get-tuple-element.26), channel_id=1, source_target_pairs={{0,3},{1,0},{2,1},{3,2},{4,7},{5,4},{6,5},{7,6},{8,11},{9,8},{10,9... | collective-permute-start | bytes 1376264 | tf_op jit(solution)/shard_map/ppermute | solution.py:52
  192.7 15.9 %collective-permute-start.22 = (bf16[4,16,3584]{2,1,0:T(8,128)(2,1)S(1)}, bf16[4,16,3584]{2,1,0:T(8,128)(2,1)S(1)}, u32[]{:S(2)}, u32[]{:S(2)}) collective-permute-start(bf16[4,16,3584]{2,1,0:T(8,128)(2,1)S(1)} %collective-permute-done.21), channel_id=1, source_target_pairs={{0,4},{4,8},{8,12},{12,0},{1,5},{5,9},{9,13},{13,1},{2,6},{6,10},{... | collective-permute-start | bytes 1376264 | tf_op jit(solution)/shard_map/ppermute | solution.py:52
  193.8 20.1 %collective-permute-start.25 = (bf16[4,16,3584]{2,1,0:T(8,128)(2,1)S(1)}, bf16[4,16,3584]{2,1,0:T(8,128)(2,1)S(1)}, u32[]{:S(2)}, u32[]{:S(2)}) collective-permute-start(bf16[4,16,3584]{2,1,0:T(8,128)(2,1)S(1)} %collective-permute-done.24), channel_id=1, source_target_pairs={{0,12},{4,0},{8,4},{12,8},{1,13},{5,1},{9,5},{13,9},{2,14},{6,2},{... | collective-permute-start | bytes 1376264 | tf_op jit(solution)/shard_map/ppermute | solution.py:52
  196.1 23.3 %collective-permute-start.31 = (bf16[4,16,3584]{2,1,0:T(8,128)(2,1)S(1)}, bf16[4,16,3584]{2,1,0:T(8,128)(2,1)S(1)}, u32[]{:S(2)}, u32[]{:S(2)}) collective-permute-start(bf16[4,16,3584]{2,1,0:T(8,128)(2,1)S(1)} %collective-permute-done.30), channel_id=1, source_target_pairs={{0,1},{1,2},{2,3},{3,0},{4,5},{5,6},{6,7},{7,4},{8,9},{9,10},{10,1... | collective-permute-start | bytes 1376264 | tf_op jit(solution)/shard_map/ppermute | solution.py:52
  197.6 21.8 %collective-permute-start.34 = (bf16[4,16,3584]{2,1,0:T(8,128)(2,1)S(1)}, bf16[4,16,3584]{2,1,0:T(8,128)(2,1)S(1)}, u32[]{:S(2)}, u32[]{:S(2)}) collective-permute-start(bf16[4,16,3584]{2,1,0:T(8,128)(2,1)S(1)} %collective-permute-done.33), channel_id=1, source_target_pairs={{0,3},{1,0},{2,1},{3,2},{4,7},{5,4},{6,5},{7,6},{8,11},{9,8},{10,9... | collective-permute-start | bytes 1376264 | tf_op jit(solution)/shard_map/ppermute | solution.py:52
  208.6 22.1 %collective-permute-start.23 = (bf16[4,16,3584]{2,1,0:T(8,128)(2,1)S(1)}, bf16[4,16,3584]{2,1,0:T(8,128)(2,1)S(1)}, u32[]{:S(2)}, u32[]{:S(2)}) collective-permute-start(bf16[4,16,3584]{2,1,0:T(8,128)(2,1)S(1)} %collective-permute-done.22), channel_id=1, source_target_pairs={{0,4},{4,8},{8,12},{12,0},{1,5},{5,9},{9,13},{13,1},{2,6},{6,10},{... | collective-permute-start | bytes 1376264 | tf_op jit(solution)/shard_map/ppermute | solution.py:52
  213.9 22.1 %collective-permute-start.26 = (bf16[4,16,3584]{2,1,0:T(8,128)(2,1)S(1)}, bf16[4,16,3584]{2,1,0:T(8,128)(2,1)S(1)}, u32[]{:S(2)}, u32[]{:S(2)}) collective-permute-start(bf16[4,16,3584]{2,1,0:T(8,128)(2,1)S(1)} %collective-permute-done.25), channel_id=1, source_target_pairs={{0,12},{4,0},{8,4},{12,8},{1,13},{5,1},{9,5},{13,9},{2,14},{6,2},{... | collective-permute-start | bytes 1376264 | tf_op jit(solution)/shard_map/ppermute | solution.py:52
  219.4 22.3 %collective-permute-start.32 = (bf16[4,16,3584]{2,1,0:T(8,128)(2,1)S(1)}, bf16[4,16,3584]{2,1,0:T(8,128)(2,1)S(1)}, u32[]{:S(2)}, u32[]{:S(2)}) collective-permute-start(bf16[4,16,3584]{2,1,0:T(8,128)(2,1)S(1)} %collective-permute-done.31), channel_id=1, source_target_pairs={{0,1},{1,2},{2,3},{3,0},{4,5},{5,6},{6,7},{7,4},{8,9},{9,10},{10,1... | collective-permute-start | bytes 1376264 | tf_op jit(solution)/shard_map/ppermute | solution.py:52
  219.4 22.4 %collective-permute-start.35 = (bf16[4,16,3584]{2,1,0:T(8,128)(2,1)S(1)}, bf16[4,16,3584]{2,1,0:T(8,128)(2,1)S(1)}, u32[]{:S(2)}, u32[]{:S(2)}) collective-permute-start(bf16[4,16,3584]{2,1,0:T(8,128)(2,1)S(1)} %collective-permute-done.34), channel_id=1, source_target_pairs={{0,3},{1,0},{2,1},{3,2},{4,7},{5,4},{6,5},{7,6},{8,11},{9,8},{10,9... | collective-permute-start | bytes 1376264 | tf_op jit(solution)/shard_map/ppermute | solution.py:52
  230.7 19.0 %copy-start.16 = (bf16[4,4,16,3584]{3,2,1,0:T(8,128)(2,1)}, bf16[4,4,16,3584]{3,2,1,0:T(8,128)(2,1)S(1)}, u32[]{:S(2)}) copy-start(bf16[4,4,16,3584]{3,2,1,0:T(8,128)(2,1)S(1)} %bitcast_dynamic-update-slice_fusion.12) | copy-start | bytes 5505028
  236.0 13.7 %copy-start.15 = (bf16[4,4,16,3584]{3,2,1,0:T(8,128)(2,1)}, bf16[4,4,16,3584]{3,2,1,0:T(8,128)(2,1)S(1)}, u32[]{:S(2)}) copy-start(bf16[4,4,16,3584]{3,2,1,0:T(8,128)(2,1)S(1)} %bitcast_dynamic-update-slice_fusion.8) | copy-start | bytes 5505028
  241.8 7.9 %copy-start.17 = (bf16[4,4,16,3584]{3,2,1,0:T(8,128)(2,1)}, bf16[4,4,16,3584]{3,2,1,0:T(8,128)(2,1)S(1)}, u32[]{:S(2)}) copy-start(bf16[4,4,16,3584]{3,2,1,0:T(8,128)(2,1)S(1)} %bitcast_dynamic-update-slice_fusion.4) | copy-start | bytes 5505028
  241.9 7.9 %copy-start.14 = (bf16[4,4,16,3584]{3,2,1,0:T(8,128)(2,1)}, bf16[4,4,16,3584]{3,2,1,0:T(8,128)(2,1)S(1)}, u32[]{:S(2)}) copy-start(bf16[4,4,16,3584]{3,2,1,0:T(8,128)(2,1)S(1)} %bitcast_dynamic-update-slice_fusion) | copy-start | bytes 5505028
  259.5 5.6 %copy-start.13 = (bf16[1024,896]{1,0:T(8,128)(2,1)S(1)}, bf16[1024,896]{1,0:T(8,128)(2,1)}, u32[]{:S(2)}) copy-start(bf16[1024,896]{1,0:T(8,128)(2,1)} %copy-done.12) | copy-start | bytes 5505028
  260.0 12.8 %collective-permute-start.36 = (bf16[2,128,896]{2,1,0:T(8,128)(2,1)S(1)}, bf16[2,128,896]{2,1,0:T(8,128)(2,1)S(1)}, u32[]{:S(2)}, u32[]{:S(2)}) collective-permute-start(bf16[2,128,896]{2,1,0:T(8,128)(2,1)S(1)} %get-tuple-element.12), channel_id=1, source_target_pairs={{0,32},{32,64},{64,96},{96,0},{1,33},{33,65},{65,97},{97,1},{2,34}... | collective-permute-start | bytes 1376264 | tf_op jit(solution)/shard_map/ppermute | solution.py:73
  261.6 13.5 %collective-permute-start.37 = (bf16[2,128,896]{2,1,0:T(8,128)(2,1)S(1)}, bf16[2,128,896]{2,1,0:T(8,128)(2,1)S(1)}, u32[]{:S(2)}, u32[]{:S(2)}) collective-permute-start(bf16[2,128,896]{2,1,0:T(8,128)(2,1)S(1)} %get-tuple-element.13), channel_id=1, source_target_pairs={{0,64},{32,96},{64,0},{96,32},{1,65},{33,97},{65,1},{97,33},{2,66}... | collective-permute-start | bytes 1376264 | tf_op jit(solution)/shard_map/ppermute | solution.py:73
  263.2 21.9 %slice-start = ((s8[7340032]{0:T(1024)(128)(4,1)}), s8[4194304]{0:T(1024)(128)(4,1)S(1)}, s32[]{:S(2)}) async-start(s8[7340032]{0:T(1024)(128)(4,1)} %bitcast.233), calls=%async_computation.4 | async-start | bytes 8388608
  263.2 21.9 %slice-start.1 = ((s8[7340032]{0:T(1024)(128)(4,1)}), s8[3145728]{0:T(1024)(128)(4,1)S(1)}, s32[]{:S(2)}) async-start(s8[7340032]{0:T(1024)(128)(4,1)} %bitcast.233), calls=%async_computation.5 | async-start | bytes 6291456
  263.2 11.8 %collective-permute-start.38 = (bf16[2,128,896]{2,1,0:T(8,128)(2,1)S(1)}, bf16[2,128,896]{2,1,0:T(8,128)(2,1)S(1)}, u32[]{:S(2)}, u32[]{:S(2)}) collective-permute-start(bf16[2,128,896]{2,1,0:T(8,128)(2,1)S(1)} %get-tuple-element.14), channel_id=1, source_target_pairs={{0,96},{32,0},{64,32},{96,64},{1,97},{33,1},{65,33},{97,65},{2,98}... | collective-permute-start | bytes 1376264 | tf_op jit(solution)/shard_map/ppermute | solution.py:73
  272.8 12.3 %copy-start.11 = (bf16[1024,896]{1,0:T(8,128)(2,1)S(1)}, bf16[1024,896]{1,0:T(8,128)(2,1)}, u32[]{:S(2)}) copy-start(bf16[1024,896]{1,0:T(8,128)(2,1)} %all-gather.3.cloned.1.call-done) | copy-start | bytes 5505028
  275.4 14.7 %collective-permute-start.39 = (f32[128,896]{1,0:T(8,128)S(1)}, f32[128,896]{1,0:T(8,128)S(1)}, u32[]{:S(2)}, u32[]{:S(2)}) collective-permute-start(f32[128,896]{1,0:T(8,128)S(1)} %dynamic-slice_bitcast_fusion), channel_id=1, source_target_pairs={{0,16},{16,0},{1,17},{17,1},{2,18},{18,2},{3,19},{19,3},{4,20},{20... | collective-permute-start | bytes 1376264 | tf_op jit(solution)/shard_map/ppermute | solution.py:130
  285.1 6.6 %copy-start.1 = (bf16[3584,448]{0,1:T(8,128)(2,1)S(1)}, bf16[3584,448]{0,1:T(8,128)(2,1)}, u32[]{:S(2)}) copy-start(bf16[3584,448]{0,1:T(8,128)(2,1)} %param.6) | copy-start | bytes 9633796
Sparse Core Ops, SparseCore 0:
  10.3 28.6 all-gather.2
  62.4 93.7 reduce-scatter.1
  161.4 89.9 all-gather.4
where the time goes:
time: 299 us; the launch traced here: 298 us
  waiting for transfers between devices  144 us (48%)
  starting transfers between devices  71.3 us (24%)
  matrix products  38.2 us (13%)
  local copies, waits for them, and re-layouts  18.2 us (6%)
  between operations  14.9 us (5%)
  other arithmetic  11.2 us (4%)
    ppermute x18, waiting for transfers between devices, ring_ag(): cur = lax.ppermute(cur, ax, perm)  52.7 us
    ppermute x18, waiting for transfers between devices, ring_rs(): acc = lax.ppermute(acc, ax, perm)  45.9 us
    ppermute x18, starting transfers between devices, ring_rs(): acc = lax.ppermute(acc, ax, perm)  31.8 us
    all_gather x1, waiting for transfers between devices, shards(): lax.all_gather(jnp.concatenate([page_tokens, upstream], 1), ROW, axis=0,...  28.4 us
    ppermute x18, starting transfers between devices, ring_ag(): cur = lax.ppermute(cur, ax, perm)  24.6 us
    reduce_scatter x1, waiting for transfers between devices, shards(): lax.psum_scatter(contract_last(upstream_all, weight_out).astype(jnp.bfloa...  14.3 us
    dot_general x2, matrix products, contract_last(): lax.dot_general(left, right, (((1,), (1,)), ((), ())), preferred_element_...  13.6 us
    dot_general x2, matrix products, contract_first(): lax.dot_general(left, right, (((0,), (0,)), ((), ())), preferred_element_...  12.7 us
  transfers between devices with their start and end apart: 43, of which 28 were waited for; matrix products, arithmetic and copies ran while one was open for 14% of the time, Pallas kernels for 0%

commit v1 on v0

--- a/solution.py
+++ b/solution.py
@@ -136,11 +136,13 @@
     features = both[:, :width]
     upstream_all = both[:, width:]
     both_ring = to_ring_order(both)
+    grad_part = contract_last(upstream_all, weight_out).astype(jnp.bfloat16)
+    grad_part, features_ring = lax.optimization_barrier((grad_part, both_ring[:, :width]))
     hidden_pre = ring_scatter_col(
-        jnp.dot(both_ring[:, :width], weight_in, preferred_element_type=jnp.float32).astype(jnp.bfloat16)
+        jnp.dot(features_ring, weight_in, preferred_element_type=jnp.float32).astype(jnp.bfloat16)
     ).astype(jnp.float32)
     grad_active = lax.psum_scatter(
-        contract_last(upstream_all, weight_out).astype(jnp.bfloat16),
+        grad_part,
         COL,
         scatter_dimension=0,
         tiled=True,

time: 299 us -> 313 us (1.047); the launches traced: 298 us -> 308 us
  starting transfers between devices: 71.3 us -> 85.3 us
  other arithmetic: 11.2 us -> 6.59 us
    reduce_scatter x1, waiting for transfers between devices: 14.3 us -> 0.01 us  [shards(): lax.psum_scatter(grad_part, COL, scatter_dimension=0, tiled=True)]
    ppermute x18, waiting for transfers between devices: 45.9 us -> 58.1 us  [ring_rs(): acc = lax.ppermute(acc, ax, perm)]
    ppermute x18, starting transfers between devices: 24.6 us -> 34.2 us  [ring_ag(): cur = lax.ppermute(cur, ax, perm)]
    ppermute x1, starting transfers between devices: 9.69 us -> 16 us  [scatter_row(): lax.ppermute(other, 'core', [(0, 1), (1, 0)])]
    add x14, other arithmetic: 5.39 us -> 0.74 us  [ring_rs(): acc + lax.dynamic_index_in_dim(blocks, (i - d * (s + 1)) % n, 0, keepdims...]
  transfers between devices with their start and end apart: 43 -> 43, of which waited for: 28 -> 27; matrix products, arithmetic and copies ran while one was open for 14% -> 11% of each run, Pallas kernels for 0% -> 0%
where the time goes in v1:
time: 313 us; the launch traced here: 308 us
  waiting for transfers between devices  145 us (46%)
  starting transfers between devices  85.3 us (27%)
  matrix products  40.1 us (13%)
  local copies, waits for them, and re-layouts  15.8 us (5%)
  between operations  14.9 us (5%)
  other arithmetic  6.59 us (2%)
    ppermute x18, waiting for transfers between devices, ring_rs(): acc = lax.ppermute(acc, ax, perm)  58.1 us
    ppermute x18, waiting for transfers between devices, ring_ag(): cur = lax.ppermute(cur, ax, perm)  54.7 us
    ppermute x18, starting transfers between devices, ring_ag(): cur = lax.ppermute(cur, ax, perm)  34.2 us
    ppermute x18, starting transfers between devices, ring_rs(): acc = lax.ppermute(acc, ax, perm)  30.5 us
    all_gather x1, waiting for transfers between devices, shards(): lax.all_gather(jnp.concatenate([page_tokens, upstream], 1), ROW, axis=0,...  28.4 us
    ppermute x1, starting transfers between devices, scatter_row(): lax.ppermute(other, 'core', [(0, 1), (1, 0)])  16 us
    dot_general x2, matrix products, contract_last(): lax.dot_general(left, right, (((1,), (1,)), ((), ())), preferred_element_...  13.6 us
    dot_general x2, matrix products, contract_first(): lax.dot_general(left, right, (((0,), (0,)), ((), ())), preferred_element_...  12.5 us
  transfers between devices with their start and end apart: 43, of which 27 were waited for; matrix products, arithmetic and copies ran while one was open for 11% of the time, Pallas kernels for 0%

profile of v1, /device:TPU:1, one launch (start us, length us, event | category | flops | bytes accessed | tf_op | source)
XLA Modules:
  0.0 307.7 jit_solution(1008080449177824174)
XLA Ops:
  7.2 1.2 copy.23
  8.4 1.0 copy.22
  10.6 28.4 %all-gather.3.cloned.1.call-done = bf16[1024,896]{1,0:T(8,128)(2,1)} async-done(((bf16[128,896]{1,0:T(8,128)(2,1)}), bf16[1024,896]{1,0:T(8,128)(2,1)}) %all-gather.3.cloned.1.call-update) | async-done | bytes 1835024 | tf_op jit(solution)/shard_map/all_gather | solution.py:135
  39.0 1.6 fusion.56
  40.9 1.2 copy-done.2
  42.1 1.1 slice.113
  44.0 6.1 %convolution_convert_fusion.1 = bf16[1024,3584]{1,0:T(8,128)(2,1)} fusion(bf16[3584,448]{0,1:T(8,128)(2,1)S(1)} %copy-done, bf16[1024,896]{1,0:T(8,128)(2,1)S(1)} %copy-done.4), kind=kOutput, calls=%fused_computation.1 | convolution fusion | flops 3292004352 | bytes 11599872 | tf_op jit(solution)/shard_map/dot_general | solution.py:24
  50.2 6.2 %convolution_convert_fusion = bf16[1024,3584]{1,0:T(8,128)(2,1)S(1)} fusion(bf16[1024,448]{1,0:T(8,128)(2,1)} %slice.113, bf16[448,3584]{1,0:T(8,128)(2,1)} %param.5), kind=kOutput, calls=%fused_computation | convolution fusion | flops 3292004352 | bytes 11468800 | tf_op jit(solution)/shard_map/dot_general | solution.py:142
  56.9 1.3 collective-permute-start.9
  58.2 1.5 collective-permute-start.12
  59.8 1.3 collective-permute-start
  61.1 1.6 collective-permute-start.3
  62.6 14.5 %collective-permute-done.9 = bf16[4,16,3584]{2,1,0:T(8,128)(2,1)S(1)} collective-permute-done((bf16[4,16,3584]{2,1,0:T(8,128)(2,1)S(1)}, bf16[4,16,3584]{2,1,0:T(8,128)(2,1)S(1)}, u32[]{:S(2)}, u32[]{:S(2)}) %collective-permute-start.9) | collective-permute-done | bytes 458784 | tf_op jit(solution)/shard_map/ppermute | solution.py:40
  77.8 1.0 collective-permute-done.12
  78.9 1.2 collective-permute-start.13
  80.7 1.8 collective-permute-start.1
  82.6 1.3 collective-permute-start.4
  83.9 14.3 %collective-permute-done.10 = bf16[4,16,3584]{2,1,0:T(8,128)(2,1)S(1)} collective-permute-done((bf16[4,16,3584]{2,1,0:T(8,128)(2,1)S(1)}, bf16[4,16,3584]{2,1,0:T(8,128)(2,1)S(1)}, u32[]{:S(2)}, u32[]{:S(2)}) %collective-permute-start.10) | collective-permute-done | bytes 458784 | tf_op jit(solution)/shard_map/ppermute | solution.py:40
  99.2 2.4 collective-permute-start.14
  102.4 1.7 collective-permute-start.2
  104.2 1.1 collective-permute-start.5
  105.3 13.7 %collective-permute-done.11 = bf16[4,16,3584]{2,1,0:T(8,128)(2,1)S(1)} collective-permute-done((bf16[4,16,3584]{2,1,0:T(8,128)(2,1)S(1)}, bf16[4,16,3584]{2,1,0:T(8,128)(2,1)S(1)}, u32[]{:S(2)}, u32[]{:S(2)}) %collective-permute-start.11) | collective-permute-done | bytes 458784 | tf_op jit(solution)/shard_map/ppermute | solution.py:40
  119.1 3.2 %collective-permute-start.15 = (bf16[2,16,3584]{2,1,0:T(8,128)(2,1)S(1)}, bf16[2,16,3584]{2,1,0:T(8,128)(2,1)S(1)}, u32[]{:S(2)}, u32[]{:S(2)}) collective-permute-start(bf16[2,16,3584]{2,1,0:T(8,128)(2,1)S(1)} %fusion.35), channel_id=1, source_target_pairs={{0,12},{4,0},{8,4},{12,8},{1,13},{5,1},{9,5},{13,9},{2,14},{6,2},{... | collective-permute-start | bytes 688136 | tf_op jit(solution)/shard_map/ppermute | solution.py:40
  122.5 1.2 collective-permute-start.6
  123.7 1.9 collective-permute-done.15
  125.6 3.5 %collective-permute-start.16 = (bf16[2,16,3584]{2,1,0:T(8,128)(2,1)S(1)}, bf16[2,16,3584]{2,1,0:T(8,128)(2,1)S(1)}, u32[]{:S(2)}, u32[]{:S(2)}) collective-permute-start(bf16[2,16,3584]{2,1,0:T(8,128)(2,1)S(1)} %fusion.38), channel_id=1, source_target_pairs={{0,12},{4,0},{8,4},{12,8},{1,13},{5,1},{9,5},{13,9},{2,14},{6,2},{... | collective-permute-start | bytes 688136 | tf_op jit(solution)/shard_map/ppermute | solution.py:40
  129.8 6.3 %collective-permute-done.16 = bf16[2,16,3584]{2,1,0:T(8,128)(2,1)S(1)} collective-permute-done((bf16[2,16,3584]{2,1,0:T(8,128)(2,1)S(1)}, bf16[2,16,3584]{2,1,0:T(8,128)(2,1)S(1)}, u32[]{:S(2)}, u32[]{:S(2)}) %collective-permute-start.16) | collective-permute-done | bytes 229408 | tf_op jit(solution)/shard_map/ppermute | solution.py:40
  136.1 3.6 %collective-permute-start.17 = (bf16[2,16,3584]{2,1,0:T(8,128)(2,1)S(1)}, bf16[2,16,3584]{2,1,0:T(8,128)(2,1)S(1)}, u32[]{:S(2)}, u32[]{:S(2)}) collective-permute-start(bf16[2,16,3584]{2,1,0:T(8,128)(2,1)S(1)} %fusion.41), channel_id=1, source_target_pairs={{0,12},{4,0},{8,4},{12,8},{1,13},{5,1},{9,5},{13,9},{2,14},{6,2},{... | collective-permute-start | bytes 688136 | tf_op jit(solution)/shard_map/ppermute | solution.py:40
  139.7 2.2 collective-permute-start.8
  141.9 3.2 %collective-permute-done.17 = bf16[2,16,3584]{2,1,0:T(8,128)(2,1)S(1)} collective-permute-done((bf16[2,16,3584]{2,1,0:T(8,128)(2,1)S(1)}, bf16[2,16,3584]{2,1,0:T(8,128)(2,1)S(1)}, u32[]{:S(2)}, u32[]{:S(2)}) %collective-permute-start.17) | collective-permute-done | bytes 229408 | tf_op jit(solution)/shard_map/ppermute | solution.py:40
  145.2 1.4 collective-permute-done.8
  147.5 2.8 fusion.10
  151.0 2.3 collective-permute-start.27
  154.4 2.1 collective-permute-done.27
  156.6 3.1 %collective-permute-start.28 = (bf16[2,16,3584]{2,1,0:T(8,128)(2,1)}, bf16[2,16,3584]{2,1,0:T(8,128)(2,1)S(1)}, u32[]{:S(2)}, u32[]{:S(2)}) collective-permute-start(bf16[2,16,3584]{2,1,0:T(8,128)(2,1)} %collective-permute-done.27), channel_id=1, source_target_pairs={{0,12},{4,0},{8,4},{12,8},{1,13},{5,1},{9,5},{13,9},{2,14},{6,2},{... | collective-permute-start | bytes 688136 | tf_op jit(solution)/shard_map/ppermute | solution.py:52
  159.7 1.0 bitcast_dynamic-update-slice_fusion.18
  161.7 2.7 collective-permute-done.28
  164.5 2.5 collective-permute-start.29
  167.1 7.7 %collective-permute-done.29 = bf16[2,16,3584]{2,1,0:T(8,128)(2,1)S(1)} collective-permute-done((bf16[2,16,3584]{2,1,0:T(8,128)(2,1)S(1)}, bf16[2,16,3584]{2,1,0:T(8,128)(2,1)S(1)}, u32[]{:S(2)}, u32[]{:S(2)}) %collective-permute-start.29) | collective-permute-done | bytes 229408 | tf_op jit(solution)/shard_map/ppermute | solution.py:52
  175.3 1.5 collective-permute-start.30
  177.2 3.5 %collective-permute-start.24 = (bf16[4,16,3584]{2,1,0:T(8,128)(2,1)S(1)}, bf16[4,16,3584]{2,1,0:T(8,128)(2,1)S(1)}, u32[]{:S(2)}, u32[]{:S(2)}) collective-permute-start(bf16[4,16,3584]{2,1,0:T(8,128)(2,1)S(1)} %get-tuple-element.28), channel_id=1, source_target_pairs={{0,12},{4,0},{8,4},{12,8},{1,13},{5,1},{9,5},{13,9},{2,14},{6,2},{... | collective-permute-start | bytes 1376264 | tf_op jit(solution)/shard_map/ppermute | solution.py:52
  181.0 5.7 %collective-permute-done.33 = bf16[4,16,3584]{2,1,0:T(8,128)(2,1)S(1)} collective-permute-done((bf16[4,16,3584]{2,1,0:T(8,128)(2,1)S(1)}, bf16[4,16,3584]{2,1,0:T(8,128)(2,1)S(1)}, u32[]{:S(2)}, u32[]{:S(2)}) %collective-permute-start.33) | collective-permute-done | bytes 458784 | tf_op jit(solution)/shard_map/ppermute | solution.py:52
  186.6 1.6 collective-permute-start.34
  188.3 2.0 collective-permute-done.30
  190.9 1.5 collective-permute-start.25
  192.6 9.0 %collective-permute-done.34 = bf16[4,16,3584]{2,1,0:T(8,128)(2,1)S(1)} collective-permute-done((bf16[4,16,3584]{2,1,0:T(8,128)(2,1)S(1)}, bf16[4,16,3584]{2,1,0:T(8,128)(2,1)S(1)}, u32[]{:S(2)}, u32[]{:S(2)}) %collective-permute-start.34) | collective-permute-done | bytes 458784 | tf_op jit(solution)/shard_map/ppermute | solution.py:52
  201.6 3.5 %collective-permute-start.35 = (bf16[4,16,3584]{2,1,0:T(8,128)(2,1)S(1)}, bf16[4,16,3584]{2,1,0:T(8,128)(2,1)S(1)}, u32[]{:S(2)}, u32[]{:S(2)}) collective-permute-start(bf16[4,16,3584]{2,1,0:T(8,128)(2,1)S(1)} %collective-permute-done.34), channel_id=1, source_target_pairs={{0,3},{1,0},{2,1},{3,2},{4,7},{5,4},{6,5},{7,6},{8,11},{9,8},{10,9... | collective-permute-start | bytes 1376264 | tf_op jit(solution)/shard_map/ppermute | solution.py:52
  205.1 2.8 collective-permute-done.31
  207.9 1.1 collective-permute-start.32
  209.1 1.5 collective-permute-done.25
  210.6 3.5 %collective-permute-start.26 = (bf16[4,16,3584]{2,1,0:T(8,128)(2,1)S(1)}, bf16[4,16,3584]{2,1,0:T(8,128)(2,1)S(1)}, u32[]{:S(2)}, u32[]{:S(2)}) collective-permute-start(bf16[4,16,3584]{2,1,0:T(8,128)(2,1)S(1)} %collective-permute-done.25), channel_id=1, source_target_pairs={{0,12},{4,0},{8,4},{12,8},{1,13},{5,1},{9,5},{13,9},{2,14},{6,2},{... | collective-permute-start | bytes 1376264 | tf_op jit(solution)/shard_map/ppermute | solution.py:52
  214.1 9.3 %collective-permute-start.23 = (bf16[4,16,3584]{2,1,0:T(8,128)(2,1)S(1)}, bf16[4,16,3584]{2,1,0:T(8,128)(2,1)S(1)}, u32[]{:S(2)}, u32[]{:S(2)}) collective-permute-start(bf16[4,16,3584]{2,1,0:T(8,128)(2,1)S(1)} %collective-permute-done.22), channel_id=1, source_target_pairs={{0,4},{4,8},{8,12},{12,0},{1,5},{5,9},{9,13},{13,1},{2,6},{6,10},{... | collective-permute-start | bytes 1376264 | tf_op jit(solution)/shard_map/ppermute | solution.py:52
  223.5 1.1 collective-permute-done.35
  224.7 5.5 %collective-permute-done.32 = bf16[4,16,3584]{2,1,0:T(8,128)(2,1)S(1)} collective-permute-done((bf16[4,16,3584]{2,1,0:T(8,128)(2,1)S(1)}, bf16[4,16,3584]{2,1,0:T(8,128)(2,1)S(1)}, u32[]{:S(2)}, u32[]{:S(2)}) %collective-permute-start.32) | collective-permute-done | bytes 458784 | tf_op jit(solution)/shard_map/ppermute | solution.py:52
  230.2 3.6 %collective-permute-done.26 = bf16[4,16,3584]{2,1,0:T(8,128)(2,1)S(1)} collective-permute-done((bf16[4,16,3584]{2,1,0:T(8,128)(2,1)S(1)}, bf16[4,16,3584]{2,1,0:T(8,128)(2,1)S(1)}, u32[]{:S(2)}, u32[]{:S(2)}) %collective-permute-start.26) | collective-permute-done | bytes 458784 | tf_op jit(solution)/shard_map/ppermute | solution.py:52
  233.8 10.8 %collective-permute-done.23 = bf16[4,16,3584]{2,1,0:T(8,128)(2,1)S(1)} collective-permute-done((bf16[4,16,3584]{2,1,0:T(8,128)(2,1)S(1)}, bf16[4,16,3584]{2,1,0:T(8,128)(2,1)S(1)}, u32[]{:S(2)}, u32[]{:S(2)}) %collective-permute-start.23) | collective-permute-done | bytes 458784 | tf_op jit(solution)/shard_map/ppermute | solution.py:52
  244.7 7.8 %convolution_convert_fusion.5 = bf16[1024,448]{0,1:T(8,128)(2,1)S(1)} fusion(bf16[3584,448]{0,1:T(8,128)(2,1)S(1)} %copy-done, bf16[256,3584]{1,0:T(8,128)(2,1)S(1)} %bitcast.224, bf16[256,3584]{1,0:T(8,128)(2,1)S(1)} %bitcast.222, bf16[256,3584]{1,0:T(8,128)(2,1)S(1)} %bitcast.226, bf16[256,3584]{1,0:T(8,128)(2,1)S(1)} %bitcast.220), kind=kOutput, calls=%fused_computation.22 | convolution fusion | flops 3318153216 | bytes 11468800 | tf_op jit(solution)/shard_map/dot_general | solution.py:155
  253.6 7.5 %convolution_convert_fusion.4 = bf16[1024,448]{0,1:T(8,128)(2,1)S(1)} fusion(bf16[1024,3584]{1,0:T(8,128)(2,1)} %all-gather.5.cloned.1.call-done, bf16[448,3584]{1,0:T(8,128)(2,1)} %param.5), kind=kOutput, calls=%fused_computation.21 | convolution fusion | flops 3288793088 | bytes 11468800 | tf_op jit(solution)/shard_map/dot_general | solution.py:24
  262.2 2.1 collective-permute-start.38
  264.3 2.5 collective-permute-start.37
  266.8 7.6 %convolution_convert_fusion.2 = bf16[3584,448]{0,1:T(8,128)(2,1)} fusion(bf16[256,3584]{1,0:T(8,128)(2,1)} %bitcast.225, bf16[256,3584]{1,0:T(8,128)(2,1)} %bitcast.223, bf16[256,3584]{1,0:T(8,128)(2,1)} %bitcast.227, bf16[256,3584]{1,0:T(8,128)(2,1)} %bitcast.221, bf16[1024,896]{1,0:T(8,128)(2,1)S(1)} %copy-done.3), kind=kOutput, calls=%fused_computation.3 | convolution fusion | flops 3319300096 | bytes 11599872 | tf_op jit(solution)/shard_map/dot_general | solution.py:30
  274.3 3.7 %collective-permute-done.36 = bf16[2,128,896]{2,1,0:T(8,128)(2,1)S(1)} collective-permute-done((bf16[2,128,896]{2,1,0:T(8,128)(2,1)S(1)}, bf16[2,128,896]{2,1,0:T(8,128)(2,1)S(1)}, u32[]{:S(2)}, u32[]{:S(2)}) %collective-permute-start.36) | collective-permute-done | bytes 458784 | tf_op jit(solution)/shard_map/ppermute | solution.py:73
  278.4 16.0 %collective-permute-start.39 = (f32[128,896]{1,0:T(8,128)S(1)}, f32[128,896]{1,0:T(8,128)S(1)}, u32[]{:S(2)}, u32[]{:S(2)}) collective-permute-start(f32[128,896]{1,0:T(8,128)S(1)} %dynamic-slice_bitcast_fusion), channel_id=1, source_target_pairs={{0,16},{16,0},{1,17},{17,1},{2,18},{18,2},{3,19},{19,3},{4,20},{20... | collective-permute-start | bytes 1376264 | tf_op jit(solution)/shard_map/ppermute | solution.py:130
  294.4 4.9 %convolution_convert_fusion.3 = bf16[448,3584]{1,0:T(8,128)(2,1)} fusion(bf16[1024,3584]{1,0:T(8,128)(2,1)S(1)} %bitcast.235, bf16[1024,896]{1,0:T(8,128)(2,1)S(1)} %copy-done.5), kind=kOutput, calls=%fused_computation.4 | convolution fusion | flops 3289939968 | bytes 11599872 | tf_op jit(solution)/shard_map/dot_general | solution.py:30
  (140 shorter events, 17.1 us)
Async XLA Ops:
  7.2 36.0 %copy-start = (bf16[3584,448]{0,1:T(8,128)(2,1)S(1)}, bf16[3584,448]{0,1:T(8,128)(2,1)}, u32[]{:S(2)}) copy-start(bf16[3584,448]{0,1:T(8,128)(2,1)} %param.6) | copy-start | bytes 9633796
  7.2 31.9 %all-gather.3.cloned.1.call-start = ((), (), s32[]{:S(2)}) async-start(), calls=%async_computation.1 | async-start | bytes 2064384 | tf_op jit(solution)/shard_map/all_gather | solution.py:135
  10.2 137.3 %reduce-scatter.2.cloned.1.call-start = ((), (), s32[]{:S(2)}) async-start(), calls=%async_computation.2 | async-start | bytes 7798784 | tf_op jit(solution)/shard_map/reduce_scatter | solution.py:144
  40.9 1.2 copy-start.2
  42.1 1.9 copy-start.4
  50.1 203.5 %all-gather.5.cloned.1.call-start = ((), (), s32[]{:S(2)}) async-start(), calls=%async_computation.3 | async-start | bytes 7798784 | tf_op jit(solution)/shard_map/all_gather | solution.py:151
  56.9 20.2 %collective-permute-start.9 = (bf16[4,16,3584]{2,1,0:T(8,128)(2,1)S(1)}, bf16[4,16,3584]{2,1,0:T(8,128)(2,1)S(1)}, u32[]{:S(2)}, u32[]{:S(2)}) collective-permute-start(bf16[4,16,3584]{2,1,0:T(8,128)(2,1)S(1)} %dynamic-slice_bitcast_fusion.2), channel_id=1, source_target_pairs={{0,1},{1,2},{2,3},{3,0},{4,5},{5,6},{6,7},{7,4},{8,9},{9,10},{10,1... | collective-permute-start | bytes 1376264 | tf_op jit(solution)/shard_map/ppermute | solution.py:40
  58.2 20.7 %collective-permute-start.12 = (bf16[4,16,3584]{2,1,0:T(8,128)(2,1)S(1)}, bf16[4,16,3584]{2,1,0:T(8,128)(2,1)S(1)}, u32[]{:S(2)}, u32[]{:S(2)}) collective-permute-start(bf16[4,16,3584]{2,1,0:T(8,128)(2,1)S(1)} %dynamic-slice_bitcast_fusion.1), channel_id=1, source_target_pairs={{0,3},{1,0},{2,1},{3,2},{4,7},{5,4},{6,5},{7,6},{8,11},{9,8},{10,9... | collective-permute-start | bytes 1376264 | tf_op jit(solution)/shard_map/ppermute | solution.py:40
  59.8 20.9 %collective-permute-start = (bf16[4,16,3584]{2,1,0:T(8,128)(2,1)S(1)}, bf16[4,16,3584]{2,1,0:T(8,128)(2,1)S(1)}, u32[]{:S(2)}, u32[]{:S(2)}) collective-permute-start(bf16[4,16,3584]{2,1,0:T(8,128)(2,1)S(1)} %dynamic-slice_bitcast_fusion.4), channel_id=1, source_target_pairs={{0,4},{4,8},{8,12},{12,0},{1,5},{5,9},{9,13},{13,1},{2,6},{6,10},{... | collective-permute-start | bytes 1376264 | tf_op jit(solution)/shard_map/ppermute | solution.py:40
  61.1 21.5 %collective-permute-start.3 = (bf16[4,16,3584]{2,1,0:T(8,128)(2,1)S(1)}, bf16[4,16,3584]{2,1,0:T(8,128)(2,1)S(1)}, u32[]{:S(2)}, u32[]{:S(2)}) collective-permute-start(bf16[4,16,3584]{2,1,0:T(8,128)(2,1)S(1)} %dynamic-slice_bitcast_fusion.3), channel_id=1, source_target_pairs={{0,12},{4,0},{8,4},{12,8},{1,13},{5,1},{9,5},{13,9},{2,14},{6,2},{... | collective-permute-start | bytes 1376264 | tf_op jit(solution)/shard_map/ppermute | solution.py:40
  77.2 21.0 %collective-permute-start.10 = (bf16[4,16,3584]{2,1,0:T(8,128)(2,1)S(1)}, bf16[4,16,3584]{2,1,0:T(8,128)(2,1)S(1)}, u32[]{:S(2)}, u32[]{:S(2)}) collective-permute-start(bf16[4,16,3584]{2,1,0:T(8,128)(2,1)S(1)} %bitcast_add_fusion.6), channel_id=1, source_target_pairs={{0,1},{1,2},{2,3},{3,0},{4,5},{5,6},{6,7},{7,4},{8,9},{9,10},{10,1... | collective-permute-start | bytes 1376264 | tf_op jit(solution)/shard_map/ppermute | solution.py:40
  78.9 20.2 %collective-permute-start.13 = (bf16[4,16,3584]{2,1,0:T(8,128)(2,1)S(1)}, bf16[4,16,3584]{2,1,0:T(8,128)(2,1)S(1)}, u32[]{:S(2)}, u32[]{:S(2)}) collective-permute-start(bf16[4,16,3584]{2,1,0:T(8,128)(2,1)S(1)} %bitcast_add_fusion.3), channel_id=1, source_target_pairs={{0,3},{1,0},{2,1},{3,2},{4,7},{5,4},{6,5},{7,6},{8,11},{9,8},{10,9... | collective-permute-start | bytes 1376264 | tf_op jit(solution)/shard_map/ppermute | solution.py:40
  80.7 21.6 %collective-permute-start.1 = (bf16[4,16,3584]{2,1,0:T(8,128)(2,1)S(1)}, bf16[4,16,3584]{2,1,0:T(8,128)(2,1)S(1)}, u32[]{:S(2)}, u32[]{:S(2)}) collective-permute-start(bf16[4,16,3584]{2,1,0:T(8,128)(2,1)S(1)} %bitcast_add_fusion.12), channel_id=1, source_target_pairs={{0,4},{4,8},{8,12},{12,0},{1,5},{5,9},{9,13},{13,1},{2,6},{6,10},{... | collective-permute-start | bytes 1376264 | tf_op jit(solution)/shard_map/ppermute | solution.py:40
  82.6 21.5 %collective-permute-start.4 = (bf16[4,16,3584]{2,1,0:T(8,128)(2,1)S(1)}, bf16[4,16,3584]{2,1,0:T(8,128)(2,1)S(1)}, u32[]{:S(2)}, u32[]{:S(2)}) collective-permute-start(bf16[4,16,3584]{2,1,0:T(8,128)(2,1)S(1)} %bitcast_add_fusion.9), channel_id=1, source_target_pairs={{0,12},{4,0},{8,4},{12,8},{1,13},{5,1},{9,5},{13,9},{2,14},{6,2},{... | collective-permute-start | bytes 1376264 | tf_op jit(solution)/shard_map/ppermute | solution.py:40
  98.2 20.7 %collective-permute-start.11 = (bf16[4,16,3584]{2,1,0:T(8,128)(2,1)S(1)}, bf16[4,16,3584]{2,1,0:T(8,128)(2,1)S(1)}, u32[]{:S(2)}, u32[]{:S(2)}) collective-permute-start(bf16[4,16,3584]{2,1,0:T(8,128)(2,1)S(1)} %bitcast_add_fusion.5), channel_id=1, source_target_pairs={{0,1},{1,2},{2,3},{3,0},{4,5},{5,6},{6,7},{7,4},{8,9},{9,10},{10,1... | collective-permute-start | bytes 1376264 | tf_op jit(solution)/shard_map/ppermute | solution.py:40
  99.2 19.8 %collective-permute-start.14 = (bf16[4,16,3584]{2,1,0:T(8,128)(2,1)S(1)}, bf16[4,16,3584]{2,1,0:T(8,128)(2,1)S(1)}, u32[]{:S(2)}, u32[]{:S(2)}) collective-permute-start(bf16[4,16,3584]{2,1,0:T(8,128)(2,1)S(1)} %bitcast_add_fusion.2), channel_id=1, source_target_pairs={{0,3},{1,0},{2,1},{3,2},{4,7},{5,4},{6,5},{7,6},{8,11},{9,8},{10,9... | collective-permute-start | bytes 1376264 | tf_op jit(solution)/shard_map/ppermute | solution.py:40
  102.4 19.9 %collective-permute-start.2 = (bf16[4,16,3584]{2,1,0:T(8,128)(2,1)S(1)}, bf16[4,16,3584]{2,1,0:T(8,128)(2,1)S(1)}, u32[]{:S(2)}, u32[]{:S(2)}) collective-permute-start(bf16[4,16,3584]{2,1,0:T(8,128)(2,1)S(1)} %bitcast_add_fusion.11), channel_id=1, source_target_pairs={{0,4},{4,8},{8,12},{12,0},{1,5},{5,9},{9,13},{13,1},{2,6},{6,10},{... | collective-permute-start | bytes 1376264 | tf_op jit(solution)/shard_map/ppermute | solution.py:40
  104.2 18.2 %collective-permute-start.5 = (bf16[4,16,3584]{2,1,0:T(8,128)(2,1)S(1)}, bf16[4,16,3584]{2,1,0:T(8,128)(2,1)S(1)}, u32[]{:S(2)}, u32[]{:S(2)}) collective-permute-start(bf16[4,16,3584]{2,1,0:T(8,128)(2,1)S(1)} %bitcast_add_fusion.8), channel_id=1, source_target_pairs={{0,12},{4,0},{8,4},{12,8},{1,13},{5,1},{9,5},{13,9},{2,14},{6,2},{... | collective-permute-start | bytes 1376264 | tf_op jit(solution)/shard_map/ppermute | solution.py:40
  119.1 6.5 %collective-permute-start.15 = (bf16[2,16,3584]{2,1,0:T(8,128)(2,1)S(1)}, bf16[2,16,3584]{2,1,0:T(8,128)(2,1)S(1)}, u32[]{:S(2)}, u32[]{:S(2)}) collective-permute-start(bf16[2,16,3584]{2,1,0:T(8,128)(2,1)S(1)} %fusion.35), channel_id=1, source_target_pairs={{0,12},{4,0},{8,4},{12,8},{1,13},{5,1},{9,5},{13,9},{2,14},{6,2},{... | collective-permute-start | bytes 688136 | tf_op jit(solution)/shard_map/ppermute | solution.py:40
  122.5 6.8 %collective-permute-start.6 = (bf16[2,16,3584]{2,1,0:T(8,128)(2,1)S(1)}, bf16[2,16,3584]{2,1,0:T(8,128)(2,1)S(1)}, u32[]{:S(2)}, u32[]{:S(2)}) collective-permute-start(bf16[2,16,3584]{2,1,0:T(8,128)(2,1)S(1)} %fusion.46), channel_id=1, source_target_pairs={{0,1},{1,2},{2,3},{3,0},{4,5},{5,6},{6,7},{7,4},{8,9},{9,10},{10,1... | collective-permute-start | bytes 688136 | tf_op jit(solution)/shard_map/ppermute | solution.py:40
  125.6 10.4 %collective-permute-start.16 = (bf16[2,16,3584]{2,1,0:T(8,128)(2,1)S(1)}, bf16[2,16,3584]{2,1,0:T(8,128)(2,1)S(1)}, u32[]{:S(2)}, u32[]{:S(2)}) collective-permute-start(bf16[2,16,3584]{2,1,0:T(8,128)(2,1)S(1)} %fusion.38), channel_id=1, source_target_pairs={{0,12},{4,0},{8,4},{12,8},{1,13},{5,1},{9,5},{13,9},{2,14},{6,2},{... | collective-permute-start | bytes 688136 | tf_op jit(solution)/shard_map/ppermute | solution.py:40
  129.3 10.4 %collective-permute-start.7 = (bf16[2,16,3584]{2,1,0:T(8,128)(2,1)S(1)}, bf16[2,16,3584]{2,1,0:T(8,128)(2,1)S(1)}, u32[]{:S(2)}, u32[]{:S(2)}) collective-permute-start(bf16[2,16,3584]{2,1,0:T(8,128)(2,1)S(1)} %fusion.49), channel_id=1, source_target_pairs={{0,1},{1,2},{2,3},{3,0},{4,5},{5,6},{6,7},{7,4},{8,9},{9,10},{10,1... | collective-permute-start | bytes 688136 | tf_op jit(solution)/shard_map/ppermute | solution.py:40
  136.1 9.1 %collective-permute-start.17 = (bf16[2,16,3584]{2,1,0:T(8,128)(2,1)S(1)}, bf16[2,16,3584]{2,1,0:T(8,128)(2,1)S(1)}, u32[]{:S(2)}, u32[]{:S(2)}) collective-permute-start(bf16[2,16,3584]{2,1,0:T(8,128)(2,1)S(1)} %fusion.41), channel_id=1, source_target_pairs={{0,12},{4,0},{8,4},{12,8},{1,13},{5,1},{9,5},{13,9},{2,14},{6,2},{... | collective-permute-start | bytes 688136 | tf_op jit(solution)/shard_map/ppermute | solution.py:40
  139.7 6.9 %collective-permute-start.8 = (bf16[2,16,3584]{2,1,0:T(8,128)(2,1)S(1)}, bf16[2,16,3584]{2,1,0:T(8,128)(2,1)S(1)}, u32[]{:S(2)}, u32[]{:S(2)}) collective-permute-start(bf16[2,16,3584]{2,1,0:T(8,128)(2,1)S(1)} %fusion.52), channel_id=1, source_target_pairs={{0,1},{1,2},{2,3},{3,0},{4,5},{5,6},{6,7},{7,4},{8,9},{9,10},{10,1... | collective-permute-start | bytes 688136 | tf_op jit(solution)/shard_map/ppermute | solution.py:40
  151.0 5.6 %collective-permute-start.27 = (bf16[2,16,3584]{2,1,0:T(8,128)(2,1)}, bf16[2,16,3584]{2,1,0:T(8,128)(2,1)}, u32[]{:S(2)}, u32[]{:S(2)}) collective-permute-start(bf16[2,16,3584]{2,1,0:T(8,128)(2,1)} %bitcast.61), channel_id=1, source_target_pairs={{0,12},{4,0},{8,4},{12,8},{1,13},{5,1},{9,5},{13,9},{2,14},{6,2},{... | collective-permute-start | bytes 688136 | tf_op jit(solution)/shard_map/ppermute | solution.py:52
  153.3 7.4 %collective-permute-start.18 = (bf16[2,16,3584]{2,1,0:T(8,128)(2,1)S(1)}, bf16[2,16,3584]{2,1,0:T(8,128)(2,1)}, u32[]{:S(2)}, u32[]{:S(2)}) collective-permute-start(bf16[2,16,3584]{2,1,0:T(8,128)(2,1)S(1)} %bitcast.232), channel_id=1, source_target_pairs={{0,1},{1,2},{2,3},{3,0},{4,5},{5,6},{6,7},{7,4},{8,9},{9,10},{10,1... | collective-permute-start | bytes 688136 | tf_op jit(solution)/shard_map/ppermute | solution.py:52
  156.6 7.9 %collective-permute-start.28 = (bf16[2,16,3584]{2,1,0:T(8,128)(2,1)}, bf16[2,16,3584]{2,1,0:T(8,128)(2,1)S(1)}, u32[]{:S(2)}, u32[]{:S(2)}) collective-permute-start(bf16[2,16,3584]{2,1,0:T(8,128)(2,1)} %collective-permute-done.27), channel_id=1, source_target_pairs={{0,12},{4,0},{8,4},{12,8},{1,13},{5,1},{9,5},{13,9},{2,14},{6,2},{... | collective-permute-start | bytes 688136 | tf_op jit(solution)/shard_map/ppermute | solution.py:52
  160.7 6.4 %collective-permute-start.19 = (bf16[2,16,3584]{2,1,0:T(8,128)(2,1)}, bf16[2,16,3584]{2,1,0:T(8,128)(2,1)S(1)}, u32[]{:S(2)}, u32[]{:S(2)}) collective-permute-start(bf16[2,16,3584]{2,1,0:T(8,128)(2,1)} %collective-permute-done.18), channel_id=1, source_target_pairs={{0,1},{1,2},{2,3},{3,0},{4,5},{5,6},{6,7},{7,4},{8,9},{9,10},{10,1... | collective-permute-start | bytes 688136 | tf_op jit(solution)/shard_map/ppermute | solution.py:52
  164.5 10.3 %collective-permute-start.29 = (bf16[2,16,3584]{2,1,0:T(8,128)(2,1)S(1)}, bf16[2,16,3584]{2,1,0:T(8,128)(2,1)S(1)}, u32[]{:S(2)}, u32[]{:S(2)}) collective-permute-start(bf16[2,16,3584]{2,1,0:T(8,128)(2,1)S(1)} %collective-permute-done.28), channel_id=1, source_target_pairs={{0,12},{4,0},{8,4},{12,8},{1,13},{5,1},{9,5},{13,9},{2,14},{6,2},{... | collective-permute-start | bytes 688136 | tf_op jit(solution)/shard_map/ppermute | solution.py:52
  167.0 9.8 %collective-permute-start.20 = (bf16[2,16,3584]{2,1,0:T(8,128)(2,1)S(1)}, bf16[2,16,3584]{2,1,0:T(8,128)(2,1)S(1)}, u32[]{:S(2)}, u32[]{:S(2)}) collective-permute-start(bf16[2,16,3584]{2,1,0:T(8,128)(2,1)S(1)} %collective-permute-done.19), channel_id=1, source_target_pairs={{0,1},{1,2},{2,3},{3,0},{4,5},{5,6},{6,7},{7,4},{8,9},{9,10},{10,1... | collective-permute-start | bytes 688136 | tf_op jit(solution)/shard_map/ppermute | solution.py:52
  175.0 11.6 %collective-permute-start.33 = (bf16[4,16,3584]{2,1,0:T(8,128)(2,1)S(1)}, bf16[4,16,3584]{2,1,0:T(8,128)(2,1)S(1)}, u32[]{:S(2)}, u32[]{:S(2)}) collective-permute-start(bf16[4,16,3584]{2,1,0:T(8,128)(2,1)S(1)} %get-tuple-element.30), channel_id=1, source_target_pairs={{0,3},{1,0},{2,1},{3,2},{4,7},{5,4},{6,5},{7,6},{8,11},{9,8},{10,9... | collective-permute-start | bytes 1376264 | tf_op jit(solution)/shard_map/ppermute | solution.py:52
  175.3 15.0 %collective-permute-start.30 = (bf16[4,16,3584]{2,1,0:T(8,128)(2,1)S(1)}, bf16[4,16,3584]{2,1,0:T(8,128)(2,1)S(1)}, u32[]{:S(2)}, u32[]{:S(2)}) collective-permute-start(bf16[4,16,3584]{2,1,0:T(8,128)(2,1)S(1)} %get-tuple-element.29), channel_id=1, source_target_pairs={{0,1},{1,2},{2,3},{3,0},{4,5},{5,6},{6,7},{7,4},{8,9},{9,10},{10,1... | collective-permute-start | bytes 1376264 | tf_op jit(solution)/shard_map/ppermute | solution.py:52
  177.2 13.7 %collective-permute-start.24 = (bf16[4,16,3584]{2,1,0:T(8,128)(2,1)S(1)}, bf16[4,16,3584]{2,1,0:T(8,128)(2,1)S(1)}, u32[]{:S(2)}, u32[]{:S(2)}) collective-permute-start(bf16[4,16,3584]{2,1,0:T(8,128)(2,1)S(1)} %get-tuple-element.28), channel_id=1, source_target_pairs={{0,12},{4,0},{8,4},{12,8},{1,13},{5,1},{9,5},{13,9},{2,14},{6,2},{... | collective-permute-start | bytes 1376264 | tf_op jit(solution)/shard_map/ppermute | solution.py:52
  180.7 11.6 %collective-permute-start.21 = (bf16[4,16,3584]{2,1,0:T(8,128)(2,1)S(1)}, bf16[4,16,3584]{2,1,0:T(8,128)(2,1)S(1)}, u32[]{:S(2)}, u32[]{:S(2)}) collective-permute-start(bf16[4,16,3584]{2,1,0:T(8,128)(2,1)S(1)} %get-tuple-element.27), channel_id=1, source_target_pairs={{0,4},{4,8},{8,12},{12,0},{1,5},{5,9},{9,13},{13,1},{2,6},{6,10},{... | collective-permute-start | bytes 1376264 | tf_op jit(solution)/shard_map/ppermute | solution.py:52
  186.6 15.0 %collective-permute-start.34 = (bf16[4,16,3584]{2,1,0:T(8,128)(2,1)S(1)}, bf16[4,16,3584]{2,1,0:T(8,128)(2,1)S(1)}, u32[]{:S(2)}, u32[]{:S(2)}) collective-permute-start(bf16[4,16,3584]{2,1,0:T(8,128)(2,1)S(1)} %collective-permute-done.33), channel_id=1, source_target_pairs={{0,3},{1,0},{2,1},{3,2},{4,7},{5,4},{6,5},{7,6},{8,11},{9,8},{10,9... | collective-permute-start | bytes 1376264 | tf_op jit(solution)/shard_map/ppermute | solution.py:52
  190.3 17.6 %collective-permute-start.31 = (bf16[4,16,3584]{2,1,0:T(8,128)(2,1)S(1)}, bf16[4,16,3584]{2,1,0:T(8,128)(2,1)S(1)}, u32[]{:S(2)}, u32[]{:S(2)}) collective-permute-start(bf16[4,16,3584]{2,1,0:T(8,128)(2,1)S(1)} %collective-permute-done.30), channel_id=1, source_target_pairs={{0,1},{1,2},{2,3},{3,0},{4,5},{5,6},{6,7},{7,4},{8,9},{9,10},{10,1... | collective-permute-start | bytes 1376264 | tf_op jit(solution)/shard_map/ppermute | solution.py:52
  190.9 19.7 %collective-permute-start.25 = (bf16[4,16,3584]{2,1,0:T(8,128)(2,1)S(1)}, bf16[4,16,3584]{2,1,0:T(8,128)(2,1)S(1)}, u32[]{:S(2)}, u32[]{:S(2)}) collective-permute-start(bf16[4,16,3584]{2,1,0:T(8,128)(2,1)S(1)} %collective-permute-done.24), channel_id=1, source_target_pairs={{0,12},{4,0},{8,4},{12,8},{1,13},{5,1},{9,5},{13,9},{2,14},{6,2},{... | collective-permute-start | bytes 1376264 | tf_op jit(solution)/shard_map/ppermute | solution.py:52
  192.4 21.7 %collective-permute-start.22 = (bf16[4,16,3584]{2,1,0:T(8,128)(2,1)S(1)}, bf16[4,16,3584]{2,1,0:T(8,128)(2,1)S(1)}, u32[]{:S(2)}, u32[]{:S(2)}) collective-permute-start(bf16[4,16,3584]{2,1,0:T(8,128)(2,1)S(1)} %collective-permute-done.21), channel_id=1, source_target_pairs={{0,4},{4,8},{8,12},{12,0},{1,5},{5,9},{9,13},{13,1},{2,6},{6,10},{... | collective-permute-start | bytes 1376264 | tf_op jit(solution)/shard_map/ppermute | solution.py:52
  201.6 23.0 %collective-permute-start.35 = (bf16[4,16,3584]{2,1,0:T(8,128)(2,1)S(1)}, bf16[4,16,3584]{2,1,0:T(8,128)(2,1)S(1)}, u32[]{:S(2)}, u32[]{:S(2)}) collective-permute-start(bf16[4,16,3584]{2,1,0:T(8,128)(2,1)S(1)} %collective-permute-done.34), channel_id=1, source_target_pairs={{0,3},{1,0},{2,1},{3,2},{4,7},{5,4},{6,5},{7,6},{8,11},{9,8},{10,9... | collective-permute-start | bytes 1376264 | tf_op jit(solution)/shard_map/ppermute | solution.py:52
  207.9 22.2 %collective-permute-start.32 = (bf16[4,16,3584]{2,1,0:T(8,128)(2,1)S(1)}, bf16[4,16,3584]{2,1,0:T(8,128)(2,1)S(1)}, u32[]{:S(2)}, u32[]{:S(2)}) collective-permute-start(bf16[4,16,3584]{2,1,0:T(8,128)(2,1)S(1)} %collective-permute-done.31), channel_id=1, source_target_pairs={{0,1},{1,2},{2,3},{3,0},{4,5},{5,6},{6,7},{7,4},{8,9},{9,10},{10,1... | collective-permute-start | bytes 1376264 | tf_op jit(solution)/shard_map/ppermute | solution.py:52
  210.6 23.2 %collective-permute-start.26 = (bf16[4,16,3584]{2,1,0:T(8,128)(2,1)S(1)}, bf16[4,16,3584]{2,1,0:T(8,128)(2,1)S(1)}, u32[]{:S(2)}, u32[]{:S(2)}) collective-permute-start(bf16[4,16,3584]{2,1,0:T(8,128)(2,1)S(1)} %collective-permute-done.25), channel_id=1, source_target_pairs={{0,12},{4,0},{8,4},{12,8},{1,13},{5,1},{9,5},{13,9},{2,14},{6,2},{... | collective-permute-start | bytes 1376264 | tf_op jit(solution)/shard_map/ppermute | solution.py:52
  214.1 30.6 %collective-permute-start.23 = (bf16[4,16,3584]{2,1,0:T(8,128)(2,1)S(1)}, bf16[4,16,3584]{2,1,0:T(8,128)(2,1)S(1)}, u32[]{:S(2)}, u32[]{:S(2)}) collective-permute-start(bf16[4,16,3584]{2,1,0:T(8,128)(2,1)S(1)} %collective-permute-done.22), channel_id=1, source_target_pairs={{0,4},{4,8},{8,12},{12,0},{1,5},{5,9},{9,13},{13,1},{2,6},{6,10},{... | collective-permute-start | bytes 1376264 | tf_op jit(solution)/shard_map/ppermute | solution.py:52
  224.7 27.9 %copy-start.8 = (bf16[4,4,16,3584]{3,2,1,0:T(8,128)(2,1)}, bf16[4,4,16,3584]{3,2,1,0:T(8,128)(2,1)S(1)}, u32[]{:S(2)}) copy-start(bf16[4,4,16,3584]{3,2,1,0:T(8,128)(2,1)S(1)} %bitcast_dynamic-update-slice_fusion) | copy-start | bytes 5505028
  230.2 22.4 %copy-start.7 = (bf16[4,4,16,3584]{3,2,1,0:T(8,128)(2,1)}, bf16[4,4,16,3584]{3,2,1,0:T(8,128)(2,1)S(1)}, u32[]{:S(2)}) copy-start(bf16[4,4,16,3584]{3,2,1,0:T(8,128)(2,1)S(1)} %bitcast_dynamic-update-slice_fusion.4) | copy-start | bytes 5505028
  233.8 18.8 %copy-start.9 = (bf16[4,4,16,3584]{3,2,1,0:T(8,128)(2,1)}, bf16[4,4,16,3584]{3,2,1,0:T(8,128)(2,1)S(1)}, u32[]{:S(2)}) copy-start(bf16[4,4,16,3584]{3,2,1,0:T(8,128)(2,1)S(1)} %bitcast_dynamic-update-slice_fusion.8) | copy-start | bytes 5505028
  244.7 7.9 %copy-start.6 = (bf16[4,4,16,3584]{3,2,1,0:T(8,128)(2,1)}, bf16[4,4,16,3584]{3,2,1,0:T(8,128)(2,1)S(1)}, u32[]{:S(2)}) copy-start(bf16[4,4,16,3584]{3,2,1,0:T(8,128)(2,1)S(1)} %bitcast_dynamic-update-slice_fusion.12) | copy-start | bytes 5505028
  261.6 5.1 %copy-start.3 = (bf16[1024,896]{1,0:T(8,128)(2,1)S(1)}, bf16[1024,896]{1,0:T(8,128)(2,1)}, u32[]{:S(2)}) copy-start(bf16[1024,896]{1,0:T(8,128)(2,1)} %copy-done.2) | copy-start | bytes 5505028
  262.2 12.2 %collective-permute-start.38 = (bf16[2,128,896]{2,1,0:T(8,128)(2,1)S(1)}, bf16[2,128,896]{2,1,0:T(8,128)(2,1)S(1)}, u32[]{:S(2)}, u32[]{:S(2)}) collective-permute-start(bf16[2,128,896]{2,1,0:T(8,128)(2,1)S(1)} %get-tuple-element.18), channel_id=1, source_target_pairs={{0,96},{32,0},{64,32},{96,64},{1,97},{33,1},{65,33},{97,65},{2,98}... | collective-permute-start | bytes 1376264 | tf_op jit(solution)/shard_map/ppermute | solution.py:73
  264.3 10.0 %collective-permute-start.37 = (bf16[2,128,896]{2,1,0:T(8,128)(2,1)S(1)}, bf16[2,128,896]{2,1,0:T(8,128)(2,1)S(1)}, u32[]{:S(2)}, u32[]{:S(2)}) collective-permute-start(bf16[2,128,896]{2,1,0:T(8,128)(2,1)S(1)} %get-tuple-element.17), channel_id=1, source_target_pairs={{0,64},{32,96},{64,0},{96,32},{1,65},{33,97},{65,1},{97,33},{2,66}... | collective-permute-start | bytes 1376264 | tf_op jit(solution)/shard_map/ppermute | solution.py:73
  266.8 27.6 %slice-start = ((s8[7340032]{0:T(1024)(128)(4,1)}), s8[4194304]{0:T(1024)(128)(4,1)S(1)}, s32[]{:S(2)}) async-start(s8[7340032]{0:T(1024)(128)(4,1)} %bitcast.234), calls=%async_computation.4 | async-start | bytes 8388608
  266.8 27.6 %slice-start.1 = ((s8[7340032]{0:T(1024)(128)(4,1)}), s8[3145728]{0:T(1024)(128)(4,1)S(1)}, s32[]{:S(2)}) async-start(s8[7340032]{0:T(1024)(128)(4,1)} %bitcast.234), calls=%async_computation.5 | async-start | bytes 6291456
  266.8 11.3 %collective-permute-start.36 = (bf16[2,128,896]{2,1,0:T(8,128)(2,1)S(1)}, bf16[2,128,896]{2,1,0:T(8,128)(2,1)S(1)}, u32[]{:S(2)}, u32[]{:S(2)}) collective-permute-start(bf16[2,128,896]{2,1,0:T(8,128)(2,1)S(1)} %get-tuple-element.16), channel_id=1, source_target_pairs={{0,32},{32,64},{64,96},{96,0},{1,33},{33,65},{65,97},{97,1},{2,34}... | collective-permute-start | bytes 1376264 | tf_op jit(solution)/shard_map/ppermute | solution.py:73
  274.3 20.0 %copy-start.5 = (bf16[1024,896]{1,0:T(8,128)(2,1)S(1)}, bf16[1024,896]{1,0:T(8,128)(2,1)}, u32[]{:S(2)}) copy-start(bf16[1024,896]{1,0:T(8,128)(2,1)} %all-gather.3.cloned.1.call-done) | copy-start | bytes 5505028
  278.4 20.9 %collective-permute-start.39 = (f32[128,896]{1,0:T(8,128)S(1)}, f32[128,896]{1,0:T(8,128)S(1)}, u32[]{:S(2)}, u32[]{:S(2)}) collective-permute-start(f32[128,896]{1,0:T(8,128)S(1)} %dynamic-slice_bitcast_fusion), channel_id=1, source_target_pairs={{0,16},{16,0},{1,17},{17,1},{2,18},{18,2},{3,19},{19,3},{4,20},{20... | collective-permute-start | bytes 1376264 | tf_op jit(solution)/shard_map/ppermute | solution.py:130
  294.4 6.6 %copy-start.1 = (bf16[3584,448]{0,1:T(8,128)(2,1)S(1)}, bf16[3584,448]{0,1:T(8,128)(2,1)}, u32[]{:S(2)}) copy-start(bf16[3584,448]{0,1:T(8,128)(2,1)} %param.6) | copy-start | bytes 9633796
Sparse Core Ops, SparseCore 0:
  10.3 28.6 all-gather.2
  50.2 95.7 reduce-scatter.1
  153.4 92.2 all-gather.4

commit v2 on v0

--- a/solution.py
+++ b/solution.py
@@ -153,7 +153,7 @@
         jnp.dot(active, weight_out, preferred_element_type=jnp.float32).astype(jnp.bfloat16)
     )
     tokens_part = contract_last(grad_hidden, weight_in).astype(jnp.bfloat16)
-    outs = scatter_row(jnp.concatenate([out_part, tokens_part], 1))
+    outs = lax.psum_scatter(jnp.concatenate([out_part, tokens_part], 1), ROW, scatter_dimension=0, tiled=True)
     block_out = outs[:, :width]
     grad_tokens = outs[:, width:]
     grad_weight_in = contract_first(features, grad_hidden).astype(jnp.bfloat16)

time: 299 us -> 314 us (1.050)
  waiting for transfers between devices: 144 us -> 163 us
  starting transfers between devices: 71.3 us -> 58.9 us
  local copies, waits for them, and re-layouts: 18.2 us -> 23.1 us
  matrix products: 38.2 us -> 41.6 us
    unnamed x3 -> x5, waiting for transfers between devices: 0.05 us -> 23.6 us
    ppermute x4 -> x0, starting transfers between devices: 14.7 us -> none  [the longest x1 9.69 us: scatter_row(): lax.ppermute(other, 'core', [(0, 1), (1, 0)])]
    unnamed x46 -> x43, local copies, waits for them, and re-layouts: 6.18 us -> 10.1 us
    dot_general x2, matrix products: 12.7 us -> 16 us  [contract_first(): lax.dot_general(left, right, (((0,), (0,)), ((), ())), preferred_element_...]
  transfers between devices with their start and end apart: 43 -> 40, of which waited for: 28 -> 27; matrix products, arithmetic and copies ran while one was open for 14% -> 14% of each run, Pallas kernels for 0% -> 0%
where the time goes in v2:
time: 314 us; the launch traced here: 311 us
  waiting for transfers between devices  163 us (52%)
  starting transfers between devices  58.9 us (19%)
  matrix products  41.6 us (13%)
  local copies, waits for them, and re-layouts  23.1 us (7%)
  between operations  14.8 us (5%)
  other arithmetic  10.5 us (3%)
    ppermute x18, waiting for transfers between devices, ring_ag(): cur = lax.ppermute(cur, ax, perm)  51.2 us
    ppermute x18, waiting for transfers between devices, ring_rs(): acc = lax.ppermute(acc, ax, perm)  45.4 us
    ppermute x18, starting transfers between devices, ring_rs(): acc = lax.ppermute(acc, ax, perm)  32.4 us
    all_gather x1, waiting for transfers between devices, shards(): lax.all_gather(jnp.concatenate([page_tokens, upstream], 1), ROW, axis=0,...  28.5 us
    ppermute x18, starting transfers between devices, ring_ag(): cur = lax.ppermute(cur, ax, perm)  26.3 us
    unnamed x5, waiting for transfers between devices  23.6 us
    dot_general x2, matrix products, contract_first(): lax.dot_general(left, right, (((0,), (0,)), ((), ())), preferred_element_...  16 us
    reduce_scatter x1, waiting for transfers between devices, shards(): lax.psum_scatter(contract_last(upstream_all, weight_out).astype(jnp.bfloa...  13.8 us
  transfers between devices with their start and end apart: 40, of which 27 were waited for; matrix products, arithmetic and copies ran while one was open for 14% of the time, Pallas kernels for 0%

profile of v2, /device:TPU:1, one launch (start us, length us, event | category | flops | bytes accessed | tf_op | source)
XLA Modules:
  0.0 311.4 jit_solution(12686602120287096205)
XLA Ops:
  7.2 1.2 copy.23
  8.4 1.0 copy.24
  10.5 28.5 %all-gather.3.cloned.1.call-done = bf16[1024,896]{1,0:T(8,128)(2,1)} async-done(((bf16[128,896]{1,0:T(8,128)(2,1)}), bf16[1024,896]{1,0:T(8,128)(2,1)}) %all-gather.3.cloned.1.call-update) | async-done | bytes 1835024 | tf_op jit(solution)/shard_map/all_gather | solution.py:135
  39.0 1.6 fusion.46
  40.9 1.2 copy-done.12
  42.1 1.2 copy-done.18
  43.3 4.2 %convolution_convert_fusion.1 = bf16[1024,3584]{1,0:T(8,128)(2,1)S(1)} fusion(bf16[448,3584]{1,0:T(8,128)(2,1)S(1)} %copy-done.18, bf16[1024,896]{1,0:T(8,128)(2,1)S(1)} %pad_maximum_fusion.1), kind=kOutput, calls=%fused_computation.1 | convolution fusion | flops 3292004352 | bytes 11599872 | tf_op jit(solution)/shard_map/dot_general | solution.py:140
  48.8 2.4 collective-permute-start.3
  52.9 2.5 collective-permute-start.12
  56.2 6.1 %convolution_convert_fusion = bf16[1024,3584]{1,0:T(8,128)(2,1)} fusion(bf16[3584,448]{0,1:T(8,128)(2,1)S(1)} %copy-done, bf16[1024,896]{1,0:T(8,128)(2,1)S(1)} %copy-done.10), kind=kOutput, calls=%fused_computation | convolution fusion | flops 3292004352 | bytes 11599872 | tf_op jit(solution)/shard_map/dot_general | solution.py:24
  62.4 1.3 bitcast_add_fusion.8
  63.8 2.7 collective-permute-start.4
  66.5 1.2 bitcast_add_fusion.11
  67.8 1.3 bitcast_add_fusion.2
  69.2 2.7 collective-permute-start.13
  71.9 1.1 bitcast_add_fusion.5
  73.1 4.7 %collective-permute-done.4 = bf16[4,16,3584]{2,1,0:T(8,128)(2,1)S(1)} collective-permute-done((bf16[4,16,3584]{2,1,0:T(8,128)(2,1)S(1)}, bf16[4,16,3584]{2,1,0:T(8,128)(2,1)S(1)}, u32[]{:S(2)}, u32[]{:S(2)}) %collective-permute-start.4) | collective-permute-done | bytes 458784 | tf_op jit(solution)/shard_map/ppermute | solution.py:40
  77.9 3.5 %collective-permute-start.5 = (bf16[4,16,3584]{2,1,0:T(8,128)(2,1)S(1)}, bf16[4,16,3584]{2,1,0:T(8,128)(2,1)S(1)}, u32[]{:S(2)}, u32[]{:S(2)}) collective-permute-start(bf16[4,16,3584]{2,1,0:T(8,128)(2,1)S(1)} %bitcast_add_fusion.7), channel_id=1, source_target_pairs={{0,12},{4,0},{8,4},{12,8},{1,13},{5,1},{9,5},{13,9},{2,14},{6,2},{... | collective-permute-start | bytes 1376264 | tf_op jit(solution)/shard_map/ppermute | solution.py:40
  81.4 2.1 collective-permute-done.1
  83.6 5.3 %collective-permute-done.13 = bf16[4,16,3584]{2,1,0:T(8,128)(2,1)S(1)} collective-permute-done((bf16[4,16,3584]{2,1,0:T(8,128)(2,1)S(1)}, bf16[4,16,3584]{2,1,0:T(8,128)(2,1)S(1)}, u32[]{:S(2)}, u32[]{:S(2)}) %collective-permute-start.13) | collective-permute-done | bytes 458784 | tf_op jit(solution)/shard_map/ppermute | solution.py:40
  88.9 3.6 %collective-permute-start.14 = (bf16[4,16,3584]{2,1,0:T(8,128)(2,1)S(1)}, bf16[4,16,3584]{2,1,0:T(8,128)(2,1)S(1)}, u32[]{:S(2)}, u32[]{:S(2)}) collective-permute-start(bf16[4,16,3584]{2,1,0:T(8,128)(2,1)S(1)} %bitcast_add_fusion.1), channel_id=1, source_target_pairs={{0,3},{1,0},{2,1},{3,2},{4,7},{5,4},{6,5},{7,6},{8,11},{9,8},{10,9... | collective-permute-start | bytes 1376264 | tf_op jit(solution)/shard_map/ppermute | solution.py:40
  93.1 3.0 collective-permute-done.5
  96.2 6.1 %collective-permute-done.2 = bf16[4,16,3584]{2,1,0:T(8,128)(2,1)S(1)} collective-permute-done((bf16[4,16,3584]{2,1,0:T(8,128)(2,1)S(1)}, bf16[4,16,3584]{2,1,0:T(8,128)(2,1)S(1)}, u32[]{:S(2)}, u32[]{:S(2)}) %collective-permute-start.2) | collective-permute-done | bytes 458784 | tf_op jit(solution)/shard_map/ppermute | solution.py:40
  102.4 1.3 collective-permute-start.6
  103.7 7.2 %collective-permute-done.14 = bf16[4,16,3584]{2,1,0:T(8,128)(2,1)S(1)} collective-permute-done((bf16[4,16,3584]{2,1,0:T(8,128)(2,1)S(1)}, bf16[4,16,3584]{2,1,0:T(8,128)(2,1)S(1)}, u32[]{:S(2)}, u32[]{:S(2)}) %collective-permute-start.14) | collective-permute-done | bytes 458784 | tf_op jit(solution)/shard_map/ppermute | solution.py:40
  111.8 5.0 %collective-permute-start.15 = (bf16[2,16,3584]{2,1,0:T(8,128)(2,1)S(1)}, bf16[2,16,3584]{2,1,0:T(8,128)(2,1)S(1)}, u32[]{:S(2)}, u32[]{:S(2)}) collective-permute-start(bf16[2,16,3584]{2,1,0:T(8,128)(2,1)S(1)} %fusion.25), channel_id=1, source_target_pairs={{0,12},{4,0},{8,4},{12,8},{1,13},{5,1},{9,5},{13,9},{2,14},{6,2},{... | collective-permute-start | bytes 688136 | tf_op jit(solution)/shard_map/ppermute | solution.py:40
  116.8 4.7 %collective-permute-done.6 = bf16[2,16,3584]{2,1,0:T(8,128)(2,1)S(1)} collective-permute-done((bf16[2,16,3584]{2,1,0:T(8,128)(2,1)S(1)}, bf16[2,16,3584]{2,1,0:T(8,128)(2,1)S(1)}, u32[]{:S(2)}, u32[]{:S(2)}) %collective-permute-start.6) | collective-permute-done | bytes 229408 | tf_op jit(solution)/shard_map/ppermute | solution.py:40
  121.5 1.4 collective-permute-start.7
  123.0 3.7 %collective-permute-start.16 = (bf16[2,16,3584]{2,1,0:T(8,128)(2,1)S(1)}, bf16[2,16,3584]{2,1,0:T(8,128)(2,1)S(1)}, u32[]{:S(2)}, u32[]{:S(2)}) collective-permute-start(bf16[2,16,3584]{2,1,0:T(8,128)(2,1)S(1)} %fusion.28), channel_id=1, source_target_pairs={{0,12},{4,0},{8,4},{12,8},{1,13},{5,1},{9,5},{13,9},{2,14},{6,2},{... | collective-permute-start | bytes 688136 | tf_op jit(solution)/shard_map/ppermute | solution.py:40
  126.7 5.5 %collective-permute-done.7 = bf16[2,16,3584]{2,1,0:T(8,128)(2,1)S(1)} collective-permute-done((bf16[2,16,3584]{2,1,0:T(8,128)(2,1)S(1)}, bf16[2,16,3584]{2,1,0:T(8,128)(2,1)S(1)}, u32[]{:S(2)}, u32[]{:S(2)}) %collective-permute-start.7) | collective-permute-done | bytes 229408 | tf_op jit(solution)/shard_map/ppermute | solution.py:40
  133.1 3.0 collective-permute-start.17
  136.1 2.5 collective-permute-done.8
  138.6 2.5 collective-permute-done.17
  142.0 13.8 %reduce-scatter.5.cloned.1.call-done = bf16[64,3584]{1,0:T(8,128)(2,1)} async-done(((bf16[1024,3584]{1,0:T(8,128)(2,1)}), bf16[64,3584]{1,0:T(8,128)(2,1)}) %reduce-scatter.5.cloned.1.call-update) | async-done | bytes 458768 | tf_op jit(solution)/shard_map/reduce_scatter | solution.py:142
  155.8 2.8 fusion.6
  159.7 1.2 collective-permute-start.27
  162.1 3.6 %collective-permute-done.18 = bf16[2,16,3584]{2,1,0:T(8,128)(2,1)} collective-permute-done((bf16[2,16,3584]{2,1,0:T(8,128)(2,1)}, bf16[2,16,3584]{2,1,0:T(8,128)(2,1)}, u32[]{:S(2)}, u32[]{:S(2)}) %collective-permute-start.18) | collective-permute-done | bytes 229408 | tf_op jit(solution)/shard_map/ppermute | solution.py:52
  165.7 1.0 bitcast_dynamic-update-slice_fusion.21
  166.7 2.1 collective-permute-start.28
  169.8 2.2 collective-permute-done.19
  172.1 3.3 %collective-permute-start.29 = (bf16[2,16,3584]{2,1,0:T(8,128)(2,1)S(1)}, bf16[2,16,3584]{2,1,0:T(8,128)(2,1)S(1)}, u32[]{:S(2)}, u32[]{:S(2)}) collective-permute-start(bf16[2,16,3584]{2,1,0:T(8,128)(2,1)S(1)} %collective-permute-done.28), channel_id=1, source_target_pairs={{0,12},{4,0},{8,4},{12,8},{1,13},{5,1},{9,5},{13,9},{2,14},{6,2},{... | collective-permute-start | bytes 688136 | tf_op jit(solution)/shard_map/ppermute | solution.py:52
  175.4 6.4 %collective-permute-done.20 = bf16[2,16,3584]{2,1,0:T(8,128)(2,1)S(1)} collective-permute-done((bf16[2,16,3584]{2,1,0:T(8,128)(2,1)S(1)}, bf16[2,16,3584]{2,1,0:T(8,128)(2,1)S(1)}, u32[]{:S(2)}, u32[]{:S(2)}) %collective-permute-start.20) | collective-permute-done | bytes 229408 | tf_op jit(solution)/shard_map/ppermute | solution.py:52
  183.2 2.1 collective-permute-start.24
  185.6 2.7 collective-permute-start.33
  188.5 4.4 %collective-permute-done.21 = bf16[4,16,3584]{2,1,0:T(8,128)(2,1)S(1)} collective-permute-done((bf16[4,16,3584]{2,1,0:T(8,128)(2,1)S(1)}, bf16[4,16,3584]{2,1,0:T(8,128)(2,1)S(1)}, u32[]{:S(2)}, u32[]{:S(2)}) %collective-permute-start.21) | collective-permute-done | bytes 458784 | tf_op jit(solution)/shard_map/ppermute | solution.py:52
  193.8 3.3 %collective-permute-start.25 = (bf16[4,16,3584]{2,1,0:T(8,128)(2,1)S(1)}, bf16[4,16,3584]{2,1,0:T(8,128)(2,1)S(1)}, u32[]{:S(2)}, u32[]{:S(2)}) collective-permute-start(bf16[4,16,3584]{2,1,0:T(8,128)(2,1)S(1)} %collective-permute-done.24), channel_id=1, source_target_pairs={{0,12},{4,0},{8,4},{12,8},{1,13},{5,1},{9,5},{13,9},{2,14},{6,2},{... | collective-permute-start | bytes 1376264 | tf_op jit(solution)/shard_map/ppermute | solution.py:52
  197.1 1.2 collective-permute-start.31
  198.3 1.9 collective-permute-start.34
  200.4 6.7 %collective-permute-done.22 = bf16[4,16,3584]{2,1,0:T(8,128)(2,1)S(1)} collective-permute-done((bf16[4,16,3584]{2,1,0:T(8,128)(2,1)S(1)}, bf16[4,16,3584]{2,1,0:T(8,128)(2,1)S(1)}, u32[]{:S(2)}, u32[]{:S(2)}) %collective-permute-start.22) | collective-permute-done | bytes 458784 | tf_op jit(solution)/shard_map/ppermute | solution.py:52
  207.4 8.1 %collective-permute-done.25 = bf16[4,16,3584]{2,1,0:T(8,128)(2,1)S(1)} collective-permute-done((bf16[4,16,3584]{2,1,0:T(8,128)(2,1)S(1)}, bf16[4,16,3584]{2,1,0:T(8,128)(2,1)S(1)}, u32[]{:S(2)}, u32[]{:S(2)}) %collective-permute-start.25) | collective-permute-done | bytes 458784 | tf_op jit(solution)/shard_map/ppermute | solution.py:52
  215.5 3.5 %collective-permute-start.26 = (bf16[4,16,3584]{2,1,0:T(8,128)(2,1)S(1)}, bf16[4,16,3584]{2,1,0:T(8,128)(2,1)S(1)}, u32[]{:S(2)}, u32[]{:S(2)}) collective-permute-start(bf16[4,16,3584]{2,1,0:T(8,128)(2,1)S(1)} %collective-permute-done.25), channel_id=1, source_target_pairs={{0,12},{4,0},{8,4},{12,8},{1,13},{5,1},{9,5},{13,9},{2,14},{6,2},{... | collective-permute-start | bytes 1376264 | tf_op jit(solution)/shard_map/ppermute | solution.py:52
  219.0 1.7 collective-permute-start.32
  220.7 1.8 collective-permute-start.35
  222.7 6.6 %collective-permute-done.23 = bf16[4,16,3584]{2,1,0:T(8,128)(2,1)S(1)} collective-permute-done((bf16[4,16,3584]{2,1,0:T(8,128)(2,1)S(1)}, bf16[4,16,3584]{2,1,0:T(8,128)(2,1)S(1)}, u32[]{:S(2)}, u32[]{:S(2)}) %collective-permute-start.23) | collective-permute-done | bytes 458784 | tf_op jit(solution)/shard_map/ppermute | solution.py:52
  229.3 8.3 %collective-permute-done.26 = bf16[4,16,3584]{2,1,0:T(8,128)(2,1)S(1)} collective-permute-done((bf16[4,16,3584]{2,1,0:T(8,128)(2,1)S(1)}, bf16[4,16,3584]{2,1,0:T(8,128)(2,1)S(1)}, u32[]{:S(2)}, u32[]{:S(2)}) %collective-permute-start.26) | collective-permute-done | bytes 458784 | tf_op jit(solution)/shard_map/ppermute | solution.py:52
  237.6 4.0 %collective-permute-done.32 = bf16[4,16,3584]{2,1,0:T(8,128)(2,1)S(1)} collective-permute-done((bf16[4,16,3584]{2,1,0:T(8,128)(2,1)S(1)}, bf16[4,16,3584]{2,1,0:T(8,128)(2,1)S(1)}, u32[]{:S(2)}, u32[]{:S(2)}) %collective-permute-start.32) | collective-permute-done | bytes 458784 | tf_op jit(solution)/shard_map/ppermute | solution.py:52
  241.7 7.8 %convolution_convert_fusion.5 = bf16[1024,448]{0,1:T(8,128)(2,1)S(1)} fusion(bf16[3584,448]{0,1:T(8,128)(2,1)S(1)} %copy-done, bf16[256,3584]{1,0:T(8,128)(2,1)S(1)} %bitcast.199, bf16[256,3584]{1,0:T(8,128)(2,1)S(1)} %bitcast.205, bf16[256,3584]{1,0:T(8,128)(2,1)S(1)} %bitcast.201, bf16[256,3584]{1,0:T(8,128)(2,1)S(1)} %bitcast.203), kind=kOutput, calls=%fused_computation.15 | convolution fusion | flops 3318153216 | bytes 11468800 | tf_op jit(solution)/shard_map/dot_general | solution.py:153
  251.1 7.5 %convolution_convert_fusion.4 = bf16[1024,448]{0,1:T(8,128)(2,1)S(1)} fusion(bf16[1024,3584]{1,0:T(8,128)(2,1)} %all-gather.5.cloned.1.call-done, bf16[448,3584]{1,0:T(8,128)(2,1)} %param.5), kind=kOutput, calls=%fused_computation.14 | convolution fusion | flops 3288793088 | bytes 11468800 | tf_op jit(solution)/shard_map/dot_general | solution.py:24
  258.8 2.5 copy.35
  261.3 1.5 copy-done.13
  262.7 7.5 %convolution_convert_fusion.2 = bf16[3584,448]{0,1:T(8,128)(2,1)} fusion(bf16[256,3584]{1,0:T(8,128)(2,1)} %bitcast.200, bf16[256,3584]{1,0:T(8,128)(2,1)} %bitcast.206, bf16[256,3584]{1,0:T(8,128)(2,1)} %bitcast.202, bf16[256,3584]{1,0:T(8,128)(2,1)} %bitcast.204, bf16[1024,896]{1,0:T(8,128)(2,1)S(1)} %copy-done.13), kind=kOutput, calls=%fused_computation.3 | convolution fusion | flops 3319300096 | bytes 11599872 | tf_op jit(solution)/shard_map/dot_general | solution.py:30
  270.3 8.4 %convolution_convert_fusion.3 = bf16[448,3584]{1,0:T(8,128)(2,1)} fusion(bf16[1024,3584]{1,0:T(8,128)(2,1)} %all-gather.5.cloned.1.call-done, bf16[1024,896]{1,0:T(8,128)(2,1)S(1)} %copy-done.11), kind=kOutput, calls=%fused_computation.4 | convolution fusion | flops 3289939968 | bytes 11599872 | tf_op jit(solution)/shard_map/dot_general | solution.py:30
  278.7 23.5 %reduce-scatter.7.cloned.1.call-done = bf16[128,896]{1,0:T(8,128)(2,1)} async-done(((bf16[1024,896]{1,0:T(8,128)(2,1)}), bf16[128,896]{1,0:T(8,128)(2,1)}) %reduce-scatter.7.cloned.1.call-update) | async-done | bytes 229392
  302.2 1.1 fusion.49
  (145 shorter events, 18.7 us)
Async XLA Ops:
  7.2 49.0 %copy-start = (bf16[3584,448]{0,1:T(8,128)(2,1)S(1)}, bf16[3584,448]{0,1:T(8,128)(2,1)}, u32[]{:S(2)}) copy-start(bf16[3584,448]{0,1:T(8,128)(2,1)} %param.6) | copy-start | bytes 9633796
  7.2 31.9 %all-gather.3.cloned.1.call-start = ((), (), s32[]{:S(2)}) async-start(), calls=%async_computation.2 | async-start | bytes 2064384 | tf_op jit(solution)/shard_map/all_gather | solution.py:135
  10.2 145.6 %reduce-scatter.5.cloned.1.call-start = ((), (), s32[]{:S(2)}) async-start(), calls=%async_computation.3 | async-start | bytes 7798784 | tf_op jit(solution)/shard_map/reduce_scatter | solution.py:142
  40.7 2.6 copy-start.18
  40.9 1.2 copy-start.12
  48.0 8.2 %copy-start.2 = (bf16[256,3584]{1,0:T(8,128)(2,1)}, bf16[256,3584]{1,0:T(8,128)(2,1)S(1)}, u32[]{:S(2)}) copy-start(bf16[256,3584]{1,0:T(8,128)(2,1)S(1)} %get-tuple-element.6) | copy-start | bytes 5505028
  48.0 8.2 %copy-start.4 = (bf16[256,3584]{1,0:T(8,128)(2,1)}, bf16[256,3584]{1,0:T(8,128)(2,1)S(1)}, u32[]{:S(2)}) copy-start(bf16[256,3584]{1,0:T(8,128)(2,1)S(1)} %get-tuple-element.5) | copy-start | bytes 5505028
  48.0 8.2 %copy-start.6 = (bf16[256,3584]{1,0:T(8,128)(2,1)}, bf16[256,3584]{1,0:T(8,128)(2,1)S(1)}, u32[]{:S(2)}) copy-start(bf16[256,3584]{1,0:T(8,128)(2,1)S(1)} %get-tuple-element.7) | copy-start | bytes 5505028
  48.0 8.2 %copy-start.8 = (bf16[256,3584]{1,0:T(8,128)(2,1)}, bf16[256,3584]{1,0:T(8,128)(2,1)S(1)}, u32[]{:S(2)}) copy-start(bf16[256,3584]{1,0:T(8,128)(2,1)S(1)} %get-tuple-element.4) | copy-start | bytes 5505028
  48.0 8.2 %copy-start.10 = (bf16[1024,896]{1,0:T(8,128)(2,1)S(1)}, bf16[1024,896]{1,0:T(8,128)(2,1)}, u32[]{:S(2)}) copy-start(bf16[1024,896]{1,0:T(8,128)(2,1)} %all-gather.3.cloned.1.call-done) | copy-start | bytes 5505028
  48.8 13.6 %collective-permute-start.3 = (bf16[4,16,3584]{2,1,0:T(8,128)(2,1)}, bf16[4,16,3584]{2,1,0:T(8,128)(2,1)}, u32[]{:S(2)}, u32[]{:S(2)}) collective-permute-start(bf16[4,16,3584]{2,1,0:T(8,128)(2,1)} %dynamic-slice_bitcast_fusion.2), channel_id=1, source_target_pairs={{0,12},{4,0},{8,4},{12,8},{1,13},{5,1},{9,5},{13,9},{2,14},{6,2},{... | collective-permute-start | bytes 1376264 | tf_op jit(solution)/shard_map/ppermute | solution.py:40
  52.1 14.4 %collective-permute-start = (bf16[4,16,3584]{2,1,0:T(8,128)(2,1)}, bf16[4,16,3584]{2,1,0:T(8,128)(2,1)}, u32[]{:S(2)}, u32[]{:S(2)}) collective-permute-start(bf16[4,16,3584]{2,1,0:T(8,128)(2,1)} %dynamic-slice_bitcast_fusion.3), channel_id=1, source_target_pairs={{0,4},{4,8},{8,12},{12,0},{1,5},{5,9},{9,13},{13,1},{2,6},{6,10},{... | collective-permute-start | bytes 1376264 | tf_op jit(solution)/shard_map/ppermute | solution.py:40
  52.9 14.9 %collective-permute-start.12 = (bf16[4,16,3584]{2,1,0:T(8,128)(2,1)}, bf16[4,16,3584]{2,1,0:T(8,128)(2,1)}, u32[]{:S(2)}, u32[]{:S(2)}) collective-permute-start(bf16[4,16,3584]{2,1,0:T(8,128)(2,1)} %dynamic-slice_bitcast_fusion), channel_id=1, source_target_pairs={{0,3},{1,0},{2,1},{3,2},{4,7},{5,4},{6,5},{7,6},{8,11},{9,8},{10,9... | collective-permute-start | bytes 1376264 | tf_op jit(solution)/shard_map/ppermute | solution.py:40
  56.2 15.7 %collective-permute-start.9 = (bf16[4,16,3584]{2,1,0:T(8,128)(2,1)}, bf16[4,16,3584]{2,1,0:T(8,128)(2,1)}, u32[]{:S(2)}, u32[]{:S(2)}) collective-permute-start(bf16[4,16,3584]{2,1,0:T(8,128)(2,1)} %dynamic-slice_bitcast_fusion.1), channel_id=1, source_target_pairs={{0,1},{1,2},{2,3},{3,0},{4,5},{5,6},{6,7},{7,4},{8,9},{9,10},{10,1... | collective-permute-start | bytes 1376264 | tf_op jit(solution)/shard_map/ppermute | solution.py:40
  62.4 188.7 %all-gather.5.cloned.1.call-start = ((), (), s32[]{:S(2)}) async-start(), calls=%async_computation.4 | async-start | bytes 7798784 | tf_op jit(solution)/shard_map/all_gather | solution.py:149
  62.4 9.5 %copy-start.3 = (bf16[256,3584]{1,0:T(8,128)(2,1)S(1)}, bf16[256,3584]{1,0:T(8,128)(2,1)}, u32[]{:S(2)}) copy-start(bf16[256,3584]{1,0:T(8,128)(2,1)} %copy-done.2) | copy-start | bytes 5505028
  63.8 14.0 %copy-start.9 = (bf16[256,3584]{1,0:T(8,128)(2,1)S(1)}, bf16[256,3584]{1,0:T(8,128)(2,1)}, u32[]{:S(2)}) copy-start(bf16[256,3584]{1,0:T(8,128)(2,1)} %copy-done.8) | copy-start | bytes 5505028
  63.8 14.0 %collective-permute-start.4 = (bf16[4,16,3584]{2,1,0:T(8,128)(2,1)S(1)}, bf16[4,16,3584]{2,1,0:T(8,128)(2,1)S(1)}, u32[]{:S(2)}, u32[]{:S(2)}) collective-permute-start(bf16[4,16,3584]{2,1,0:T(8,128)(2,1)S(1)} %bitcast_add_fusion.8), channel_id=1, source_target_pairs={{0,12},{4,0},{8,4},{12,8},{1,13},{5,1},{9,5},{13,9},{2,14},{6,2},{... | collective-permute-start | bytes 1376264 | tf_op jit(solution)/shard_map/ppermute | solution.py:40
  67.7 15.7 %copy-start.7 = (bf16[256,3584]{1,0:T(8,128)(2,1)S(1)}, bf16[256,3584]{1,0:T(8,128)(2,1)}, u32[]{:S(2)}) copy-start(bf16[256,3584]{1,0:T(8,128)(2,1)} %copy-done.6) | copy-start | bytes 5505028
  67.7 15.7 %collective-permute-start.1 = (bf16[4,16,3584]{2,1,0:T(8,128)(2,1)S(1)}, bf16[4,16,3584]{2,1,0:T(8,128)(2,1)S(1)}, u32[]{:S(2)}, u32[]{:S(2)}) collective-permute-start(bf16[4,16,3584]{2,1,0:T(8,128)(2,1)S(1)} %bitcast_add_fusion.11), channel_id=1, source_target_pairs={{0,4},{4,8},{8,12},{12,0},{1,5},{5,9},{9,13},{13,1},{2,6},{6,10},{... | collective-permute-start | bytes 1376264 | tf_op jit(solution)/shard_map/ppermute | solution.py:40
  69.2 19.7 %copy-start.5 = (bf16[256,3584]{1,0:T(8,128)(2,1)S(1)}, bf16[256,3584]{1,0:T(8,128)(2,1)}, u32[]{:S(2)}) copy-start(bf16[256,3584]{1,0:T(8,128)(2,1)} %copy-done.4) | copy-start | bytes 5505028
  69.2 19.7 %collective-permute-start.13 = (bf16[4,16,3584]{2,1,0:T(8,128)(2,1)S(1)}, bf16[4,16,3584]{2,1,0:T(8,128)(2,1)S(1)}, u32[]{:S(2)}, u32[]{:S(2)}) collective-permute-start(bf16[4,16,3584]{2,1,0:T(8,128)(2,1)S(1)} %bitcast_add_fusion.2), channel_id=1, source_target_pairs={{0,3},{1,0},{2,1},{3,2},{4,7},{5,4},{6,5},{7,6},{8,11},{9,8},{10,9... | collective-permute-start | bytes 1376264 | tf_op jit(solution)/shard_map/ppermute | solution.py:40
  73.0 19.9 %collective-permute-start.10 = (bf16[4,16,3584]{2,1,0:T(8,128)(2,1)S(1)}, bf16[4,16,3584]{2,1,0:T(8,128)(2,1)S(1)}, u32[]{:S(2)}, u32[]{:S(2)}) collective-permute-start(bf16[4,16,3584]{2,1,0:T(8,128)(2,1)S(1)} %bitcast_add_fusion.5), channel_id=1, source_target_pairs={{0,1},{1,2},{2,3},{3,0},{4,5},{5,6},{6,7},{7,4},{8,9},{9,10},{10,1... | collective-permute-start | bytes 1376264 | tf_op jit(solution)/shard_map/ppermute | solution.py:40
  77.9 18.3 %collective-permute-start.5 = (bf16[4,16,3584]{2,1,0:T(8,128)(2,1)S(1)}, bf16[4,16,3584]{2,1,0:T(8,128)(2,1)S(1)}, u32[]{:S(2)}, u32[]{:S(2)}) collective-permute-start(bf16[4,16,3584]{2,1,0:T(8,128)(2,1)S(1)} %bitcast_add_fusion.7), channel_id=1, source_target_pairs={{0,12},{4,0},{8,4},{12,8},{1,13},{5,1},{9,5},{13,9},{2,14},{6,2},{... | collective-permute-start | bytes 1376264 | tf_op jit(solution)/shard_map/ppermute | solution.py:40
  83.5 18.8 %collective-permute-start.2 = (bf16[4,16,3584]{2,1,0:T(8,128)(2,1)S(1)}, bf16[4,16,3584]{2,1,0:T(8,128)(2,1)S(1)}, u32[]{:S(2)}, u32[]{:S(2)}) collective-permute-start(bf16[4,16,3584]{2,1,0:T(8,128)(2,1)S(1)} %bitcast_add_fusion.10), channel_id=1, source_target_pairs={{0,4},{4,8},{8,12},{12,0},{1,5},{5,9},{9,13},{13,1},{2,6},{6,10},{... | collective-permute-start | bytes 1376264 | tf_op jit(solution)/shard_map/ppermute | solution.py:40
  88.9 22.0 %collective-permute-start.14 = (bf16[4,16,3584]{2,1,0:T(8,128)(2,1)S(1)}, bf16[4,16,3584]{2,1,0:T(8,128)(2,1)S(1)}, u32[]{:S(2)}, u32[]{:S(2)}) collective-permute-start(bf16[4,16,3584]{2,1,0:T(8,128)(2,1)S(1)} %bitcast_add_fusion.1), channel_id=1, source_target_pairs={{0,3},{1,0},{2,1},{3,2},{4,7},{5,4},{6,5},{7,6},{8,11},{9,8},{10,9... | collective-permute-start | bytes 1376264 | tf_op jit(solution)/shard_map/ppermute | solution.py:40
  93.0 18.7 %collective-permute-start.11 = (bf16[4,16,3584]{2,1,0:T(8,128)(2,1)S(1)}, bf16[4,16,3584]{2,1,0:T(8,128)(2,1)S(1)}, u32[]{:S(2)}, u32[]{:S(2)}) collective-permute-start(bf16[4,16,3584]{2,1,0:T(8,128)(2,1)S(1)} %bitcast_add_fusion.4), channel_id=1, source_target_pairs={{0,1},{1,2},{2,3},{3,0},{4,5},{5,6},{6,7},{7,4},{8,9},{9,10},{10,1... | collective-permute-start | bytes 1376264 | tf_op jit(solution)/shard_map/ppermute | solution.py:40
  102.4 19.1 %collective-permute-start.6 = (bf16[2,16,3584]{2,1,0:T(8,128)(2,1)S(1)}, bf16[2,16,3584]{2,1,0:T(8,128)(2,1)S(1)}, u32[]{:S(2)}, u32[]{:S(2)}) collective-permute-start(bf16[2,16,3584]{2,1,0:T(8,128)(2,1)S(1)} %fusion.36), channel_id=1, source_target_pairs={{0,1},{1,2},{2,3},{3,0},{4,5},{5,6},{6,7},{7,4},{8,9},{9,10},{10,1... | collective-permute-start | bytes 688136 | tf_op jit(solution)/shard_map/ppermute | solution.py:40
  111.8 11.1 %collective-permute-start.15 = (bf16[2,16,3584]{2,1,0:T(8,128)(2,1)S(1)}, bf16[2,16,3584]{2,1,0:T(8,128)(2,1)S(1)}, u32[]{:S(2)}, u32[]{:S(2)}) collective-permute-start(bf16[2,16,3584]{2,1,0:T(8,128)(2,1)S(1)} %fusion.25), channel_id=1, source_target_pairs={{0,12},{4,0},{8,4},{12,8},{1,13},{5,1},{9,5},{13,9},{2,14},{6,2},{... | collective-permute-start | bytes 688136 | tf_op jit(solution)/shard_map/ppermute | solution.py:40
  121.5 10.7 %collective-permute-start.7 = (bf16[2,16,3584]{2,1,0:T(8,128)(2,1)S(1)}, bf16[2,16,3584]{2,1,0:T(8,128)(2,1)S(1)}, u32[]{:S(2)}, u32[]{:S(2)}) collective-permute-start(bf16[2,16,3584]{2,1,0:T(8,128)(2,1)S(1)} %fusion.39), channel_id=1, source_target_pairs={{0,1},{1,2},{2,3},{3,0},{4,5},{5,6},{6,7},{7,4},{8,9},{9,10},{10,1... | collective-permute-start | bytes 688136 | tf_op jit(solution)/shard_map/ppermute | solution.py:40
  123.0 10.1 %collective-permute-start.16 = (bf16[2,16,3584]{2,1,0:T(8,128)(2,1)S(1)}, bf16[2,16,3584]{2,1,0:T(8,128)(2,1)S(1)}, u32[]{:S(2)}, u32[]{:S(2)}) collective-permute-start(bf16[2,16,3584]{2,1,0:T(8,128)(2,1)S(1)} %fusion.28), channel_id=1, source_target_pairs={{0,12},{4,0},{8,4},{12,8},{1,13},{5,1},{9,5},{13,9},{2,14},{6,2},{... | collective-permute-start | bytes 688136 | tf_op jit(solution)/shard_map/ppermute | solution.py:40
  132.3 6.3 %collective-permute-start.8 = (bf16[2,16,3584]{2,1,0:T(8,128)(2,1)S(1)}, bf16[2,16,3584]{2,1,0:T(8,128)(2,1)S(1)}, u32[]{:S(2)}, u32[]{:S(2)}) collective-permute-start(bf16[2,16,3584]{2,1,0:T(8,128)(2,1)S(1)} %fusion.42), channel_id=1, source_target_pairs={{0,1},{1,2},{2,3},{3,0},{4,5},{5,6},{6,7},{7,4},{8,9},{9,10},{10,1... | collective-permute-start | bytes 688136 | tf_op jit(solution)/shard_map/ppermute | solution.py:40
  133.1 8.0 %collective-permute-start.17 = (bf16[2,16,3584]{2,1,0:T(8,128)(2,1)S(1)}, bf16[2,16,3584]{2,1,0:T(8,128)(2,1)S(1)}, u32[]{:S(2)}, u32[]{:S(2)}) collective-permute-start(bf16[2,16,3584]{2,1,0:T(8,128)(2,1)S(1)} %fusion.31), channel_id=1, source_target_pairs={{0,12},{4,0},{8,4},{12,8},{1,13},{5,1},{9,5},{13,9},{2,14},{6,2},{... | collective-permute-start | bytes 688136 | tf_op jit(solution)/shard_map/ppermute | solution.py:40
  159.3 6.4 %collective-permute-start.18 = (bf16[2,16,3584]{2,1,0:T(8,128)(2,1)}, bf16[2,16,3584]{2,1,0:T(8,128)(2,1)}, u32[]{:S(2)}, u32[]{:S(2)}) collective-permute-start(bf16[2,16,3584]{2,1,0:T(8,128)(2,1)} %bitcast.44), channel_id=1, source_target_pairs={{0,1},{1,2},{2,3},{3,0},{4,5},{5,6},{6,7},{7,4},{8,9},{9,10},{10,1... | collective-permute-start | bytes 688136 | tf_op jit(solution)/shard_map/ppermute | solution.py:52
  159.7 7.0 %collective-permute-start.27 = (bf16[2,16,3584]{2,1,0:T(8,128)(2,1)S(1)}, bf16[2,16,3584]{2,1,0:T(8,128)(2,1)}, u32[]{:S(2)}, u32[]{:S(2)}) collective-permute-start(bf16[2,16,3584]{2,1,0:T(8,128)(2,1)S(1)} %bitcast.211), channel_id=1, source_target_pairs={{0,12},{4,0},{8,4},{12,8},{1,13},{5,1},{9,5},{13,9},{2,14},{6,2},{... | collective-permute-start | bytes 688136 | tf_op jit(solution)/shard_map/ppermute | solution.py:52
  160.9 141.3 %reduce-scatter.7.cloned.1.call-start = ((), (), s32[]{:S(2)}) async-start(), calls=%async_computation.5 | async-start | bytes 2064384
  165.7 6.3 %collective-permute-start.19 = (bf16[2,16,3584]{2,1,0:T(8,128)(2,1)}, bf16[2,16,3584]{2,1,0:T(8,128)(2,1)S(1)}, u32[]{:S(2)}, u32[]{:S(2)}) collective-permute-start(bf16[2,16,3584]{2,1,0:T(8,128)(2,1)} %collective-permute-done.18), channel_id=1, source_target_pairs={{0,1},{1,2},{2,3},{3,0},{4,5},{5,6},{6,7},{7,4},{8,9},{9,10},{10,1... | collective-permute-start | bytes 688136 | tf_op jit(solution)/shard_map/ppermute | solution.py:52
  166.7 5.4 %collective-permute-start.28 = (bf16[2,16,3584]{2,1,0:T(8,128)(2,1)}, bf16[2,16,3584]{2,1,0:T(8,128)(2,1)S(1)}, u32[]{:S(2)}, u32[]{:S(2)}) collective-permute-start(bf16[2,16,3584]{2,1,0:T(8,128)(2,1)} %collective-permute-done.27), channel_id=1, source_target_pairs={{0,12},{4,0},{8,4},{12,8},{1,13},{5,1},{9,5},{13,9},{2,14},{6,2},{... | collective-permute-start | bytes 688136 | tf_op jit(solution)/shard_map/ppermute | solution.py:52
  172.0 9.9 %collective-permute-start.20 = (bf16[2,16,3584]{2,1,0:T(8,128)(2,1)S(1)}, bf16[2,16,3584]{2,1,0:T(8,128)(2,1)S(1)}, u32[]{:S(2)}, u32[]{:S(2)}) collective-permute-start(bf16[2,16,3584]{2,1,0:T(8,128)(2,1)S(1)} %collective-permute-done.19), channel_id=1, source_target_pairs={{0,1},{1,2},{2,3},{3,0},{4,5},{5,6},{6,7},{7,4},{8,9},{9,10},{10,1... | collective-permute-start | bytes 688136 | tf_op jit(solution)/shard_map/ppermute | solution.py:52
  172.1 13.1 %collective-permute-start.29 = (bf16[2,16,3584]{2,1,0:T(8,128)(2,1)S(1)}, bf16[2,16,3584]{2,1,0:T(8,128)(2,1)S(1)}, u32[]{:S(2)}, u32[]{:S(2)}) collective-permute-start(bf16[2,16,3584]{2,1,0:T(8,128)(2,1)S(1)} %collective-permute-done.28), channel_id=1, source_target_pairs={{0,12},{4,0},{8,4},{12,8},{1,13},{5,1},{9,5},{13,9},{2,14},{6,2},{... | collective-permute-start | bytes 688136 | tf_op jit(solution)/shard_map/ppermute | solution.py:52
  182.2 10.7 %collective-permute-start.21 = (bf16[4,16,3584]{2,1,0:T(8,128)(2,1)S(1)}, bf16[4,16,3584]{2,1,0:T(8,128)(2,1)S(1)}, u32[]{:S(2)}, u32[]{:S(2)}) collective-permute-start(bf16[4,16,3584]{2,1,0:T(8,128)(2,1)S(1)} %get-tuple-element.16), channel_id=1, source_target_pairs={{0,4},{4,8},{8,12},{12,0},{1,5},{5,9},{9,13},{13,1},{2,6},{6,10},{... | collective-permute-start | bytes 1376264 | tf_op jit(solution)/shard_map/ppermute | solution.py:52
  183.2 10.6 %collective-permute-start.24 = (bf16[4,16,3584]{2,1,0:T(8,128)(2,1)S(1)}, bf16[4,16,3584]{2,1,0:T(8,128)(2,1)S(1)}, u32[]{:S(2)}, u32[]{:S(2)}) collective-permute-start(bf16[4,16,3584]{2,1,0:T(8,128)(2,1)S(1)} %get-tuple-element.17), channel_id=1, source_target_pairs={{0,12},{4,0},{8,4},{12,8},{1,13},{5,1},{9,5},{13,9},{2,14},{6,2},{... | collective-permute-start | bytes 1376264 | tf_op jit(solution)/shard_map/ppermute | solution.py:52
  185.6 11.6 %collective-permute-start.30 = (bf16[4,16,3584]{2,1,0:T(8,128)(2,1)S(1)}, bf16[4,16,3584]{2,1,0:T(8,128)(2,1)S(1)}, u32[]{:S(2)}, u32[]{:S(2)}) collective-permute-start(bf16[4,16,3584]{2,1,0:T(8,128)(2,1)S(1)} %get-tuple-element.18), channel_id=1, source_target_pairs={{0,1},{1,2},{2,3},{3,0},{4,5},{5,6},{6,7},{7,4},{8,9},{9,10},{10,1... | collective-permute-start | bytes 1376264 | tf_op jit(solution)/shard_map/ppermute | solution.py:52
  185.6 12.7 %collective-permute-start.33 = (bf16[4,16,3584]{2,1,0:T(8,128)(2,1)S(1)}, bf16[4,16,3584]{2,1,0:T(8,128)(2,1)S(1)}, u32[]{:S(2)}, u32[]{:S(2)}) collective-permute-start(bf16[4,16,3584]{2,1,0:T(8,128)(2,1)S(1)} %get-tuple-element.19), channel_id=1, source_target_pairs={{0,3},{1,0},{2,1},{3,2},{4,7},{5,4},{6,5},{7,6},{8,11},{9,8},{10,9... | collective-permute-start | bytes 1376264 | tf_op jit(solution)/shard_map/ppermute | solution.py:52
  192.9 14.2 %collective-permute-start.22 = (bf16[4,16,3584]{2,1,0:T(8,128)(2,1)S(1)}, bf16[4,16,3584]{2,1,0:T(8,128)(2,1)S(1)}, u32[]{:S(2)}, u32[]{:S(2)}) collective-permute-start(bf16[4,16,3584]{2,1,0:T(8,128)(2,1)S(1)} %collective-permute-done.21), channel_id=1, source_target_pairs={{0,4},{4,8},{8,12},{12,0},{1,5},{5,9},{9,13},{13,1},{2,6},{6,10},{... | collective-permute-start | bytes 1376264 | tf_op jit(solution)/shard_map/ppermute | solution.py:52
  193.8 21.7 %collective-permute-start.25 = (bf16[4,16,3584]{2,1,0:T(8,128)(2,1)S(1)}, bf16[4,16,3584]{2,1,0:T(8,128)(2,1)S(1)}, u32[]{:S(2)}, u32[]{:S(2)}) collective-permute-start(bf16[4,16,3584]{2,1,0:T(8,128)(2,1)S(1)} %collective-permute-done.24), channel_id=1, source_target_pairs={{0,12},{4,0},{8,4},{12,8},{1,13},{5,1},{9,5},{13,9},{2,14},{6,2},{... | collective-permute-start | bytes 1376264 | tf_op jit(solution)/shard_map/ppermute | solution.py:52
  197.1 21.9 %collective-permute-start.31 = (bf16[4,16,3584]{2,1,0:T(8,128)(2,1)S(1)}, bf16[4,16,3584]{2,1,0:T(8,128)(2,1)S(1)}, u32[]{:S(2)}, u32[]{:S(2)}) collective-permute-start(bf16[4,16,3584]{2,1,0:T(8,128)(2,1)S(1)} %collective-permute-done.30), channel_id=1, source_target_pairs={{0,1},{1,2},{2,3},{3,0},{4,5},{5,6},{6,7},{7,4},{8,9},{9,10},{10,1... | collective-permute-start | bytes 1376264 | tf_op jit(solution)/shard_map/ppermute | solution.py:52
  198.3 22.3 %collective-permute-start.34 = (bf16[4,16,3584]{2,1,0:T(8,128)(2,1)S(1)}, bf16[4,16,3584]{2,1,0:T(8,128)(2,1)S(1)}, u32[]{:S(2)}, u32[]{:S(2)}) collective-permute-start(bf16[4,16,3584]{2,1,0:T(8,128)(2,1)S(1)} %collective-permute-done.33), channel_id=1, source_target_pairs={{0,3},{1,0},{2,1},{3,2},{4,7},{5,4},{6,5},{7,6},{8,11},{9,8},{10,9... | collective-permute-start | bytes 1376264 | tf_op jit(solution)/shard_map/ppermute | solution.py:52
  207.1 22.1 %collective-permute-start.23 = (bf16[4,16,3584]{2,1,0:T(8,128)(2,1)S(1)}, bf16[4,16,3584]{2,1,0:T(8,128)(2,1)S(1)}, u32[]{:S(2)}, u32[]{:S(2)}) collective-permute-start(bf16[4,16,3584]{2,1,0:T(8,128)(2,1)S(1)} %collective-permute-done.22), channel_id=1, source_target_pairs={{0,4},{4,8},{8,12},{12,0},{1,5},{5,9},{9,13},{13,1},{2,6},{6,10},{... | collective-permute-start | bytes 1376264 | tf_op jit(solution)/shard_map/ppermute | solution.py:52
  215.5 22.1 %collective-permute-start.26 = (bf16[4,16,3584]{2,1,0:T(8,128)(2,1)S(1)}, bf16[4,16,3584]{2,1,0:T(8,128)(2,1)S(1)}, u32[]{:S(2)}, u32[]{:S(2)}) collective-permute-start(bf16[4,16,3584]{2,1,0:T(8,128)(2,1)S(1)} %collective-permute-done.25), channel_id=1, source_target_pairs={{0,12},{4,0},{8,4},{12,8},{1,13},{5,1},{9,5},{13,9},{2,14},{6,2},{... | collective-permute-start | bytes 1376264 | tf_op jit(solution)/shard_map/ppermute | solution.py:52
  219.0 22.6 %collective-permute-start.32 = (bf16[4,16,3584]{2,1,0:T(8,128)(2,1)S(1)}, bf16[4,16,3584]{2,1,0:T(8,128)(2,1)S(1)}, u32[]{:S(2)}, u32[]{:S(2)}) collective-permute-start(bf16[4,16,3584]{2,1,0:T(8,128)(2,1)S(1)} %collective-permute-done.31), channel_id=1, source_target_pairs={{0,1},{1,2},{2,3},{3,0},{4,5},{5,6},{6,7},{7,4},{8,9},{9,10},{10,1... | collective-permute-start | bytes 1376264 | tf_op jit(solution)/shard_map/ppermute | solution.py:52
  220.7 21.0 %collective-permute-start.35 = (bf16[4,16,3584]{2,1,0:T(8,128)(2,1)S(1)}, bf16[4,16,3584]{2,1,0:T(8,128)(2,1)S(1)}, u32[]{:S(2)}, u32[]{:S(2)}) collective-permute-start(bf16[4,16,3584]{2,1,0:T(8,128)(2,1)S(1)} %collective-permute-done.34), channel_id=1, source_target_pairs={{0,3},{1,0},{2,1},{3,2},{4,7},{5,4},{6,5},{7,6},{8,11},{9,8},{10,9... | collective-permute-start | bytes 1376264 | tf_op jit(solution)/shard_map/ppermute | solution.py:52
  229.3 20.3 %copy-start.16 = (bf16[4,4,16,3584]{3,2,1,0:T(8,128)(2,1)}, bf16[4,4,16,3584]{3,2,1,0:T(8,128)(2,1)S(1)}, u32[]{:S(2)}) copy-start(bf16[4,4,16,3584]{3,2,1,0:T(8,128)(2,1)S(1)} %bitcast_dynamic-update-slice_fusion.12) | copy-start | bytes 5505028
  237.6 12.0 %copy-start.15 = (bf16[4,4,16,3584]{3,2,1,0:T(8,128)(2,1)}, bf16[4,4,16,3584]{3,2,1,0:T(8,128)(2,1)S(1)}, u32[]{:S(2)}) copy-start(bf16[4,4,16,3584]{3,2,1,0:T(8,128)(2,1)S(1)} %bitcast_dynamic-update-slice_fusion.8) | copy-start | bytes 5505028
  241.6 7.9 %copy-start.17 = (bf16[4,4,16,3584]{3,2,1,0:T(8,128)(2,1)}, bf16[4,4,16,3584]{3,2,1,0:T(8,128)(2,1)S(1)}, u32[]{:S(2)}) copy-start(bf16[4,4,16,3584]{3,2,1,0:T(8,128)(2,1)S(1)} %bitcast_dynamic-update-slice_fusion.4) | copy-start | bytes 5505028
  241.7 7.9 %copy-start.14 = (bf16[4,4,16,3584]{3,2,1,0:T(8,128)(2,1)}, bf16[4,4,16,3584]{3,2,1,0:T(8,128)(2,1)S(1)}, u32[]{:S(2)}) copy-start(bf16[4,4,16,3584]{3,2,1,0:T(8,128)(2,1)S(1)} %bitcast_dynamic-update-slice_fusion) | copy-start | bytes 5505028
  261.2 1.5 copy-start.13
  262.7 7.5 %copy-start.11 = (bf16[1024,896]{1,0:T(8,128)(2,1)S(1)}, bf16[1024,896]{1,0:T(8,128)(2,1)}, u32[]{:S(2)}) copy-start(bf16[1024,896]{1,0:T(8,128)(2,1)} %all-gather.3.cloned.1.call-done) | copy-start | bytes 5505028
  270.3 34.6 %copy-start.1 = (bf16[3584,448]{0,1:T(8,128)(2,1)S(1)}, bf16[3584,448]{0,1:T(8,128)(2,1)}, u32[]{:S(2)}) copy-start(bf16[3584,448]{0,1:T(8,128)(2,1)} %param.6) | copy-start | bytes 9633796
Sparse Core Ops, SparseCore 0:
  10.3 28.6 all-gather.2
  62.5 93.2 reduce-scatter.4
  161.0 89.4 all-gather.4
  261.4 40.8 reduce-scatter.6

commit v3 on v0

--- a/solution.py
+++ b/solution.py
@@ -123,11 +123,11 @@
 
 def scatter_row(part):
     p4 = part.reshape(4, 2, part.shape[0] // 8, part.shape[-1])
-    acc = direct_rs(p4, "z", 4)
     c = lax.axis_index("core")
-    mine = lax.dynamic_index_in_dim(acc, c, 0, keepdims=False)
-    other = lax.dynamic_index_in_dim(acc, 1 - c, 0, keepdims=False)
-    return (mine + lax.ppermute(other, "core", [(0, 1), (1, 0)])).astype(jnp.bfloat16)
+    mine = lax.dynamic_index_in_dim(p4, c, 1, keepdims=False)
+    other = lax.dynamic_index_in_dim(p4, 1 - c, 1, keepdims=False)
+    pair = mine.astype(jnp.float32) + lax.ppermute(other, "core", [(0, 1), (1, 0)]).astype(jnp.float32)
+    return direct_rs(pair.astype(jnp.bfloat16), "z", 4).astype(jnp.bfloat16)
 
 
 def shards(page_tokens, weight_in, weight_out, upstream):

time: 299 us -> 299 us (level)
  transfers between devices with their start and end apart: 43 -> 43, of which waited for: 28 -> 29; matrix products, arithmetic and copies ran while one was open for 14% -> 14% of each run, Pallas kernels for 0% -> 0%
where the time goes in v3:
time: 299 us; the launch traced here: 297 us
  waiting for transfers between devices  144 us (48%)
  starting transfers between devices  70.2 us (23%)
  matrix products  37.9 us (13%)
  local copies, waits for them, and re-layouts  18.3 us (6%)
  between operations  14.9 us (5%)
  other arithmetic  11.2 us (4%)
    ppermute x18, waiting for transfers between devices, ring_ag(): cur = lax.ppermute(cur, ax, perm)  52.7 us
    ppermute x18, waiting for transfers between devices, ring_rs(): acc = lax.ppermute(acc, ax, perm)  45.9 us
    ppermute x18, starting transfers between devices, ring_rs(): acc = lax.ppermute(acc, ax, perm)  31.8 us
    all_gather x1, waiting for transfers between devices, shards(): lax.all_gather(jnp.concatenate([page_tokens, upstream], 1), ROW, axis=0,...  28.4 us
    ppermute x18, starting transfers between devices, ring_ag(): cur = lax.ppermute(cur, ax, perm)  24.6 us
    reduce_scatter x1, waiting for transfers between devices, shards(): lax.psum_scatter(contract_last(upstream_all, weight_out).astype(jnp.bfloa...  14.3 us
    dot_general x2, matrix products, contract_last(): lax.dot_general(left, right, (((1,), (1,)), ((), ())), preferred_element_...  13.6 us
    dot_general x2, matrix products, contract_first(): lax.dot_general(left, right, (((0,), (0,)), ((), ())), preferred_element_...  12.3 us
  transfers between devices with their start and end apart: 43, of which 29 were waited for; matrix products, arithmetic and copies ran while one was open for 14% of the time, Pallas kernels for 0%

profile of v3, /device:TPU:1, one launch (start us, length us, event | category | flops | bytes accessed | tf_op | source)
XLA Modules:
  0.0 296.8 jit_solution(10191040732510506083)
XLA Ops:
  7.2 1.2 copy.11
  10.6 28.4 %all-gather.3.cloned.1.call-done = bf16[1024,896]{1,0:T(8,128)(2,1)} async-done(((bf16[128,896]{1,0:T(8,128)(2,1)}), bf16[1024,896]{1,0:T(8,128)(2,1)}) %all-gather.3.cloned.1.call-update) | async-done | bytes 1835024 | tf_op jit(solution)/shard_map/all_gather | solution.py:135
  39.0 1.6 fusion.54
  40.9 1.2 copy-done.12
  42.1 1.2 copy-done.18
  43.3 4.2 %convolution_convert_fusion.1 = bf16[1024,3584]{1,0:T(8,128)(2,1)S(1)} fusion(bf16[448,3584]{1,0:T(8,128)(2,1)S(1)} %copy-done.18, bf16[1024,896]{1,0:T(8,128)(2,1)S(1)} %pad_maximum_fusion.1), kind=kOutput, calls=%fused_computation.1 | convolution fusion | flops 3292004352 | bytes 11599872 | tf_op jit(solution)/shard_map/dot_general | solution.py:140
  48.8 2.4 collective-permute-start.3
  52.8 2.5 collective-permute-start.12
  56.2 6.1 %convolution_convert_fusion = bf16[1024,3584]{1,0:T(8,128)(2,1)} fusion(bf16[3584,448]{0,1:T(8,128)(2,1)S(1)} %copy-done, bf16[1024,896]{1,0:T(8,128)(2,1)S(1)} %copy-done.10), kind=kOutput, calls=%fused_computation | convolution fusion | flops 3292004352 | bytes 11599872 | tf_op jit(solution)/shard_map/dot_general | solution.py:24
  62.4 1.3 bitcast_add_fusion.8
  63.7 2.7 collective-permute-start.4
  66.5 1.2 bitcast_add_fusion.11
  67.8 1.3 bitcast_add_fusion.2
  69.1 2.7 collective-permute-start.13
  71.8 1.1 bitcast_add_fusion.5
  73.1 4.6 %collective-permute-done.4 = bf16[4,16,3584]{2,1,0:T(8,128)(2,1)S(1)} collective-permute-done((bf16[4,16,3584]{2,1,0:T(8,128)(2,1)S(1)}, bf16[4,16,3584]{2,1,0:T(8,128)(2,1)S(1)}, u32[]{:S(2)}, u32[]{:S(2)}) %collective-permute-start.4) | collective-permute-done | bytes 458784 | tf_op jit(solution)/shard_map/ppermute | solution.py:40
  77.8 3.5 %collective-permute-start.5 = (bf16[4,16,3584]{2,1,0:T(8,128)(2,1)S(1)}, bf16[4,16,3584]{2,1,0:T(8,128)(2,1)S(1)}, u32[]{:S(2)}, u32[]{:S(2)}) collective-permute-start(bf16[4,16,3584]{2,1,0:T(8,128)(2,1)S(1)} %bitcast_add_fusion.7), channel_id=1, source_target_pairs={{0,12},{4,0},{8,4},{12,8},{1,13},{5,1},{9,5},{13,9},{2,14},{6,2},{... | collective-permute-start | bytes 1376264 | tf_op jit(solution)/shard_map/ppermute | solution.py:40
  81.3 2.1 collective-permute-done.1
  83.5 5.3 %collective-permute-done.13 = bf16[4,16,3584]{2,1,0:T(8,128)(2,1)S(1)} collective-permute-done((bf16[4,16,3584]{2,1,0:T(8,128)(2,1)S(1)}, bf16[4,16,3584]{2,1,0:T(8,128)(2,1)S(1)}, u32[]{:S(2)}, u32[]{:S(2)}) %collective-permute-start.13) | collective-permute-done | bytes 458784 | tf_op jit(solution)/shard_map/ppermute | solution.py:40
  88.9 3.6 %collective-permute-start.14 = (bf16[4,16,3584]{2,1,0:T(8,128)(2,1)S(1)}, bf16[4,16,3584]{2,1,0:T(8,128)(2,1)S(1)}, u32[]{:S(2)}, u32[]{:S(2)}) collective-permute-start(bf16[4,16,3584]{2,1,0:T(8,128)(2,1)S(1)} %bitcast_add_fusion.1), channel_id=1, source_target_pairs={{0,3},{1,0},{2,1},{3,2},{4,7},{5,4},{6,5},{7,6},{8,11},{9,8},{10,9... | collective-permute-start | bytes 1376264 | tf_op jit(solution)/shard_map/ppermute | solution.py:40
  93.0 3.1 %collective-permute-done.5 = bf16[4,16,3584]{2,1,0:T(8,128)(2,1)S(1)} collective-permute-done((bf16[4,16,3584]{2,1,0:T(8,128)(2,1)S(1)}, bf16[4,16,3584]{2,1,0:T(8,128)(2,1)S(1)}, u32[]{:S(2)}, u32[]{:S(2)}) %collective-permute-start.5) | collective-permute-done | bytes 458784 | tf_op jit(solution)/shard_map/ppermute | solution.py:40
  96.2 5.9 %collective-permute-done.2 = bf16[4,16,3584]{2,1,0:T(8,128)(2,1)S(1)} collective-permute-done((bf16[4,16,3584]{2,1,0:T(8,128)(2,1)S(1)}, bf16[4,16,3584]{2,1,0:T(8,128)(2,1)S(1)}, u32[]{:S(2)}, u32[]{:S(2)}) %collective-permute-start.2) | collective-permute-done | bytes 458784 | tf_op jit(solution)/shard_map/ppermute | solution.py:40
  102.3 1.5 collective-permute-start.6
  103.7 7.2 %collective-permute-done.14 = bf16[4,16,3584]{2,1,0:T(8,128)(2,1)S(1)} collective-permute-done((bf16[4,16,3584]{2,1,0:T(8,128)(2,1)S(1)}, bf16[4,16,3584]{2,1,0:T(8,128)(2,1)S(1)}, u32[]{:S(2)}, u32[]{:S(2)}) %collective-permute-start.14) | collective-permute-done | bytes 458784 | tf_op jit(solution)/shard_map/ppermute | solution.py:40
  112.0 4.6 %collective-permute-start.15 = (bf16[2,16,3584]{2,1,0:T(8,128)(2,1)S(1)}, bf16[2,16,3584]{2,1,0:T(8,128)(2,1)S(1)}, u32[]{:S(2)}, u32[]{:S(2)}) collective-permute-start(bf16[2,16,3584]{2,1,0:T(8,128)(2,1)S(1)} %fusion.33), channel_id=1, source_target_pairs={{0,12},{4,0},{8,4},{12,8},{1,13},{5,1},{9,5},{13,9},{2,14},{6,2},{... | collective-permute-start | bytes 688136 | tf_op jit(solution)/shard_map/ppermute | solution.py:40
  116.6 5.1 %collective-permute-done.6 = bf16[2,16,3584]{2,1,0:T(8,128)(2,1)S(1)} collective-permute-done((bf16[2,16,3584]{2,1,0:T(8,128)(2,1)S(1)}, bf16[2,16,3584]{2,1,0:T(8,128)(2,1)S(1)}, u32[]{:S(2)}, u32[]{:S(2)}) %collective-permute-start.6) | collective-permute-done | bytes 229408 | tf_op jit(solution)/shard_map/ppermute | solution.py:40
  121.8 1.1 collective-permute-start.7
  122.9 3.6 %collective-permute-start.16 = (bf16[2,16,3584]{2,1,0:T(8,128)(2,1)S(1)}, bf16[2,16,3584]{2,1,0:T(8,128)(2,1)S(1)}, u32[]{:S(2)}, u32[]{:S(2)}) collective-permute-start(bf16[2,16,3584]{2,1,0:T(8,128)(2,1)S(1)} %fusion.36), channel_id=1, source_target_pairs={{0,12},{4,0},{8,4},{12,8},{1,13},{5,1},{9,5},{13,9},{2,14},{6,2},{... | collective-permute-start | bytes 688136 | tf_op jit(solution)/shard_map/ppermute | solution.py:40
  126.5 5.6 %collective-permute-done.7 = bf16[2,16,3584]{2,1,0:T(8,128)(2,1)S(1)} collective-permute-done((bf16[2,16,3584]{2,1,0:T(8,128)(2,1)S(1)}, bf16[2,16,3584]{2,1,0:T(8,128)(2,1)S(1)}, u32[]{:S(2)}, u32[]{:S(2)}) %collective-permute-start.7) | collective-permute-done | bytes 229408 | tf_op jit(solution)/shard_map/ppermute | solution.py:40
  132.9 3.1 %collective-permute-start.17 = (bf16[2,16,3584]{2,1,0:T(8,128)(2,1)S(1)}, bf16[2,16,3584]{2,1,0:T(8,128)(2,1)S(1)}, u32[]{:S(2)}, u32[]{:S(2)}) collective-permute-start(bf16[2,16,3584]{2,1,0:T(8,128)(2,1)S(1)} %fusion.39), channel_id=1, source_target_pairs={{0,12},{4,0},{8,4},{12,8},{1,13},{5,1},{9,5},{13,9},{2,14},{6,2},{... | collective-permute-start | bytes 688136 | tf_op jit(solution)/shard_map/ppermute | solution.py:40
  136.0 2.5 collective-permute-done.8
  138.5 2.5 collective-permute-done.17
  141.9 14.3 %reduce-scatter.2.cloned.1.call-done = bf16[64,3584]{1,0:T(8,128)(2,1)} async-done(((bf16[1024,3584]{1,0:T(8,128)(2,1)}), bf16[64,3584]{1,0:T(8,128)(2,1)}) %reduce-scatter.2.cloned.1.call-update) | async-done | bytes 458768 | tf_op jit(solution)/shard_map/reduce_scatter | solution.py:142
  156.2 2.8 fusion.12
  159.8 1.4 collective-permute-start.27
  162.4 4.0 %collective-permute-done.18 = bf16[2,16,3584]{2,1,0:T(8,128)(2,1)} collective-permute-done((bf16[2,16,3584]{2,1,0:T(8,128)(2,1)}, bf16[2,16,3584]{2,1,0:T(8,128)(2,1)}, u32[]{:S(2)}, u32[]{:S(2)}) %collective-permute-start.18) | collective-permute-done | bytes 229408 | tf_op jit(solution)/shard_map/ppermute | solution.py:52
  167.5 1.4 collective-permute-start.28
  169.9 2.9 collective-permute-done.19
  172.8 2.7 collective-permute-start.29
  175.5 7.7 %collective-permute-done.20 = bf16[2,16,3584]{2,1,0:T(8,128)(2,1)S(1)} collective-permute-done((bf16[2,16,3584]{2,1,0:T(8,128)(2,1)S(1)}, bf16[2,16,3584]{2,1,0:T(8,128)(2,1)S(1)}, u32[]{:S(2)}, u32[]{:S(2)}) %collective-permute-start.20) | collective-permute-done | bytes 229408 | tf_op jit(solution)/shard_map/ppermute | solution.py:52
  183.8 2.7 collective-permute-start.24
  187.0 2.7 collective-permute-start.33
  189.9 2.8 collective-permute-done.21
  192.7 1.1 collective-permute-done.24
  193.8 2.4 collective-permute-start.25
  196.1 1.5 collective-permute-start.31
  197.6 2.8 collective-permute-start.34
  200.6 8.0 %collective-permute-done.22 = bf16[4,16,3584]{2,1,0:T(8,128)(2,1)S(1)} collective-permute-done((bf16[4,16,3584]{2,1,0:T(8,128)(2,1)S(1)}, bf16[4,16,3584]{2,1,0:T(8,128)(2,1)S(1)}, u32[]{:S(2)}, u32[]{:S(2)}) %collective-permute-start.22) | collective-permute-done | bytes 458784 | tf_op jit(solution)/shard_map/ppermute | solution.py:52
  208.6 5.3 %collective-permute-done.25 = bf16[4,16,3584]{2,1,0:T(8,128)(2,1)S(1)} collective-permute-done((bf16[4,16,3584]{2,1,0:T(8,128)(2,1)S(1)}, bf16[4,16,3584]{2,1,0:T(8,128)(2,1)S(1)}, u32[]{:S(2)}, u32[]{:S(2)}) %collective-permute-start.25) | collective-permute-done | bytes 458784 | tf_op jit(solution)/shard_map/ppermute | solution.py:52
  213.9 3.5 %collective-permute-start.26 = (bf16[4,16,3584]{2,1,0:T(8,128)(2,1)S(1)}, bf16[4,16,3584]{2,1,0:T(8,128)(2,1)S(1)}, u32[]{:S(2)}, u32[]{:S(2)}) collective-permute-start(bf16[4,16,3584]{2,1,0:T(8,128)(2,1)S(1)} %collective-permute-done.25), channel_id=1, source_target_pairs={{0,12},{4,0},{8,4},{12,8},{1,13},{5,1},{9,5},{13,9},{2,14},{6,2},{... | collective-permute-start | bytes 1376264 | tf_op jit(solution)/shard_map/ppermute | solution.py:52
  217.4 2.1 collective-permute-done.31
  219.4 3.2 %collective-permute-start.35 = (bf16[4,16,3584]{2,1,0:T(8,128)(2,1)S(1)}, bf16[4,16,3584]{2,1,0:T(8,128)(2,1)S(1)}, u32[]{:S(2)}, u32[]{:S(2)}) collective-permute-start(bf16[4,16,3584]{2,1,0:T(8,128)(2,1)S(1)} %collective-permute-done.34), channel_id=1, source_target_pairs={{0,3},{1,0},{2,1},{3,2},{4,7},{5,4},{6,5},{7,6},{8,11},{9,8},{10,9... | collective-permute-start | bytes 1376264 | tf_op jit(solution)/shard_map/ppermute | solution.py:52
  222.8 7.8 %collective-permute-done.23 = bf16[4,16,3584]{2,1,0:T(8,128)(2,1)S(1)} collective-permute-done((bf16[4,16,3584]{2,1,0:T(8,128)(2,1)S(1)}, bf16[4,16,3584]{2,1,0:T(8,128)(2,1)S(1)}, u32[]{:S(2)}, u32[]{:S(2)}) %collective-permute-start.23) | collective-permute-done | bytes 458784 | tf_op jit(solution)/shard_map/ppermute | solution.py:52
  230.7 5.2 %collective-permute-done.26 = bf16[4,16,3584]{2,1,0:T(8,128)(2,1)S(1)} collective-permute-done((bf16[4,16,3584]{2,1,0:T(8,128)(2,1)S(1)}, bf16[4,16,3584]{2,1,0:T(8,128)(2,1)S(1)}, u32[]{:S(2)}, u32[]{:S(2)}) %collective-permute-start.26) | collective-permute-done | bytes 458784 | tf_op jit(solution)/shard_map/ppermute | solution.py:52
  236.0 5.8 %collective-permute-done.32 = bf16[4,16,3584]{2,1,0:T(8,128)(2,1)S(1)} collective-permute-done((bf16[4,16,3584]{2,1,0:T(8,128)(2,1)S(1)}, bf16[4,16,3584]{2,1,0:T(8,128)(2,1)S(1)}, u32[]{:S(2)}, u32[]{:S(2)}) %collective-permute-start.32) | collective-permute-done | bytes 458784 | tf_op jit(solution)/shard_map/ppermute | solution.py:52
  241.9 7.8 %convolution_convert_fusion.5 = bf16[1024,448]{0,1:T(8,128)(2,1)S(1)} fusion(bf16[3584,448]{0,1:T(8,128)(2,1)S(1)} %copy-done, bf16[256,3584]{1,0:T(8,128)(2,1)S(1)} %bitcast.218, bf16[256,3584]{1,0:T(8,128)(2,1)S(1)} %bitcast.224, bf16[256,3584]{1,0:T(8,128)(2,1)S(1)} %bitcast.220, bf16[256,3584]{1,0:T(8,128)(2,1)S(1)} %bitcast.222), kind=kOutput, calls=%fused_computation.20 | convolution fusion | flops 3318153216 | bytes 11468800 | tf_op jit(solution)/shard_map/dot_general | solution.py:153
  251.4 7.5 %convolution_convert_fusion.4 = bf16[1024,448]{0,1:T(8,128)(2,1)S(1)} fusion(bf16[1024,3584]{1,0:T(8,128)(2,1)} %all-gather.5.cloned.1.call-done, bf16[448,3584]{1,0:T(8,128)(2,1)} %param.5), kind=kOutput, calls=%fused_computation.19 | convolution fusion | flops 3288793088 | bytes 11468800 | tf_op jit(solution)/shard_map/dot_general | solution.py:24
  259.8 8.7 %collective-permute-start.36 = (bf16[4,128,896]{2,1,0:T(8,128)(2,1)S(1)}, bf16[4,128,896]{2,1,0:T(8,128)(2,1)S(1)}, u32[]{:S(2)}, u32[]{:S(2)}) collective-permute-start(bf16[4,128,896]{2,1,0:T(8,128)(2,1)S(1)} %fusion.16), channel_id=1, source_target_pairs={{0,16},{16,0},{1,17},{17,1},{2,18},{18,2},{3,19},{19,3},{4,20},{20... | collective-permute-start | bytes 2752520 | tf_op jit(solution)/shard_map/ppermute | solution.py:129
  268.5 7.4 %convolution_convert_fusion.2 = bf16[3584,448]{0,1:T(8,128)(2,1)} fusion(bf16[256,3584]{1,0:T(8,128)(2,1)} %bitcast.219, bf16[256,3584]{1,0:T(8,128)(2,1)} %bitcast.225, bf16[256,3584]{1,0:T(8,128)(2,1)} %bitcast.221, bf16[256,3584]{1,0:T(8,128)(2,1)} %bitcast.223, bf16[1024,896]{1,0:T(8,128)(2,1)S(1)} %copy-done.13), kind=kOutput, calls=%fused_computation.3 | convolution fusion | flops 3319300096 | bytes 11599872 | tf_op jit(solution)/shard_map/dot_general | solution.py:30
  276.4 1.6 collective-permute-start.37
  278.0 1.5 collective-permute-start.38
  279.5 2.0 collective-permute-start.39
  281.5 4.9 %convolution_convert_fusion.3 = bf16[448,3584]{1,0:T(8,128)(2,1)} fusion(bf16[1024,3584]{1,0:T(8,128)(2,1)S(1)} %bitcast.233, bf16[1024,896]{1,0:T(8,128)(2,1)S(1)} %copy-done.11), kind=kOutput, calls=%fused_computation.4 | convolution fusion | flops 3289939968 | bytes 11599872 | tf_op jit(solution)/shard_map/dot_general | solution.py:30
  286.4 1.9 collective-permute-done.38
  (157 shorter events, 20.5 us)
Async XLA Ops:
  7.2 49.0 %copy-start = (bf16[3584,448]{0,1:T(8,128)(2,1)S(1)}, bf16[3584,448]{0,1:T(8,128)(2,1)}, u32[]{:S(2)}) copy-start(bf16[3584,448]{0,1:T(8,128)(2,1)} %param.6) | copy-start | bytes 9633796
  7.2 31.9 %all-gather.3.cloned.1.call-start = ((), (), s32[]{:S(2)}) async-start(), calls=%async_computation.1 | async-start | bytes 2064384 | tf_op jit(solution)/shard_map/all_gather | solution.py:135
  10.2 146.0 %reduce-scatter.2.cloned.1.call-start = ((), (), s32[]{:S(2)}) async-start(), calls=%async_computation.2 | async-start | bytes 7798784 | tf_op jit(solution)/shard_map/reduce_scatter | solution.py:142
  40.7 2.6 copy-start.18
  40.9 1.2 copy-start.12
  48.0 8.2 %copy-start.2 = (bf16[256,3584]{1,0:T(8,128)(2,1)}, bf16[256,3584]{1,0:T(8,128)(2,1)S(1)}, u32[]{:S(2)}) copy-start(bf16[256,3584]{1,0:T(8,128)(2,1)S(1)} %get-tuple-element.10) | copy-start | bytes 5505028
  48.0 8.2 %copy-start.4 = (bf16[256,3584]{1,0:T(8,128)(2,1)}, bf16[256,3584]{1,0:T(8,128)(2,1)S(1)}, u32[]{:S(2)}) copy-start(bf16[256,3584]{1,0:T(8,128)(2,1)S(1)} %get-tuple-element.9) | copy-start | bytes 5505028
  48.0 8.2 %copy-start.6 = (bf16[256,3584]{1,0:T(8,128)(2,1)}, bf16[256,3584]{1,0:T(8,128)(2,1)S(1)}, u32[]{:S(2)}) copy-start(bf16[256,3584]{1,0:T(8,128)(2,1)S(1)} %get-tuple-element.11) | copy-start | bytes 5505028
  48.0 8.2 %copy-start.8 = (bf16[256,3584]{1,0:T(8,128)(2,1)}, bf16[256,3584]{1,0:T(8,128)(2,1)S(1)}, u32[]{:S(2)}) copy-start(bf16[256,3584]{1,0:T(8,128)(2,1)S(1)} %get-tuple-element.8) | copy-start | bytes 5505028
  48.0 8.2 %copy-start.10 = (bf16[1024,896]{1,0:T(8,128)(2,1)S(1)}, bf16[1024,896]{1,0:T(8,128)(2,1)}, u32[]{:S(2)}) copy-start(bf16[1024,896]{1,0:T(8,128)(2,1)} %all-gather.3.cloned.1.call-done) | copy-start | bytes 5505028
  48.8 13.5 %collective-permute-start.3 = (bf16[4,16,3584]{2,1,0:T(8,128)(2,1)}, bf16[4,16,3584]{2,1,0:T(8,128)(2,1)}, u32[]{:S(2)}, u32[]{:S(2)}) collective-permute-start(bf16[4,16,3584]{2,1,0:T(8,128)(2,1)} %dynamic-slice_bitcast_fusion.2), channel_id=1, source_target_pairs={{0,12},{4,0},{8,4},{12,8},{1,13},{5,1},{9,5},{13,9},{2,14},{6,2},{... | collective-permute-start | bytes 1376264 | tf_op jit(solution)/shard_map/ppermute | solution.py:40
  52.0 14.4 %collective-permute-start = (bf16[4,16,3584]{2,1,0:T(8,128)(2,1)}, bf16[4,16,3584]{2,1,0:T(8,128)(2,1)}, u32[]{:S(2)}, u32[]{:S(2)}) collective-permute-start(bf16[4,16,3584]{2,1,0:T(8,128)(2,1)} %dynamic-slice_bitcast_fusion.3), channel_id=1, source_target_pairs={{0,4},{4,8},{8,12},{12,0},{1,5},{5,9},{9,13},{13,1},{2,6},{6,10},{... | collective-permute-start | bytes 1376264 | tf_op jit(solution)/shard_map/ppermute | solution.py:40
  52.8 14.9 %collective-permute-start.12 = (bf16[4,16,3584]{2,1,0:T(8,128)(2,1)}, bf16[4,16,3584]{2,1,0:T(8,128)(2,1)}, u32[]{:S(2)}, u32[]{:S(2)}) collective-permute-start(bf16[4,16,3584]{2,1,0:T(8,128)(2,1)} %dynamic-slice_bitcast_fusion), channel_id=1, source_target_pairs={{0,3},{1,0},{2,1},{3,2},{4,7},{5,4},{6,5},{7,6},{8,11},{9,8},{10,9... | collective-permute-start | bytes 1376264 | tf_op jit(solution)/shard_map/ppermute | solution.py:40
  56.1 15.7 %collective-permute-start.9 = (bf16[4,16,3584]{2,1,0:T(8,128)(2,1)}, bf16[4,16,3584]{2,1,0:T(8,128)(2,1)}, u32[]{:S(2)}, u32[]{:S(2)}) collective-permute-start(bf16[4,16,3584]{2,1,0:T(8,128)(2,1)} %dynamic-slice_bitcast_fusion.1), channel_id=1, source_target_pairs={{0,1},{1,2},{2,3},{3,0},{4,5},{5,6},{6,7},{7,4},{8,9},{9,10},{10,1... | collective-permute-start | bytes 1376264 | tf_op jit(solution)/shard_map/ppermute | solution.py:40
  62.3 189.1 %all-gather.5.cloned.1.call-start = ((), (), s32[]{:S(2)}) async-start(), calls=%async_computation.3 | async-start | bytes 7798784 | tf_op jit(solution)/shard_map/all_gather | solution.py:149
  62.3 9.5 %copy-start.3 = (bf16[256,3584]{1,0:T(8,128)(2,1)S(1)}, bf16[256,3584]{1,0:T(8,128)(2,1)}, u32[]{:S(2)}) copy-start(bf16[256,3584]{1,0:T(8,128)(2,1)} %copy-done.2) | copy-start | bytes 5505028
  63.7 14.0 %copy-start.9 = (bf16[256,3584]{1,0:T(8,128)(2,1)S(1)}, bf16[256,3584]{1,0:T(8,128)(2,1)}, u32[]{:S(2)}) copy-start(bf16[256,3584]{1,0:T(8,128)(2,1)} %copy-done.8) | copy-start | bytes 5505028
  63.7 14.0 %collective-permute-start.4 = (bf16[4,16,3584]{2,1,0:T(8,128)(2,1)S(1)}, bf16[4,16,3584]{2,1,0:T(8,128)(2,1)S(1)}, u32[]{:S(2)}, u32[]{:S(2)}) collective-permute-start(bf16[4,16,3584]{2,1,0:T(8,128)(2,1)S(1)} %bitcast_add_fusion.8), channel_id=1, source_target_pairs={{0,12},{4,0},{8,4},{12,8},{1,13},{5,1},{9,5},{13,9},{2,14},{6,2},{... | collective-permute-start | bytes 1376264 | tf_op jit(solution)/shard_map/ppermute | solution.py:40
  67.7 15.7 %copy-start.7 = (bf16[256,3584]{1,0:T(8,128)(2,1)S(1)}, bf16[256,3584]{1,0:T(8,128)(2,1)}, u32[]{:S(2)}) copy-start(bf16[256,3584]{1,0:T(8,128)(2,1)} %copy-done.6) | copy-start | bytes 5505028
  67.7 15.7 %collective-permute-start.1 = (bf16[4,16,3584]{2,1,0:T(8,128)(2,1)S(1)}, bf16[4,16,3584]{2,1,0:T(8,128)(2,1)S(1)}, u32[]{:S(2)}, u32[]{:S(2)}) collective-permute-start(bf16[4,16,3584]{2,1,0:T(8,128)(2,1)S(1)} %bitcast_add_fusion.11), channel_id=1, source_target_pairs={{0,4},{4,8},{8,12},{12,0},{1,5},{5,9},{9,13},{13,1},{2,6},{6,10},{... | collective-permute-start | bytes 1376264 | tf_op jit(solution)/shard_map/ppermute | solution.py:40
  69.1 19.8 %copy-start.5 = (bf16[256,3584]{1,0:T(8,128)(2,1)S(1)}, bf16[256,3584]{1,0:T(8,128)(2,1)}, u32[]{:S(2)}) copy-start(bf16[256,3584]{1,0:T(8,128)(2,1)} %copy-done.4) | copy-start | bytes 5505028
  69.1 19.8 %collective-permute-start.13 = (bf16[4,16,3584]{2,1,0:T(8,128)(2,1)S(1)}, bf16[4,16,3584]{2,1,0:T(8,128)(2,1)S(1)}, u32[]{:S(2)}, u32[]{:S(2)}) collective-permute-start(bf16[4,16,3584]{2,1,0:T(8,128)(2,1)S(1)} %bitcast_add_fusion.2), channel_id=1, source_target_pairs={{0,3},{1,0},{2,1},{3,2},{4,7},{5,4},{6,5},{7,6},{8,11},{9,8},{10,9... | collective-permute-start | bytes 1376264 | tf_op jit(solution)/shard_map/ppermute | solution.py:40
  73.0 19.9 %collective-permute-start.10 = (bf16[4,16,3584]{2,1,0:T(8,128)(2,1)S(1)}, bf16[4,16,3584]{2,1,0:T(8,128)(2,1)S(1)}, u32[]{:S(2)}, u32[]{:S(2)}) collective-permute-start(bf16[4,16,3584]{2,1,0:T(8,128)(2,1)S(1)} %bitcast_add_fusion.5), channel_id=1, source_target_pairs={{0,1},{1,2},{2,3},{3,0},{4,5},{5,6},{6,7},{7,4},{8,9},{9,10},{10,1... | collective-permute-start | bytes 1376264 | tf_op jit(solution)/shard_map/ppermute | solution.py:40
  77.8 18.4 %collective-permute-start.5 = (bf16[4,16,3584]{2,1,0:T(8,128)(2,1)S(1)}, bf16[4,16,3584]{2,1,0:T(8,128)(2,1)S(1)}, u32[]{:S(2)}, u32[]{:S(2)}) collective-permute-start(bf16[4,16,3584]{2,1,0:T(8,128)(2,1)S(1)} %bitcast_add_fusion.7), channel_id=1, source_target_pairs={{0,12},{4,0},{8,4},{12,8},{1,13},{5,1},{9,5},{13,9},{2,14},{6,2},{... | collective-permute-start | bytes 1376264 | tf_op jit(solution)/shard_map/ppermute | solution.py:40
  83.4 18.7 %collective-permute-start.2 = (bf16[4,16,3584]{2,1,0:T(8,128)(2,1)S(1)}, bf16[4,16,3584]{2,1,0:T(8,128)(2,1)S(1)}, u32[]{:S(2)}, u32[]{:S(2)}) collective-permute-start(bf16[4,16,3584]{2,1,0:T(8,128)(2,1)S(1)} %bitcast_add_fusion.10), channel_id=1, source_target_pairs={{0,4},{4,8},{8,12},{12,0},{1,5},{5,9},{9,13},{13,1},{2,6},{6,10},{... | collective-permute-start | bytes 1376264 | tf_op jit(solution)/shard_map/ppermute | solution.py:40
  88.9 22.0 %collective-permute-start.14 = (bf16[4,16,3584]{2,1,0:T(8,128)(2,1)S(1)}, bf16[4,16,3584]{2,1,0:T(8,128)(2,1)S(1)}, u32[]{:S(2)}, u32[]{:S(2)}) collective-permute-start(bf16[4,16,3584]{2,1,0:T(8,128)(2,1)S(1)} %bitcast_add_fusion.1), channel_id=1, source_target_pairs={{0,3},{1,0},{2,1},{3,2},{4,7},{5,4},{6,5},{7,6},{8,11},{9,8},{10,9... | collective-permute-start | bytes 1376264 | tf_op jit(solution)/shard_map/ppermute | solution.py:40
  93.0 19.0 %collective-permute-start.11 = (bf16[4,16,3584]{2,1,0:T(8,128)(2,1)S(1)}, bf16[4,16,3584]{2,1,0:T(8,128)(2,1)S(1)}, u32[]{:S(2)}, u32[]{:S(2)}) collective-permute-start(bf16[4,16,3584]{2,1,0:T(8,128)(2,1)S(1)} %bitcast_add_fusion.4), channel_id=1, source_target_pairs={{0,1},{1,2},{2,3},{3,0},{4,5},{5,6},{6,7},{7,4},{8,9},{9,10},{10,1... | collective-permute-start | bytes 1376264 | tf_op jit(solution)/shard_map/ppermute | solution.py:40
  102.3 19.5 %collective-permute-start.6 = (bf16[2,16,3584]{2,1,0:T(8,128)(2,1)S(1)}, bf16[2,16,3584]{2,1,0:T(8,128)(2,1)S(1)}, u32[]{:S(2)}, u32[]{:S(2)}) collective-permute-start(bf16[2,16,3584]{2,1,0:T(8,128)(2,1)S(1)} %fusion.44), channel_id=1, source_target_pairs={{0,1},{1,2},{2,3},{3,0},{4,5},{5,6},{6,7},{7,4},{8,9},{9,10},{10,1... | collective-permute-start | bytes 688136 | tf_op jit(solution)/shard_map/ppermute | solution.py:40
  112.0 10.8 %collective-permute-start.15 = (bf16[2,16,3584]{2,1,0:T(8,128)(2,1)S(1)}, bf16[2,16,3584]{2,1,0:T(8,128)(2,1)S(1)}, u32[]{:S(2)}, u32[]{:S(2)}) collective-permute-start(bf16[2,16,3584]{2,1,0:T(8,128)(2,1)S(1)} %fusion.33), channel_id=1, source_target_pairs={{0,12},{4,0},{8,4},{12,8},{1,13},{5,1},{9,5},{13,9},{2,14},{6,2},{... | collective-permute-start | bytes 688136 | tf_op jit(solution)/shard_map/ppermute | solution.py:40
  121.8 10.3 %collective-permute-start.7 = (bf16[2,16,3584]{2,1,0:T(8,128)(2,1)S(1)}, bf16[2,16,3584]{2,1,0:T(8,128)(2,1)S(1)}, u32[]{:S(2)}, u32[]{:S(2)}) collective-permute-start(bf16[2,16,3584]{2,1,0:T(8,128)(2,1)S(1)} %fusion.47), channel_id=1, source_target_pairs={{0,1},{1,2},{2,3},{3,0},{4,5},{5,6},{6,7},{7,4},{8,9},{9,10},{10,1... | collective-permute-start | bytes 688136 | tf_op jit(solution)/shard_map/ppermute | solution.py:40
  122.9 10.0 %collective-permute-start.16 = (bf16[2,16,3584]{2,1,0:T(8,128)(2,1)S(1)}, bf16[2,16,3584]{2,1,0:T(8,128)(2,1)S(1)}, u32[]{:S(2)}, u32[]{:S(2)}) collective-permute-start(bf16[2,16,3584]{2,1,0:T(8,128)(2,1)S(1)} %fusion.36), channel_id=1, source_target_pairs={{0,12},{4,0},{8,4},{12,8},{1,13},{5,1},{9,5},{13,9},{2,14},{6,2},{... | collective-permute-start | bytes 688136 | tf_op jit(solution)/shard_map/ppermute | solution.py:40
  132.2 6.3 %collective-permute-start.8 = (bf16[2,16,3584]{2,1,0:T(8,128)(2,1)S(1)}, bf16[2,16,3584]{2,1,0:T(8,128)(2,1)S(1)}, u32[]{:S(2)}, u32[]{:S(2)}) collective-permute-start(bf16[2,16,3584]{2,1,0:T(8,128)(2,1)S(1)} %fusion.50), channel_id=1, source_target_pairs={{0,1},{1,2},{2,3},{3,0},{4,5},{5,6},{6,7},{7,4},{8,9},{9,10},{10,1... | collective-permute-start | bytes 688136 | tf_op jit(solution)/shard_map/ppermute | solution.py:40
  132.9 8.1 %collective-permute-start.17 = (bf16[2,16,3584]{2,1,0:T(8,128)(2,1)S(1)}, bf16[2,16,3584]{2,1,0:T(8,128)(2,1)S(1)}, u32[]{:S(2)}, u32[]{:S(2)}) collective-permute-start(bf16[2,16,3584]{2,1,0:T(8,128)(2,1)S(1)} %fusion.39), channel_id=1, source_target_pairs={{0,12},{4,0},{8,4},{12,8},{1,13},{5,1},{9,5},{13,9},{2,14},{6,2},{... | collective-permute-start | bytes 688136 | tf_op jit(solution)/shard_map/ppermute | solution.py:40
  159.7 6.8 %collective-permute-start.18 = (bf16[2,16,3584]{2,1,0:T(8,128)(2,1)}, bf16[2,16,3584]{2,1,0:T(8,128)(2,1)}, u32[]{:S(2)}, u32[]{:S(2)}) collective-permute-start(bf16[2,16,3584]{2,1,0:T(8,128)(2,1)} %bitcast.44), channel_id=1, source_target_pairs={{0,1},{1,2},{2,3},{3,0},{4,5},{5,6},{6,7},{7,4},{8,9},{9,10},{10,1... | collective-permute-start | bytes 688136 | tf_op jit(solution)/shard_map/ppermute | solution.py:52
  159.8 7.6 %collective-permute-start.27 = (bf16[2,16,3584]{2,1,0:T(8,128)(2,1)S(1)}, bf16[2,16,3584]{2,1,0:T(8,128)(2,1)}, u32[]{:S(2)}, u32[]{:S(2)}) collective-permute-start(bf16[2,16,3584]{2,1,0:T(8,128)(2,1)S(1)} %bitcast.230), channel_id=1, source_target_pairs={{0,12},{4,0},{8,4},{12,8},{1,13},{5,1},{9,5},{13,9},{2,14},{6,2},{... | collective-permute-start | bytes 688136 | tf_op jit(solution)/shard_map/ppermute | solution.py:52
  166.5 6.3 %collective-permute-start.19 = (bf16[2,16,3584]{2,1,0:T(8,128)(2,1)}, bf16[2,16,3584]{2,1,0:T(8,128)(2,1)S(1)}, u32[]{:S(2)}, u32[]{:S(2)}) collective-permute-start(bf16[2,16,3584]{2,1,0:T(8,128)(2,1)} %collective-permute-done.18), channel_id=1, source_target_pairs={{0,1},{1,2},{2,3},{3,0},{4,5},{5,6},{6,7},{7,4},{8,9},{9,10},{10,1... | collective-permute-start | bytes 688136 | tf_op jit(solution)/shard_map/ppermute | solution.py:52
  167.5 5.3 %collective-permute-start.28 = (bf16[2,16,3584]{2,1,0:T(8,128)(2,1)}, bf16[2,16,3584]{2,1,0:T(8,128)(2,1)S(1)}, u32[]{:S(2)}, u32[]{:S(2)}) collective-permute-start(bf16[2,16,3584]{2,1,0:T(8,128)(2,1)} %collective-permute-done.27), channel_id=1, source_target_pairs={{0,12},{4,0},{8,4},{12,8},{1,13},{5,1},{9,5},{13,9},{2,14},{6,2},{... | collective-permute-start | bytes 688136 | tf_op jit(solution)/shard_map/ppermute | solution.py:52
  172.7 10.5 %collective-permute-start.20 = (bf16[2,16,3584]{2,1,0:T(8,128)(2,1)S(1)}, bf16[2,16,3584]{2,1,0:T(8,128)(2,1)S(1)}, u32[]{:S(2)}, u32[]{:S(2)}) collective-permute-start(bf16[2,16,3584]{2,1,0:T(8,128)(2,1)S(1)} %collective-permute-done.19), channel_id=1, source_target_pairs={{0,1},{1,2},{2,3},{3,0},{4,5},{5,6},{6,7},{7,4},{8,9},{9,10},{10,1... | collective-permute-start | bytes 688136 | tf_op jit(solution)/shard_map/ppermute | solution.py:52
  172.8 13.8 %collective-permute-start.29 = (bf16[2,16,3584]{2,1,0:T(8,128)(2,1)S(1)}, bf16[2,16,3584]{2,1,0:T(8,128)(2,1)S(1)}, u32[]{:S(2)}, u32[]{:S(2)}) collective-permute-start(bf16[2,16,3584]{2,1,0:T(8,128)(2,1)S(1)} %collective-permute-done.28), channel_id=1, source_target_pairs={{0,12},{4,0},{8,4},{12,8},{1,13},{5,1},{9,5},{13,9},{2,14},{6,2},{... | collective-permute-start | bytes 688136 | tf_op jit(solution)/shard_map/ppermute | solution.py:52
  183.5 9.2 %collective-permute-start.21 = (bf16[4,16,3584]{2,1,0:T(8,128)(2,1)S(1)}, bf16[4,16,3584]{2,1,0:T(8,128)(2,1)S(1)}, u32[]{:S(2)}, u32[]{:S(2)}) collective-permute-start(bf16[4,16,3584]{2,1,0:T(8,128)(2,1)S(1)} %get-tuple-element.23), channel_id=1, source_target_pairs={{0,4},{4,8},{8,12},{12,0},{1,5},{5,9},{9,13},{13,1},{2,6},{6,10},{... | collective-permute-start | bytes 1376264 | tf_op jit(solution)/shard_map/ppermute | solution.py:52
  183.8 9.9 %collective-permute-start.24 = (bf16[4,16,3584]{2,1,0:T(8,128)(2,1)S(1)}, bf16[4,16,3584]{2,1,0:T(8,128)(2,1)S(1)}, u32[]{:S(2)}, u32[]{:S(2)}) collective-permute-start(bf16[4,16,3584]{2,1,0:T(8,128)(2,1)S(1)} %get-tuple-element.24), channel_id=1, source_target_pairs={{0,12},{4,0},{8,4},{12,8},{1,13},{5,1},{9,5},{13,9},{2,14},{6,2},{... | collective-permute-start | bytes 1376264 | tf_op jit(solution)/shard_map/ppermute | solution.py:52
  186.9 9.3 %collective-permute-start.30 = (bf16[4,16,3584]{2,1,0:T(8,128)(2,1)S(1)}, bf16[4,16,3584]{2,1,0:T(8,128)(2,1)S(1)}, u32[]{:S(2)}, u32[]{:S(2)}) collective-permute-start(bf16[4,16,3584]{2,1,0:T(8,128)(2,1)S(1)} %get-tuple-element.25), channel_id=1, source_target_pairs={{0,1},{1,2},{2,3},{3,0},{4,5},{5,6},{6,7},{7,4},{8,9},{9,10},{10,1... | collective-permute-start | bytes 1376264 | tf_op jit(solution)/shard_map/ppermute | solution.py:52
  187.0 10.7 %collective-permute-start.33 = (bf16[4,16,3584]{2,1,0:T(8,128)(2,1)S(1)}, bf16[4,16,3584]{2,1,0:T(8,128)(2,1)S(1)}, u32[]{:S(2)}, u32[]{:S(2)}) collective-permute-start(bf16[4,16,3584]{2,1,0:T(8,128)(2,1)S(1)} %get-tuple-element.26), channel_id=1, source_target_pairs={{0,3},{1,0},{2,1},{3,2},{4,7},{5,4},{6,5},{7,6},{8,11},{9,8},{10,9... | collective-permute-start | bytes 1376264 | tf_op jit(solution)/shard_map/ppermute | solution.py:52
  192.7 15.9 %collective-permute-start.22 = (bf16[4,16,3584]{2,1,0:T(8,128)(2,1)S(1)}, bf16[4,16,3584]{2,1,0:T(8,128)(2,1)S(1)}, u32[]{:S(2)}, u32[]{:S(2)}) collective-permute-start(bf16[4,16,3584]{2,1,0:T(8,128)(2,1)S(1)} %collective-permute-done.21), channel_id=1, source_target_pairs={{0,4},{4,8},{8,12},{12,0},{1,5},{5,9},{9,13},{13,1},{2,6},{6,10},{... | collective-permute-start | bytes 1376264 | tf_op jit(solution)/shard_map/ppermute | solution.py:52
  193.8 20.1 %collective-permute-start.25 = (bf16[4,16,3584]{2,1,0:T(8,128)(2,1)S(1)}, bf16[4,16,3584]{2,1,0:T(8,128)(2,1)S(1)}, u32[]{:S(2)}, u32[]{:S(2)}) collective-permute-start(bf16[4,16,3584]{2,1,0:T(8,128)(2,1)S(1)} %collective-permute-done.24), channel_id=1, source_target_pairs={{0,12},{4,0},{8,4},{12,8},{1,13},{5,1},{9,5},{13,9},{2,14},{6,2},{... | collective-permute-start | bytes 1376264 | tf_op jit(solution)/shard_map/ppermute | solution.py:52
  196.1 23.3 %collective-permute-start.31 = (bf16[4,16,3584]{2,1,0:T(8,128)(2,1)S(1)}, bf16[4,16,3584]{2,1,0:T(8,128)(2,1)S(1)}, u32[]{:S(2)}, u32[]{:S(2)}) collective-permute-start(bf16[4,16,3584]{2,1,0:T(8,128)(2,1)S(1)} %collective-permute-done.30), channel_id=1, source_target_pairs={{0,1},{1,2},{2,3},{3,0},{4,5},{5,6},{6,7},{7,4},{8,9},{9,10},{10,1... | collective-permute-start | bytes 1376264 | tf_op jit(solution)/shard_map/ppermute | solution.py:52
  197.6 21.8 %collective-permute-start.34 = (bf16[4,16,3584]{2,1,0:T(8,128)(2,1)S(1)}, bf16[4,16,3584]{2,1,0:T(8,128)(2,1)S(1)}, u32[]{:S(2)}, u32[]{:S(2)}) collective-permute-start(bf16[4,16,3584]{2,1,0:T(8,128)(2,1)S(1)} %collective-permute-done.33), channel_id=1, source_target_pairs={{0,3},{1,0},{2,1},{3,2},{4,7},{5,4},{6,5},{7,6},{8,11},{9,8},{10,9... | collective-permute-start | bytes 1376264 | tf_op jit(solution)/shard_map/ppermute | solution.py:52
  208.6 22.1 %collective-permute-start.23 = (bf16[4,16,3584]{2,1,0:T(8,128)(2,1)S(1)}, bf16[4,16,3584]{2,1,0:T(8,128)(2,1)S(1)}, u32[]{:S(2)}, u32[]{:S(2)}) collective-permute-start(bf16[4,16,3584]{2,1,0:T(8,128)(2,1)S(1)} %collective-permute-done.22), channel_id=1, source_target_pairs={{0,4},{4,8},{8,12},{12,0},{1,5},{5,9},{9,13},{13,1},{2,6},{6,10},{... | collective-permute-start | bytes 1376264 | tf_op jit(solution)/shard_map/ppermute | solution.py:52
  213.9 22.1 %collective-permute-start.26 = (bf16[4,16,3584]{2,1,0:T(8,128)(2,1)S(1)}, bf16[4,16,3584]{2,1,0:T(8,128)(2,1)S(1)}, u32[]{:S(2)}, u32[]{:S(2)}) collective-permute-start(bf16[4,16,3584]{2,1,0:T(8,128)(2,1)S(1)} %collective-permute-done.25), channel_id=1, source_target_pairs={{0,12},{4,0},{8,4},{12,8},{1,13},{5,1},{9,5},{13,9},{2,14},{6,2},{... | collective-permute-start | bytes 1376264 | tf_op jit(solution)/shard_map/ppermute | solution.py:52
  219.4 22.3 %collective-permute-start.32 = (bf16[4,16,3584]{2,1,0:T(8,128)(2,1)S(1)}, bf16[4,16,3584]{2,1,0:T(8,128)(2,1)S(1)}, u32[]{:S(2)}, u32[]{:S(2)}) collective-permute-start(bf16[4,16,3584]{2,1,0:T(8,128)(2,1)S(1)} %collective-permute-done.31), channel_id=1, source_target_pairs={{0,1},{1,2},{2,3},{3,0},{4,5},{5,6},{6,7},{7,4},{8,9},{9,10},{10,1... | collective-permute-start | bytes 1376264 | tf_op jit(solution)/shard_map/ppermute | solution.py:52
  219.4 22.4 %collective-permute-start.35 = (bf16[4,16,3584]{2,1,0:T(8,128)(2,1)S(1)}, bf16[4,16,3584]{2,1,0:T(8,128)(2,1)S(1)}, u32[]{:S(2)}, u32[]{:S(2)}) collective-permute-start(bf16[4,16,3584]{2,1,0:T(8,128)(2,1)S(1)} %collective-permute-done.34), channel_id=1, source_target_pairs={{0,3},{1,0},{2,1},{3,2},{4,7},{5,4},{6,5},{7,6},{8,11},{9,8},{10,9... | collective-permute-start | bytes 1376264 | tf_op jit(solution)/shard_map/ppermute | solution.py:52
  230.7 19.0 %copy-start.16 = (bf16[4,4,16,3584]{3,2,1,0:T(8,128)(2,1)}, bf16[4,4,16,3584]{3,2,1,0:T(8,128)(2,1)S(1)}, u32[]{:S(2)}) copy-start(bf16[4,4,16,3584]{3,2,1,0:T(8,128)(2,1)S(1)} %bitcast_dynamic-update-slice_fusion.12) | copy-start | bytes 5505028
  236.0 13.7 %copy-start.15 = (bf16[4,4,16,3584]{3,2,1,0:T(8,128)(2,1)}, bf16[4,4,16,3584]{3,2,1,0:T(8,128)(2,1)S(1)}, u32[]{:S(2)}) copy-start(bf16[4,4,16,3584]{3,2,1,0:T(8,128)(2,1)S(1)} %bitcast_dynamic-update-slice_fusion.8) | copy-start | bytes 5505028
  241.8 7.9 %copy-start.17 = (bf16[4,4,16,3584]{3,2,1,0:T(8,128)(2,1)}, bf16[4,4,16,3584]{3,2,1,0:T(8,128)(2,1)S(1)}, u32[]{:S(2)}) copy-start(bf16[4,4,16,3584]{3,2,1,0:T(8,128)(2,1)S(1)} %bitcast_dynamic-update-slice_fusion.4) | copy-start | bytes 5505028
  241.9 7.9 %copy-start.14 = (bf16[4,4,16,3584]{3,2,1,0:T(8,128)(2,1)}, bf16[4,4,16,3584]{3,2,1,0:T(8,128)(2,1)S(1)}, u32[]{:S(2)}) copy-start(bf16[4,4,16,3584]{3,2,1,0:T(8,128)(2,1)S(1)} %bitcast_dynamic-update-slice_fusion) | copy-start | bytes 5505028
  259.5 9.1 %copy-start.13 = (bf16[1024,896]{1,0:T(8,128)(2,1)S(1)}, bf16[1024,896]{1,0:T(8,128)(2,1)}, u32[]{:S(2)}) copy-start(bf16[1024,896]{1,0:T(8,128)(2,1)} %copy-done.12) | copy-start | bytes 5505028
  259.5 22.0 %slice-start = ((s8[7340032]{0:T(1024)(128)(4,1)}), s8[4194304]{0:T(1024)(128)(4,1)S(1)}, s32[]{:S(2)}) async-start(s8[7340032]{0:T(1024)(128)(4,1)} %bitcast.232), calls=%async_computation.4 | async-start | bytes 8388608
  259.8 21.7 %slice-start.1 = ((s8[7340032]{0:T(1024)(128)(4,1)}), s8[3145728]{0:T(1024)(128)(4,1)S(1)}, s32[]{:S(2)}) async-start(s8[7340032]{0:T(1024)(128)(4,1)} %bitcast.232), calls=%async_computation.5 | async-start | bytes 6291456
  259.8 16.1 %collective-permute-start.36 = (bf16[4,128,896]{2,1,0:T(8,128)(2,1)S(1)}, bf16[4,128,896]{2,1,0:T(8,128)(2,1)S(1)}, u32[]{:S(2)}, u32[]{:S(2)}) collective-permute-start(bf16[4,128,896]{2,1,0:T(8,128)(2,1)S(1)} %fusion.16), channel_id=1, source_target_pairs={{0,16},{16,0},{1,17},{17,1},{2,18},{18,2},{3,19},{19,3},{4,20},{20... | collective-permute-start | bytes 2752520 | tf_op jit(solution)/shard_map/ppermute | solution.py:129
  275.9 5.6 %copy-start.11 = (bf16[1024,896]{1,0:T(8,128)(2,1)S(1)}, bf16[1024,896]{1,0:T(8,128)(2,1)}, u32[]{:S(2)}) copy-start(bf16[1024,896]{1,0:T(8,128)(2,1)} %all-gather.3.cloned.1.call-done) | copy-start | bytes 5505028
  276.4 10.0 %collective-permute-start.37 = (bf16[128,896]{1,0:T(8,128)(2,1)S(1)}, bf16[128,896]{1,0:T(8,128)(2,1)S(1)}, u32[]{:S(2)}, u32[]{:S(2)}) collective-permute-start(bf16[128,896]{1,0:T(8,128)(2,1)S(1)} %get-tuple-element.16), channel_id=1, source_target_pairs={{0,32},{32,64},{64,96},{96,0},{1,33},{33,65},{65,97},{97,1},{2,34}... | collective-permute-start | bytes 688136 | tf_op jit(solution)/shard_map/ppermute | solution.py:73
  278.0 10.3 %collective-permute-start.38 = (bf16[128,896]{1,0:T(8,128)(2,1)S(1)}, bf16[128,896]{1,0:T(8,128)(2,1)S(1)}, u32[]{:S(2)}, u32[]{:S(2)}) collective-permute-start(bf16[128,896]{1,0:T(8,128)(2,1)S(1)} %get-tuple-element.18), channel_id=1, source_target_pairs={{0,64},{32,96},{64,0},{96,32},{1,65},{33,97},{65,1},{97,33},{2,66}... | collective-permute-start | bytes 688136 | tf_op jit(solution)/shard_map/ppermute | solution.py:73
  279.5 9.0 %collective-permute-start.39 = (bf16[128,896]{1,0:T(8,128)(2,1)S(1)}, bf16[128,896]{1,0:T(8,128)(2,1)S(1)}, u32[]{:S(2)}, u32[]{:S(2)}) collective-permute-start(bf16[128,896]{1,0:T(8,128)(2,1)S(1)} %get-tuple-element.17), channel_id=1, source_target_pairs={{0,96},{32,0},{64,32},{96,64},{1,97},{33,1},{65,33},{97,65},{2,98}... | collective-permute-start | bytes 688136 | tf_op jit(solution)/shard_map/ppermute | solution.py:73
  281.5 8.8 %copy-start.1 = (bf16[3584,448]{0,1:T(8,128)(2,1)S(1)}, bf16[3584,448]{0,1:T(8,128)(2,1)}, u32[]{:S(2)}) copy-start(bf16[3584,448]{0,1:T(8,128)(2,1)} %param.6) | copy-start | bytes 9633796
Sparse Core Ops, SparseCore 0:
  10.3 28.6 all-gather.2
  62.4 93.7 reduce-scatter.1
  161.4 89.9 all-gather.4
